TPU v7x, 512 devices: a whole 4x8x8 slice. The times are simulated.
512 devices in a mesh: wide: 64 (over y, z), narrow: 8 (over x, core).
Axes of the slice: x: 4, y: 8, z: 8, core: 2. Of those that a mesh axis runs over, the one named last changes fastest.
Arguments:
- amplitudes: bfloat16 [384, 2048], P('wide', 'narrow'), may hold values from -6 to 6
- integrals: bfloat16 [262144, 2048], P('wide', 'narrow'), may hold values from -0.375 to 0.375
- virtual_irrep: int32 [512], replicated, may hold values from 0 to 7
- column_irrep: int32 [2048], P('narrow'), may hold values from 0 to 7
- pair_energy: float32 [384], P('narrow'), may hold values from -4 to -1
- virtual_energy: float32 [512], replicated, may hold values from 0.5 to 3
- residual_in: bfloat16 [384, 262144], P('narrow', 'wide'), may hold values from -6 to 6
Outputs:
- new_amplitudes: bfloat16 [384, 262144], P('narrow', 'wide')
All inputs are finite; a program needn't handle non-finite values.
Results may differ from a plain program's by a relative error of at most 0.012.
Values may be sent and summed in bfloat16 or wider, within the bound.
No kernel may reach another device: no remote copies, remote signals or barrier semaphores. Data moves between devices by JAX's collectives and lax.ppermute only.
A program may use at most 64 MiB of HBM per device.

v0:
```python
import jax
import jax.numpy as jnp
from jax import lax
from jax.sharding import PartitionSpec as P


def local(
    amplitudes, integrals, virtual_irrep, column_irrep, pair_energy, virtual_energy, residual_in
):
    wide_size = lax.axis_size("wide")
    num_virt = virtual_irrep.shape[0]
    a_local = num_virt // wide_size
    first_a = lax.axis_index("wide") * a_local
    local_irrep = lax.dynamic_slice_in_dim(virtual_irrep, first_a, a_local, 0)
    row_irrep = jnp.bitwise_xor(local_irrep[:, None], virtual_irrep[None, :]).reshape(
        a_local * num_virt
    )
    masked = jnp.where(
        row_irrep[:, None] == column_irrep[None, :], integrals, jnp.zeros((), integrals.dtype)
    )
    contract = (((1,), (1,)), ((), ()))
    terms = lax.dot_general(
        lax.all_gather(amplitudes, "wide", axis=0, tiled=True),
        masked,
        contract,
        preferred_element_type=jnp.float32,
    )
    ladder = lax.psum_scatter(
        terms.astype(jnp.bfloat16), "narrow", scatter_dimension=0, tiled=True
    ).astype(jnp.float32)
    pair_rows = ladder.shape[0]
    ladder_cube = ladder.reshape(pair_rows, a_local, num_virt)
    swapped = lax.all_to_all(
        ladder_cube.astype(jnp.bfloat16), "wide", split_axis=2, concat_axis=2, tiled=True
    ).astype(ladder_cube.dtype)
    mirrored = swapped.reshape(pair_rows, a_local, wide_size, a_local)
    mirrored = jnp.transpose(mirrored, (0, 3, 2, 1)).reshape(pair_rows, a_local * num_virt)
    local_energy = lax.dynamic_slice_in_dim(virtual_energy, first_a, a_local, 0)
    denominator = (
        pair_energy[:, None, None] - local_energy[None, :, None] - virtual_energy[None, None, :]
    )
    denominator = denominator.reshape(pair_rows, a_local * num_virt)
    total = residual_in.astype(jnp.float32) + ladder - mirrored
    return (total / denominator).astype(jnp.bfloat16)


def solution(mesh):
    return jax.shard_map(
        local,
        mesh=mesh,
        in_specs=(
            P("wide", "narrow"),
            P("wide", "narrow"),
            P(),
            P("narrow"),
            P("narrow"),
            P(),
            P("narrow", "wide"),
        ),
        out_specs=P("narrow", "wide"),
        check_vma=False,
    )
```

profile of v0, /device:TPU:23, one launch (start us, length us, event | category | flops | bytes accessed | tf_op | source)
XLA Modules:
  0.0 151.3 jit_solution(6612598673634443218)
XLA Ops:
  6.5 0.0 reduce-scatter.4.cloned.1.call-start
  6.5 0.8 dynamic_slice.6
  7.3 0.8 xor_bitcast_fusion
  8.1 44.1 %all-gather = bf16[64,6,256]{2,1,0:T(8,128)(2,1)S(1)} all-gather(bf16[1,6,256]{2,1,0:T(8,128)(2,1)} %bitcast.31), channel_id=1, replica_groups=mesh['wide'=64,'narrow'=8] {'wide'}, dimensions={0}, use_global_device_ids=true | all-gather | bytes 199680 | tf_op jit(solution)/shard_map/all_gather | solution.py:23
  52.1 0.1 reshape.74
  52.2 2.8 %fusion = bf16[384,4096]{0,1:T(8,128)(2,1)S(1)} fusion(bf16[384,256]{1,0:T(8,128)(2,1)S(1)} %reshape.74, bf16[4096,256]{1,0:T(8,128)(2,1)} %param.8, s32[256]{0:T(256)} %param.10, s32[4096]{0:T(1024)S(1)} %bitcast.30), kind=kOutput, calls=%fused_computation.1 | convolution fusion | flops 808976384 | bytes 5456896 | tf_op jit(solution)/shard_map/dot_general | solution.py:22
  55.0 2.9 %copy.25 = bf16[384,4096]{1,0:T(8,128)(2,1)} copy(bf16[384,4096]{0,1:T(8,128)(2,1)S(1)} %fusion) | data formatting | bytes 6291456
  57.9 0.0 reduce-scatter.4.cloned.1.call-update
  57.9 47.4 %reduce-scatter.4.cloned.1.call-done = bf16[48,4096]{1,0:T(8,128)(2,1)} async-done(((bf16[384,4096]{1,0:T(8,128)(2,1)}), bf16[48,4096]{1,0:T(8,128)(2,1)}) %reduce-scatter.4.cloned.1.call-update) | async-done | bytes 393232 | tf_op jit(solution)/shard_map/reduce_scatter | solution.py:28
  105.4 1.5 copy.26
  106.8 0.0 copy-start.2
  106.8 0.0 copy-start.3
  106.9 0.7 copy.31
  107.5 2.5 %reshape.77 = bf16[64,2,1536]{2,1,0:T(2,128)(2,1)} reshape(bf16[512,8,48]{2,1,0:T(8,128)(2,1)S(1)} %bitcast.25) | data formatting | bytes 786432
  110.0 12.8 %all-to-all-start = ((bf16[64,2,1536]{2,1,0:T(2,128)(2,1)}), bf16[64,2,1536]{2,1,0:T(2,128)(2,1)S(1)}, u32[]{:S(2)}, u32[]{:S(2)}) async-start(bf16[64,2,1536]{2,1,0:T(2,128)(2,1)} %reshape.77), calls=%async_computation | async-start | bytes 786432 | tf_op jit(solution)/shard_map/all_to_all | solution.py:33
  122.8 0.0 copy-done.2
  122.9 0.1 dynamic_slice.7
  122.9 0.0 copy-done.3
  122.9 0.1 broadcast_subtract_fusion
  123.0 0.1 sub.45
  123.1 1.3 copy.28
  124.5 15.1 %all-to-all-done = bf16[64,2,1536]{2,1,0:T(2,128)(2,1)S(1)} async-done(((bf16[64,2,1536]{2,1,0:T(2,128)(2,1)}), bf16[64,2,1536]{2,1,0:T(2,128)(2,1)S(1)}, u32[]{:S(2)}, u32[]{:S(2)}) %all-to-all-start) | async-done | bytes 393248 | tf_op jit(solution)/shard_map/all_to_all | solution.py:33
  139.6 1.0 reshape.78
  140.6 0.1 copy.23
  140.8 0.0 copy-start
  140.8 0.0 copy-start.1
  140.8 1.5 copy.24
  142.3 0.0 copy-done
  142.3 0.0 copy-done.1
  142.3 2.2 %divide_convert_fusion = bf16[48,4096]{1,0:T(8,128)(2,1)} fusion(f32[48,4096]{1,0:T(8,128)S(1)} %bitcast.28, f32[48,4096]{1,0:T(8,128)} %copy.24, bf16[48,4096]{1,0:T(8,128)(2,1)S(1)} %copy-done.1, bf16[48,4096]{1,0:T(8,128)(2,1)} %param.13, f32[4096]{0:T(1024)S(1)} %bitcast.29), kind=kLoop, calls=%fused_computation.6 | loop fusion | flops 1376256 | bytes 2768896 | tf_op jit(solution)/shard_map/convert_element_type | solution.py:44
  (3 shorter events, 0.0 us)
Async XLA Ops:
  6.5 98.8 %reduce-scatter.4.cloned.1.call-start = ((), (), s32[]{:S(2)}) async-start(), calls=%async_computation.2 | async-start | bytes 3538944 | tf_op jit(solution)/shard_map/reduce_scatter | solution.py:28
  106.8 16.0 %copy-start.2 = (f32[512]{0:T(512)S(1)}, f32[512]{0:T(512)}, u32[]{:S(2)}) copy-start(f32[512]{0:T(512)} %param.12) | copy-start | bytes 6148
  106.8 16.1 %copy-start.3 = (f32[48]{0:T(128)S(1)}, f32[48]{0:T(128)}, u32[]{:S(2)}) copy-start(f32[48]{0:T(128)} %param.11) | copy-start | bytes 580
  110.0 29.6 %all-to-all-start = ((bf16[64,2,1536]{2,1,0:T(2,128)(2,1)}), bf16[64,2,1536]{2,1,0:T(2,128)(2,1)S(1)}, u32[]{:S(2)}, u32[]{:S(2)}) async-start(bf16[64,2,1536]{2,1,0:T(2,128)(2,1)} %reshape.77), calls=%async_computation | async-start | bytes 786432 | tf_op jit(solution)/shard_map/all_to_all | solution.py:33
  140.8 1.5 copy-start
  140.8 1.5 copy-start.1
Sparse Core Ops, SparseCore 0:
  58.1 47.2 reduce-scatter.3
where the time goes:
time: 152 us; the launch traced here: 151 us
  waiting for transfers between devices  62.5 us (41%)
  blocking collectives  44.1 us (29%)
  between operations  13.5 us (9%)
  starting transfers between devices  12.8 us (8%)
  local copies, waits for them, and re-layouts  12.6 us (8%)
  other arithmetic  3 us (2%)
  matrix products  2.8 us (2%)
    reduce_scatter x1, waiting for transfers between devices, local(): lax.psum_scatter(terms.astype(jnp.bfloat16), 'narrow', scatter_dimension=...  47.4 us
    all_gather x1, blocking collectives, local(): lax.all_gather(amplitudes, 'wide', axis=0, tiled=True)  44.1 us
    all_to_all x1, waiting for transfers between devices, local(): lax.all_to_all(ladder_cube.astype(jnp.bfloat16), 'wide', split_axis=2, co...  15.1 us
    all_to_all x1, starting transfers between devices, local(): lax.all_to_all(ladder_cube.astype(jnp.bfloat16), 'wide', split_axis=2, co...  12.8 us
    unnamed x17, local copies, waits for them, and re-layouts  9.39 us
  transfers between devices with their start and end apart: 2, of which 2 were waited for; matrix products, arithmetic and copies ran while one was open for 1% of the time, Pallas kernels for 0%

commit v1 on v0

v1 whole, which is shorter than its diff:
```python
import jax
import jax.numpy as jnp
from jax import lax
from jax.sharding import Mesh
from jax.sharding import PartitionSpec as P

WIDE = ("y", "z")
NARROW = ("x", "c")


def local(
    amplitudes, integrals, virtual_irrep, column_irrep, pair_energy, virtual_energy, residual_in
):
    ny, nz = lax.axis_size("y"), lax.axis_size("z")
    nx, nc = lax.axis_size("x"), lax.axis_size("c")
    wide_size = ny * nz
    num_virt = virtual_irrep.shape[0]
    a_local = num_virt // wide_size
    wide_index = lax.axis_index("y") * nz + lax.axis_index("z")
    first_a = wide_index * a_local
    local_irrep = lax.dynamic_slice_in_dim(virtual_irrep, first_a, a_local, 0)
    row_irrep = jnp.bitwise_xor(local_irrep[:, None], virtual_irrep[None, :]).reshape(
        a_local * num_virt
    )
    masked = jnp.where(
        row_irrep[:, None] == column_irrep[None, :], integrals, jnp.zeros((), integrals.dtype)
    )
    amp = lax.all_gather(amplitudes, "z", axis=0, tiled=True)
    amp = lax.all_gather(amp, "y", axis=0, tiled=True)
    pairs = amp.shape[0]
    block = pairs // (nx * nc)
    amp = amp.reshape(nx, nc, block, amp.shape[1]).transpose(1, 0, 2, 3).reshape(pairs, -1)
    contract = (((1,), (1,)), ((), ()))
    terms = lax.dot_general(amp, masked, contract, preferred_element_type=jnp.float32)
    terms = terms.astype(jnp.bfloat16)
    terms = lax.psum_scatter(terms, "c", scatter_dimension=0, tiled=True)
    ladder = lax.psum_scatter(terms, "x", scatter_dimension=0, tiled=True).astype(jnp.float32)
    pair_rows = ladder.shape[0]
    ladder_cube = ladder.reshape(pair_rows, a_local, num_virt)
    swapped = lax.all_to_all(
        ladder_cube.astype(jnp.bfloat16), WIDE, split_axis=2, concat_axis=2, tiled=True
    ).astype(ladder_cube.dtype)
    mirrored = swapped.reshape(pair_rows, a_local, wide_size, a_local)
    mirrored = jnp.transpose(mirrored, (0, 3, 2, 1)).reshape(pair_rows, a_local * num_virt)
    local_energy = lax.dynamic_slice_in_dim(virtual_energy, first_a, a_local, 0)
    denominator = (
        pair_energy[:, None, None] - local_energy[None, :, None] - virtual_energy[None, None, :]
    )
    denominator = denominator.reshape(pair_rows, a_local * num_virt)
    total = residual_in.astype(jnp.float32) + ladder - mirrored
    return (total / denominator).astype(jnp.bfloat16)


def solution(mesh):
    ny, nz = 8, mesh.devices.shape[0] // 8
    nx, nc = mesh.devices.shape[1] // 2, 2
    fine = Mesh(mesh.devices.reshape(ny, nz, nx, nc), ("y", "z", "x", "c"))
    return jax.shard_map(
        local,
        mesh=fine,
        in_specs=(
            P(WIDE, NARROW),
            P(WIDE, NARROW),
            P(),
            P(NARROW),
            P(NARROW),
            P(),
            P(NARROW, WIDE),
        ),
        out_specs=P(NARROW, WIDE),
        check_vma=False,
    )
```

time: 152 us -> 168 us (1.11)
  the two profiles are of different devices: /device:TPU:23 before, /device:TPU:16 now
where the time goes in v1:
time: 168 us
  waiting for transfers between devices  65.7 us (39%)
  blocking collectives  56.8 us (34%)
  between operations  13.5 us (8%)
  starting transfers between devices  13.4 us (8%)
  local copies, waits for them, and re-layouts  12.6 us (8%)
  other arithmetic  3 us (2%)
  matrix products  2.8 us (2%)
    reduce_scatter x1, waiting for transfers between devices, local(): lax.psum_scatter(terms, 'x', scatter_dimension=0, tiled=True)  35.4 us
    all_gather x1, blocking collectives, local(): amp = lax.all_gather(amplitudes, 'z', axis=0, tiled=True)  30.9 us
    all_gather x1, blocking collectives, local(): amp = lax.all_gather(amp, 'y', axis=0, tiled=True)  25.8 us
    unnamed x3, waiting for transfers between devices  16.2 us
    all_to_all x1, waiting for transfers between devices, local(): lax.all_to_all(ladder_cube.astype(jnp.bfloat16), WIDE, split_axis=2, conc...  14 us
    all_to_all x1, starting transfers between devices, local(): lax.all_to_all(ladder_cube.astype(jnp.bfloat16), WIDE, split_axis=2, conc...  13.4 us
    unnamed x17, local copies, waits for them, and re-layouts  9.33 us
  transfers between devices with their start and end apart: 3, of which 3 were waited for; matrix products, arithmetic and copies ran while one was open for 1% of the time, Pallas kernels for 0%

profile of v1, /device:TPU:16, one launch (start us, length us, event | category | flops | bytes accessed | tf_op | source)
XLA Modules:
  0.0 167.7 jit_solution(14889387374544633759)
XLA Ops:
  6.5 0.0 reduce-scatter.7.cloned.1.call-start
  6.5 0.8 dynamic_slice.6
  7.3 0.8 xor_bitcast_fusion
  8.1 30.9 %all-gather = bf16[8,6,256]{2,1,0:T(8,128)(2,1)S(1)} all-gather(bf16[1,6,256]{2,1,0:T(8,128)(2,1)} %bitcast.38), channel_id=1, replica_groups=mesh['y'=8,'z'=8,'x'=4,'c'=2] {'z'}, dimensions={0}, use_global_device_ids=true | all-gather | bytes 27648 | tf_op jit(solution)/shard_map/all_gather | solution.py:28
  39.0 25.8 %all_gather.7 = bf16[384,256]{1,0:T(8,128)(2,1)S(1)} all-gather(bf16[48,256]{1,0:T(8,128)(2,1)S(1)} %reshape.82), channel_id=1, replica_groups=mesh['y'=8,'z'=8,'x'=4,'c'=2] {'y'}, dimensions={0}, use_global_device_ids=true | all-gather | bytes 221184 | tf_op jit(solution)/shard_map/all_gather | solution.py:29
  64.8 2.8 %fusion = bf16[384,4096]{0,1:T(8,128)(2,1)S(1)} fusion(bf16[384,256]{1,0:T(8,128)(2,1)S(1)} %bitcast.35, bf16[4096,256]{1,0:T(8,128)(2,1)} %param.8, s32[256]{0:T(256)} %param.10, s32[4096]{0:T(1024)S(1)} %bitcast.37), kind=kOutput, calls=%fused_computation.1 | convolution fusion | flops 808976384 | bytes 5456896 | tf_op jit(solution)/shard_map/dot_general | solution.py:34
  67.7 2.9 %copy.29 = bf16[384,4096]{1,0:T(8,128)(2,1)} copy(bf16[384,4096]{0,1:T(8,128)(2,1)S(1)} %fusion) | data formatting | bytes 6291456
  70.6 0.0 reduce-scatter.7.cloned.1.call-update
  70.6 0.0 reduce-scatter.9.cloned.1.call-start
  70.7 16.2 %reduce-scatter.7.cloned.1.call-done = bf16[192,4096]{1,0:T(8,128)(2,1)} async-done(((bf16[384,4096]{1,0:T(8,128)(2,1)}), bf16[192,4096]{1,0:T(8,128)(2,1)}) %reduce-scatter.7.cloned.1.call-update) | async-done | bytes 1572880
  86.8 0.0 reduce-scatter.9.cloned.1.call-update
  86.9 35.4 %reduce-scatter.9.cloned.1.call-done = bf16[48,4096]{1,0:T(8,128)(2,1)} async-done(((bf16[192,4096]{1,0:T(8,128)(2,1)}), bf16[48,4096]{1,0:T(8,128)(2,1)}) %reduce-scatter.9.cloned.1.call-update) | async-done | bytes 393232 | tf_op jit(solution)/shard_map/reduce_scatter | solution.py:37
  122.3 1.5 copy.32
  123.8 0.0 copy-start.2
  123.8 0.0 copy-start.3
  123.8 0.7 copy.37
  124.5 2.5 %reshape.87 = bf16[64,2,1536]{2,1,0:T(2,128)(2,1)} reshape(bf16[512,8,48]{2,1,0:T(8,128)(2,1)S(1)} %bitcast.30) | data formatting | bytes 786432
  127.0 13.4 %all-to-all-start = ((bf16[64,2,1536]{2,1,0:T(2,128)(2,1)}), bf16[64,2,1536]{2,1,0:T(2,128)(2,1)S(1)}, u32[]{:S(2)}, u32[]{:S(2)}) async-start(bf16[64,2,1536]{2,1,0:T(2,128)(2,1)} %reshape.87), calls=%async_computation | async-start | bytes 786432 | tf_op jit(solution)/shard_map/all_to_all | solution.py:40
  140.4 0.0 copy-done.2
  140.4 0.1 dynamic_slice.7
  140.4 0.0 copy-done.3
  140.4 0.1 broadcast_subtract_fusion
  140.5 0.1 sub.45
  140.6 1.3 copy.34
  142.0 14.0 %all-to-all-done = bf16[64,2,1536]{2,1,0:T(2,128)(2,1)S(1)} async-done(((bf16[64,2,1536]{2,1,0:T(2,128)(2,1)}), bf16[64,2,1536]{2,1,0:T(2,128)(2,1)S(1)}, u32[]{:S(2)}, u32[]{:S(2)}) %all-to-all-start) | async-done | bytes 393248 | tf_op jit(solution)/shard_map/all_to_all | solution.py:40
  156.0 1.0 reshape.88
  157.1 0.1 copy.27
  157.2 0.0 copy-start
  157.2 0.0 copy-start.1
  157.2 1.5 copy.28
  158.7 0.0 copy-done
  158.7 0.0 copy-done.1
  158.7 2.2 %divide_convert_fusion = bf16[48,4096]{1,0:T(8,128)(2,1)} fusion(f32[48,4096]{1,0:T(8,128)S(1)} %bitcast.33, f32[48,4096]{1,0:T(8,128)} %copy.28, bf16[48,4096]{1,0:T(8,128)(2,1)S(1)} %copy-done.1, bf16[48,4096]{1,0:T(8,128)(2,1)} %param.13, f32[4096]{0:T(1024)S(1)} %bitcast.36), kind=kLoop, calls=%fused_computation.6 | loop fusion | flops 1376256 | bytes 2768896 | tf_op jit(solution)/shard_map/convert_element_type | solution.py:51
  (5 shorter events, 0.0 us)
Async XLA Ops:
  6.5 80.3 %reduce-scatter.7.cloned.1.call-start = ((), (), s32[]{:S(2)}) async-start(), calls=%async_computation.3 | async-start | bytes 4718592
  70.6 51.7 %reduce-scatter.9.cloned.1.call-start = ((), (), s32[]{:S(2)}) async-start(), calls=%async_computation.4 | async-start | bytes 1966080 | tf_op jit(solution)/shard_map/reduce_scatter | solution.py:37
  123.8 16.6 %copy-start.2 = (f32[512]{0:T(512)S(1)}, f32[512]{0:T(512)}, u32[]{:S(2)}) copy-start(f32[512]{0:T(512)} %param.12) | copy-start | bytes 6148
  123.8 16.7 %copy-start.3 = (f32[48]{0:T(128)S(1)}, f32[48]{0:T(128)}, u32[]{:S(2)}) copy-start(f32[48]{0:T(128)} %param.11) | copy-start | bytes 580
  127.0 29.0 %all-to-all-start = ((bf16[64,2,1536]{2,1,0:T(2,128)(2,1)}), bf16[64,2,1536]{2,1,0:T(2,128)(2,1)S(1)}, u32[]{:S(2)}, u32[]{:S(2)}) async-start(bf16[64,2,1536]{2,1,0:T(2,128)(2,1)} %reshape.87), calls=%async_computation | async-start | bytes 786432 | tf_op jit(solution)/shard_map/all_to_all | solution.py:40
  157.2 1.5 copy-start
  157.2 1.5 copy-start.1
Sparse Core Ops, SparseCore 0:
  70.7 16.0 reduce-scatter.6
  89.9 32.3 reduce-scatter.8

commit v2 on v1

v2 whole, which is shorter than its diff:
```python
import jax
import jax.numpy as jnp
from jax import lax
from jax.sharding import Mesh
from jax.sharding import PartitionSpec as P

WIDE = ("y", "z")
NARROW = ("x", "c")


def gather_rows(block, name):
    n = lax.axis_size(name)
    copies = jnp.broadcast_to(block[None], (n,) + block.shape)
    got = lax.all_to_all(copies, name, 0, 0, tiled=True)
    return got.reshape((n * block.shape[0],) + block.shape[1:])


def local(
    amplitudes, integrals, virtual_irrep, column_irrep, pair_energy, virtual_energy, residual_in
):
    nz = lax.axis_size("z")
    wide_size = lax.axis_size("y") * nz
    num_virt = virtual_irrep.shape[0]
    a_local = num_virt // wide_size
    wide_index = lax.axis_index("y") * nz + lax.axis_index("z")
    first_a = wide_index * a_local
    local_irrep = lax.dynamic_slice_in_dim(virtual_irrep, first_a, a_local, 0)
    row_irrep = jnp.bitwise_xor(local_irrep[:, None], virtual_irrep[None, :]).reshape(
        a_local * num_virt
    )
    masked = jnp.where(
        row_irrep[:, None] == column_irrep[None, :], integrals, jnp.zeros((), integrals.dtype)
    )
    amp = gather_rows(gather_rows(amplitudes, "z"), "y")
    contract = (((1,), (1,)), ((), ()))
    terms = lax.dot_general(amp, masked, contract, preferred_element_type=jnp.float32)
    ladder = lax.psum_scatter(
        terms.astype(jnp.bfloat16), NARROW, scatter_dimension=0, tiled=True
    ).astype(jnp.float32)
    pair_rows = ladder.shape[0]
    outgoing = ladder.astype(jnp.bfloat16).reshape(pair_rows, a_local, wide_size, a_local)
    outgoing = jnp.transpose(outgoing, (2, 0, 1, 3))
    got = lax.all_to_all(outgoing, WIDE, 0, 0, tiled=True)
    mirrored = jnp.transpose(got, (1, 3, 0, 2)).astype(jnp.float32)
    mirrored = mirrored.reshape(pair_rows, a_local * num_virt)
    local_energy = lax.dynamic_slice_in_dim(virtual_energy, first_a, a_local, 0)
    denominator = (
        pair_energy[:, None, None] - local_energy[None, :, None] - virtual_energy[None, None, :]
    )
    denominator = denominator.reshape(pair_rows, a_local * num_virt)
    total = residual_in.astype(jnp.float32) + ladder - mirrored
    return (total / denominator).astype(jnp.bfloat16)


def solution(mesh):
    wide, narrow = mesh.devices.shape
    fine = Mesh(mesh.devices.reshape(8, wide // 8, narrow // 2, 2), ("y", "z", "x", "c"))
    return jax.shard_map(
        local,
        mesh=fine,
        in_specs=(
            P(WIDE, NARROW),
            P(WIDE, NARROW),
            P(),
            P(NARROW),
            P(NARROW),
            P(),
            P(NARROW, WIDE),
        ),
        out_specs=P(NARROW, WIDE),
        check_vma=False,
    )
```

time: 168 us -> 125 us (0.74)
  the two profiles are of different devices: /device:TPU:16 before, /device:TPU:23 now
where the time goes in v2:
time: 125 us
  waiting for transfers between devices  56.1 us (45%)
  starting transfers between devices  19.7 us (16%)
  blocking collectives  16.7 us (13%)
  between operations  13.5 us (11%)
  local copies, waits for them, and re-layouts  12.9 us (10%)
  other arithmetic  3.25 us (3%)
  matrix products  2.78 us (2%)
    reduce_scatter x1, waiting for transfers between devices, local(): lax.psum_scatter(terms.astype(jnp.bfloat16), NARROW, scatter_dimension=0,...  35.6 us
    all_to_all x1, blocking collectives, gather_rows(): got = lax.all_to_all(copies, name, 0, 0, tiled=True)  16.7 us
    all_to_all x1, waiting for transfers between devices, local(): got = lax.all_to_all(outgoing, WIDE, 0, 0, tiled=True)  15.9 us
    all_to_all x1, starting transfers between devices, local(): got = lax.all_to_all(outgoing, WIDE, 0, 0, tiled=True)  12.8 us
    unnamed x14, local copies, waits for them, and re-layouts  8.44 us
    all_to_all x1, starting transfers between devices, gather_rows(): got = lax.all_to_all(copies, name, 0, 0, tiled=True)  6.87 us
    all_to_all x1, waiting for transfers between devices, gather_rows(): got = lax.all_to_all(copies, name, 0, 0, tiled=True)  4.51 us
    dot_general x1, matrix products, local(): lax.dot_general(amp, masked, contract, preferred_element_type=jnp.float32)  2.78 us
  transfers between devices with their start and end apart: 3, of which 3 were waited for; matrix products, arithmetic and copies ran while one was open for 2% of the time, Pallas kernels for 0%

profile of v2, /device:TPU:23, one launch (start us, length us, event | category | flops | bytes accessed | tf_op | source)
XLA Modules:
  0.0 125.0 jit_solution(8988951293922036562)
XLA Ops:
  6.5 0.7 broadcast_in_dim.11
  7.2 16.7 %all_to_all.15 = bf16[8,6,256]{2,1,0:T(8,128)(2,1)S(1)} all-to-all(bf16[8,6,256]{2,1,0:T(8,128)(2,1)S(1)} %broadcast_in_dim.11), channel_id=1, replica_groups=mesh['y'=8,'z'=8,'x'=4,'c'=2] {'z'}, dimensions={0} | all-to-all | bytes 49152 | tf_op jit(solution)/shard_map/all_to_all | solution.py:14
  23.9 0.7 broadcast_in_dim.13
  24.6 6.9 %all-to-all-start.1 = ((bf16[8,48,256]{2,1,0:T(8,128)(2,1)}), bf16[8,48,256]{2,1,0:T(8,128)(2,1)S(1)}, u32[]{:S(2)}, u32[]{:S(2)}) async-start(bf16[8,48,256]{2,1,0:T(8,128)(2,1)} %broadcast_in_dim.13), calls=%async_computation.1 | async-start | bytes 393216 | tf_op jit(solution)/shard_map/all_to_all | solution.py:14
  31.5 0.0 reduce-scatter.4.cloned.1.call-start
  31.5 0.8 dynamic_slice.6
  32.3 0.8 xor_bitcast_fusion
  33.0 4.5 %all-to-all-done.1 = bf16[8,48,256]{2,1,0:T(8,128)(2,1)S(1)} async-done(((bf16[8,48,256]{2,1,0:T(8,128)(2,1)}), bf16[8,48,256]{2,1,0:T(8,128)(2,1)S(1)}, u32[]{:S(2)}, u32[]{:S(2)}) %all-to-all-start.1) | async-done | bytes 196640 | tf_op jit(solution)/shard_map/all_to_all | solution.py:14
  37.5 2.8 %fusion = bf16[384,4096]{0,1:T(8,128)(2,1)S(1)} fusion(bf16[384,256]{1,0:T(8,128)(2,1)S(1)} %bitcast.32, bf16[4096,256]{1,0:T(8,128)(2,1)} %param.8, s32[256]{0:T(256)} %param.10, s32[4096]{0:T(1024)S(1)} %bitcast.34), kind=kOutput, calls=%fused_computation.1 | convolution fusion | flops 808976384 | bytes 5456896 | tf_op jit(solution)/shard_map/dot_general | solution.py:36
  40.3 2.9 %copy.25 = bf16[384,4096]{1,0:T(8,128)(2,1)} copy(bf16[384,4096]{0,1:T(8,128)(2,1)S(1)} %fusion) | data formatting | bytes 6291456
  43.3 0.0 reduce-scatter.4.cloned.1.call-update
  43.3 35.6 %reduce-scatter.4.cloned.1.call-done = bf16[48,4096]{1,0:T(8,128)(2,1)} async-done(((bf16[384,4096]{1,0:T(8,128)(2,1)}), bf16[48,4096]{1,0:T(8,128)(2,1)}) %reduce-scatter.4.cloned.1.call-update) | async-done | bytes 393232 | tf_op jit(solution)/shard_map/reduce_scatter | solution.py:37
  78.9 1.5 %copy.26 = bf16[48,4096]{0,1:T(8,128)(2,1)S(1)} copy(bf16[48,4096]{1,0:T(8,128)(2,1)} %reduce-scatter.4.cloned.1.call-done) | data formatting | bytes 786432
  80.4 0.0 copy-start.1
  80.4 0.0 copy-start.2
  80.4 0.3 copy.33
  80.7 2.5 %reshape.77 = bf16[64,2,1536]{2,1,0:T(2,128)(2,1)} reshape(bf16[64,8,8,48]{3,2,1,0:T(8,128)(2,1)S(1)} %bitcast.28) | data formatting | bytes 786432
  83.2 12.8 %all-to-all-start.2 = ((bf16[64,2,1536]{2,1,0:T(2,128)(2,1)}), bf16[64,2,1536]{2,1,0:T(2,128)(2,1)S(1)}, u32[]{:S(2)}, u32[]{:S(2)}) async-start(bf16[64,2,1536]{2,1,0:T(2,128)(2,1)} %reshape.77), calls=%async_computation.2 | async-start | bytes 786432 | tf_op jit(solution)/shard_map/all_to_all | solution.py:43
  96.0 0.0 copy-done.1
  96.1 0.1 dynamic_slice.7
  96.1 0.0 copy-done.2
  96.1 0.1 broadcast_subtract_fusion
  96.2 0.1 sub.45
  96.3 0.5 copy.28
  96.8 15.9 %all-to-all-done.2 = bf16[64,2,1536]{2,1,0:T(2,128)(2,1)S(1)} async-done(((bf16[64,2,1536]{2,1,0:T(2,128)(2,1)}), bf16[64,2,1536]{2,1,0:T(2,128)(2,1)S(1)}, u32[]{:S(2)}, u32[]{:S(2)}) %all-to-all-start.2) | async-done | bytes 393248 | tf_op jit(solution)/shard_map/all_to_all | solution.py:43
  112.8 1.0 reshape.78
  113.8 0.2 convert_bitcast_fusion
  114.1 0.4 copy.23
  114.5 0.0 copy-start
  114.5 1.5 %copy.24 = f32[48,4096]{1,0:T(8,128)} copy(f32[48,4096]{0,1:T(8,128)S(1)} %bitcast.27) | data formatting | bytes 1572864 | tf_op jit(solution)/shard_map/reshape | solution.py:45
  116.0 0.0 copy-done
  116.0 2.2 %divide_convert_fusion = bf16[48,4096]{1,0:T(8,128)(2,1)} fusion(f32[48,4096]{1,0:T(8,128)S(1)} %bitcast.31, f32[48,4096]{1,0:T(8,128)} %copy.24, bf16[48,4096]{1,0:T(8,128)(2,1)S(1)} %copy-done, bf16[48,4096]{1,0:T(8,128)(2,1)} %param.13, f32[4096]{0:T(1024)S(1)} %bitcast.33), kind=kLoop, calls=%fused_computation.8 | loop fusion | flops 1376256 | bytes 2768896 | tf_op jit(solution)/shard_map/convert_element_type | solution.py:52
  (4 shorter events, 0.0 us)
Async XLA Ops:
  24.6 12.9 %all-to-all-start.1 = ((bf16[8,48,256]{2,1,0:T(8,128)(2,1)}), bf16[8,48,256]{2,1,0:T(8,128)(2,1)S(1)}, u32[]{:S(2)}, u32[]{:S(2)}) async-start(bf16[8,48,256]{2,1,0:T(8,128)(2,1)} %broadcast_in_dim.13), calls=%async_computation.1 | async-start | bytes 393216 | tf_op jit(solution)/shard_map/all_to_all | solution.py:14
  31.5 47.4 %reduce-scatter.4.cloned.1.call-start = ((), (), s32[]{:S(2)}) async-start(), calls=%async_computation.4 | async-start | bytes 3538944 | tf_op jit(solution)/shard_map/reduce_scatter | solution.py:37
  80.4 15.6 %copy-start.1 = (f32[512]{0:T(512)S(1)}, f32[512]{0:T(512)}, u32[]{:S(2)}) copy-start(f32[512]{0:T(512)} %param.12) | copy-start | bytes 6148
  80.4 15.7 %copy-start.2 = (f32[48]{0:T(128)S(1)}, f32[48]{0:T(128)}, u32[]{:S(2)}) copy-start(f32[48]{0:T(128)} %param.11) | copy-start | bytes 580
  83.2 29.5 %all-to-all-start.2 = ((bf16[64,2,1536]{2,1,0:T(2,128)(2,1)}), bf16[64,2,1536]{2,1,0:T(2,128)(2,1)S(1)}, u32[]{:S(2)}, u32[]{:S(2)}) async-start(bf16[64,2,1536]{2,1,0:T(2,128)(2,1)} %reshape.77), calls=%async_computation.2 | async-start | bytes 786432 | tf_op jit(solution)/shard_map/all_to_all | solution.py:43
  114.5 1.5 %copy-start = (bf16[48,4096]{1,0:T(8,128)(2,1)S(1)}, bf16[48,4096]{1,0:T(8,128)(2,1)}, u32[]{:S(2)}) copy-start(bf16[48,4096]{1,0:T(8,128)(2,1)} %reduce-scatter.4.cloned.1.call-done) | copy-start | bytes 1179652
Sparse Core Ops, SparseCore 0:
  43.4 35.4 reduce-scatter.3

commit v3 on v2

--- a/solution.py
+++ b/solution.py
@@ -22,33 +22,37 @@
     wide_size = lax.axis_size("y") * nz
     num_virt = virtual_irrep.shape[0]
     a_local = num_virt // wide_size
+    cd_local = integrals.shape[1]
     wide_index = lax.axis_index("y") * nz + lax.axis_index("z")
     first_a = wide_index * a_local
+    outgoing = integrals.reshape(a_local, wide_size, a_local, cd_local).transpose(1, 0, 2, 3)
+    got = lax.all_to_all(outgoing, WIDE, 0, 0, tiled=True)
+    swapped = got.transpose(2, 0, 1, 3).reshape(a_local * num_virt, cd_local)
     local_irrep = lax.dynamic_slice_in_dim(virtual_irrep, first_a, a_local, 0)
     row_irrep = jnp.bitwise_xor(local_irrep[:, None], virtual_irrep[None, :]).reshape(
         a_local * num_virt
     )
-    masked = jnp.where(
-        row_irrep[:, None] == column_irrep[None, :], integrals, jnp.zeros((), integrals.dtype)
-    )
+    keep = row_irrep[:, None] == column_irrep[None, :]
+    zero = jnp.zeros((), integrals.dtype)
+    masked = jnp.where(keep, integrals, zero)
+    masked_swapped = jnp.where(keep, swapped, zero)
     amp = gather_rows(gather_rows(amplitudes, "z"), "y")
     contract = (((1,), (1,)), ((), ()))
-    terms = lax.dot_general(amp, masked, contract, preferred_element_type=jnp.float32)
+    direct = lax.dot_general(amp, masked, contract, preferred_element_type=jnp.float32)
+    mirror = lax.dot_general(amp, masked_swapped, contract, preferred_element_type=jnp.float32)
+    diff = direct.astype(jnp.bfloat16).astype(jnp.float32) - mirror.astype(
+        jnp.bfloat16
+    ).astype(jnp.float32)
     ladder = lax.psum_scatter(
-        terms.astype(jnp.bfloat16), NARROW, scatter_dimension=0, tiled=True
+        diff.astype(jnp.bfloat16), NARROW, scatter_dimension=0, tiled=True
     ).astype(jnp.float32)
     pair_rows = ladder.shape[0]
-    outgoing = ladder.astype(jnp.bfloat16).reshape(pair_rows, a_local, wide_size, a_local)
-    outgoing = jnp.transpose(outgoing, (2, 0, 1, 3))
-    got = lax.all_to_all(outgoing, WIDE, 0, 0, tiled=True)
-    mirrored = jnp.transpose(got, (1, 3, 0, 2)).astype(jnp.float32)
-    mirrored = mirrored.reshape(pair_rows, a_local * num_virt)
     local_energy = lax.dynamic_slice_in_dim(virtual_energy, first_a, a_local, 0)
     denominator = (
         pair_energy[:, None, None] - local_energy[None, :, None] - virtual_energy[None, None, :]
     )
     denominator = denominator.reshape(pair_rows, a_local * num_virt)
-    total = residual_in.astype(jnp.float32) + ladder - mirrored
+    total = residual_in.astype(jnp.float32) + ladder
     return (total / denominator).astype(jnp.bfloat16)
 
 

time: 125 us -> 156 us (1.25)
  the two profiles are of different devices: /device:TPU:23 before, /device:TPU:8 now
where the time goes in v3:
time: 156 us; the launch traced here: 155 us
  waiting for transfers between devices  95 us (61%)
  starting transfers between devices  27.9 us (18%)
  between operations  13.5 us (9%)
  local copies, waits for them, and re-layouts  9.97 us (6%)
  other arithmetic  5.24 us (3%)
  matrix products  3.71 us (2%)
    all_to_all x1, waiting for transfers between devices, local(): got = lax.all_to_all(outgoing, WIDE, 0, 0, tiled=True)  50.8 us
    reduce_scatter x1, waiting for transfers between devices, local(): lax.psum_scatter(diff.astype(jnp.bfloat16), NARROW, scatter_dimension=0,...  34.3 us
    all_to_all x2, starting transfers between devices, gather_rows(): got = lax.all_to_all(copies, name, 0, 0, tiled=True)  19.1 us
    all_to_all x2, waiting for transfers between devices, gather_rows(): got = lax.all_to_all(copies, name, 0, 0, tiled=True)  9.92 us
    all_to_all x1, starting transfers between devices, local(): got = lax.all_to_all(outgoing, WIDE, 0, 0, tiled=True)  8.79 us
    unnamed x19, local copies, waits for them, and re-layouts  4.38 us
    transpose x1, local copies, waits for them, and re-layouts, local(): integrals.reshape(a_local, wide_size, a_local, cd_local)  3.2 us
  transfers between devices with their start and end apart: 4, of which 4 were waited for; matrix products, arithmetic and copies ran while one was open for 5% of the time, Pallas kernels for 0%

profile of v3, /device:TPU:8, one launch (start us, length us, event | category | flops | bytes accessed | tf_op | source)
XLA Modules:
  0.0 155.4 jit_solution(1849229819533575275)
XLA Ops:
  6.5 1.3 broadcast_in_dim.14
  7.8 10.3 %all-to-all-start = ((bf16[8,6,256]{2,1,0:T(8,128)(2,1)}), bf16[8,6,256]{2,1,0:T(8,128)(2,1)S(1)}, u32[]{:S(2)}, u32[]{:S(2)}) async-start(bf16[8,6,256]{2,1,0:T(8,128)(2,1)} %broadcast_in_dim.14), calls=%async_computation | async-start | bytes 65536 | tf_op jit(solution)/shard_map/all_to_all | solution.py:14
  18.2 3.2 %copy.20 = bf16[64,8,8,256]{3,2,1,0:T(8,128)(2,1)} copy(bf16[64,8,8,256]{3,2,0,1:T(8,128)(2,1)} %bitcast.24) | data formatting | bytes 4194304 | tf_op jit(solution)/shard_map/transpose | solution.py:28
  21.4 0.0 copy-start.3
  21.4 0.0 copy-start.5
  21.4 4.8 %all-to-all-done = bf16[8,6,256]{2,1,0:T(8,128)(2,1)S(1)} async-done(((bf16[8,6,256]{2,1,0:T(8,128)(2,1)}), bf16[8,6,256]{2,1,0:T(8,128)(2,1)S(1)}, u32[]{:S(2)}, u32[]{:S(2)}) %all-to-all-start) | async-done | bytes 24608 | tf_op jit(solution)/shard_map/all_to_all | solution.py:14
  26.2 8.8 %all-to-all-start.2 = ((bf16[64,8,8,256]{3,2,1,0:T(8,128)(2,1)}), bf16[64,8,8,256]{3,2,1,0:T(8,128)(2,1)S(1)}, u32[]{:S(2)}, u32[]{:S(2)}) async-start(bf16[64,8,8,256]{3,2,1,0:T(8,128)(2,1)} %copy.20), calls=%async_computation.2 | async-start | bytes 4194304 | tf_op jit(solution)/shard_map/all_to_all | solution.py:29
  35.0 0.0 copy-done.3
  35.0 0.1 xor.34
  35.1 0.1 dynamic_slice.6
  35.2 0.1 broadcast_xor_fusion
  35.3 50.8 %all-to-all-done.2 = bf16[64,8,8,256]{3,2,1,0:T(8,128)(2,1)S(1)} async-done(((bf16[64,8,8,256]{3,2,1,0:T(8,128)(2,1)}), bf16[64,8,8,256]{3,2,1,0:T(8,128)(2,1)S(1)}, u32[]{:S(2)}, u32[]{:S(2)}) %all-to-all-start.2) | async-done | bytes 2097184 | tf_op jit(solution)/shard_map/all_to_all | solution.py:29
  86.1 0.0 copy-start
  86.1 0.7 broadcast_in_dim.29
  86.8 8.8 %all-to-all-start.1 = ((bf16[8,48,256]{2,1,0:T(8,128)(2,1)}), bf16[8,48,256]{2,1,0:T(8,128)(2,1)S(1)}, u32[]{:S(2)}, u32[]{:S(2)}) async-start(bf16[8,48,256]{2,1,0:T(8,128)(2,1)} %broadcast_in_dim.29), calls=%async_computation.1 | async-start | bytes 393216 | tf_op jit(solution)/shard_map/all_to_all | solution.py:14
  95.6 0.0 reduce-scatter.4.cloned.1.call-start
  95.6 0.1 xor_bitcast_fusion
  95.7 0.0 copy-done
  95.7 0.0 copy-done.5
  95.7 3.1 %compare_select_fusion = bf16[8,64,8,256]{3,2,1,0:T(8,128)(2,1)S(1)} fusion(bf16[64,8,8,256]{3,2,1,0:T(8,128)(2,1)} %copy-done, s32[256]{0:T(256)S(1)} %copy-done.5, s32[8,64,8]{2,1,0:T(8,128)S(1)} %broadcast_xor_fusion), kind=kLoop, calls=%fused_computation.4 | loop fusion | flops 2097152 | bytes 4211712 | tf_op jit(solution)/shard_map/jit(_where)/select_n | solution.py:38
  98.8 5.1 %all-to-all-done.1 = bf16[8,48,256]{2,1,0:T(8,128)(2,1)S(1)} async-done(((bf16[8,48,256]{2,1,0:T(8,128)(2,1)}), bf16[8,48,256]{2,1,0:T(8,128)(2,1)S(1)}, u32[]{:S(2)}, u32[]{:S(2)}) %all-to-all-start.1) | async-done | bytes 196640 | tf_op jit(solution)/shard_map/all_to_all | solution.py:14
  103.9 0.0 copy-start.1
  103.9 1.3 convolution_convert_fusion
  105.2 0.3 copy-done.1
  105.5 2.4 %fusion = bf16[384,4096]{0,1:T(8,128)(2,1)S(1)} fusion(bf16[4096,384]{1,0:T(8,128)(2,1)S(1)} %convolution_convert_fusion, bf16[384,256]{1,0:T(8,128)(2,1)S(1)} %bitcast.26, bf16[4096,256]{1,0:T(8,128)(2,1)S(1)} %copy-done.1, s32[256]{0:T(256)S(1)} %copy-done.5, s32[4096]{0:T(1024)S(1)} %bitcast.28), kind=kOutput, calls=%fused_computation.3 | convolution fusion | flops 815267840 | bytes 8602624 | tf_op jit(solution)/shard_map/dot_general | solution.py:41
  107.9 2.9 %copy.23 = bf16[384,4096]{1,0:T(8,128)(2,1)} copy(bf16[384,4096]{0,1:T(8,128)(2,1)S(1)} %fusion) | data formatting | bytes 6291456
  110.8 0.0 copy-start.4
  110.8 0.0 copy-start.6
  110.8 0.0 copy-start.2
  110.8 0.0 reduce-scatter.4.cloned.1.call-update
  110.9 0.7 copy-done.4
  111.5 0.1 dynamic_slice.7
  111.6 0.0 copy-done.6
  111.6 0.1 broadcast_subtract_fusion
  111.7 0.1 sub.46
  111.8 0.5 copy.26
  112.3 34.3 %reduce-scatter.4.cloned.1.call-done = bf16[48,4096]{1,0:T(8,128)(2,1)} async-done(((bf16[384,4096]{1,0:T(8,128)(2,1)}), bf16[48,4096]{1,0:T(8,128)(2,1)}) %reduce-scatter.4.cloned.1.call-update) | async-done | bytes 393232 | tf_op jit(solution)/shard_map/reduce_scatter | solution.py:46
  146.6 0.0 copy-done.2
  146.6 1.9 %divide_convert_fusion = bf16[48,4096]{1,0:T(8,128)(2,1)} fusion(f32[48,4096]{1,0:T(8,128)S(1)} %bitcast.23, bf16[48,4096]{1,0:T(8,128)(2,1)} %reduce-scatter.4.cloned.1.call-done, bf16[48,4096]{1,0:T(8,128)(2,1)S(1)} %copy-done.2, f32[4096]{0:T(1024)S(1)} %bitcast.27), kind=kLoop, calls=%fused_computation.9 | loop fusion | flops 1179648 | bytes 1982464 | tf_op jit(solution)/shard_map/convert_element_type | solution.py:56
  (4 shorter events, 0.0 us)
Async XLA Ops:
  7.8 18.3 %all-to-all-start = ((bf16[8,6,256]{2,1,0:T(8,128)(2,1)}), bf16[8,6,256]{2,1,0:T(8,128)(2,1)S(1)}, u32[]{:S(2)}, u32[]{:S(2)}) async-start(bf16[8,6,256]{2,1,0:T(8,128)(2,1)} %broadcast_in_dim.14), calls=%async_computation | async-start | bytes 65536 | tf_op jit(solution)/shard_map/all_to_all | solution.py:14
  21.4 13.6 %copy-start.3 = (s32[512]{0:T(512)S(1)}, s32[512]{0:T(512)}, u32[]{:S(2)}) copy-start(s32[512]{0:T(512)} %param.9) | copy-start | bytes 6148
  21.4 74.3 %copy-start.5 = (s32[256]{0:T(256)S(1)}, s32[256]{0:T(256)}, u32[]{:S(2)}) copy-start(s32[256]{0:T(256)} %param.10) | copy-start | bytes 3076
  26.2 59.9 %all-to-all-start.2 = ((bf16[64,8,8,256]{3,2,1,0:T(8,128)(2,1)}), bf16[64,8,8,256]{3,2,1,0:T(8,128)(2,1)S(1)}, u32[]{:S(2)}, u32[]{:S(2)}) async-start(bf16[64,8,8,256]{3,2,1,0:T(8,128)(2,1)} %copy.20), calls=%async_computation.2 | async-start | bytes 4194304 | tf_op jit(solution)/shard_map/all_to_all | solution.py:29
  86.1 9.6 %copy-start = (bf16[64,8,8,256]{3,2,1,0:T(8,128)(2,1)}, bf16[64,8,8,256]{3,2,1,0:T(8,128)(2,1)S(1)}, u32[]{:S(2)}) copy-start(bf16[64,8,8,256]{3,2,1,0:T(8,128)(2,1)S(1)} %all-to-all-done.2) | copy-start | bytes 6291460
  86.8 17.1 %all-to-all-start.1 = ((bf16[8,48,256]{2,1,0:T(8,128)(2,1)}), bf16[8,48,256]{2,1,0:T(8,128)(2,1)S(1)}, u32[]{:S(2)}, u32[]{:S(2)}) async-start(bf16[8,48,256]{2,1,0:T(8,128)(2,1)} %broadcast_in_dim.29), calls=%async_computation.1 | async-start | bytes 393216 | tf_op jit(solution)/shard_map/all_to_all | solution.py:14
  95.6 51.0 %reduce-scatter.4.cloned.1.call-start = ((), (), s32[]{:S(2)}) async-start(), calls=%async_computation.4 | async-start | bytes 3538944 | tf_op jit(solution)/shard_map/reduce_scatter | solution.py:46
  103.9 1.6 %copy-start.1 = (bf16[4096,256]{1,0:T(8,128)(2,1)S(1)}, bf16[4096,256]{1,0:T(8,128)(2,1)}, u32[]{:S(2)}) copy-start(bf16[4096,256]{1,0:T(8,128)(2,1)} %param.8) | copy-start | bytes 6291460
  110.8 0.7 copy-start.4
  110.8 0.8 copy-start.6
  110.8 35.8 %copy-start.2 = (bf16[48,4096]{1,0:T(8,128)(2,1)S(1)}, bf16[48,4096]{1,0:T(8,128)(2,1)}, u32[]{:S(2)}) copy-start(bf16[48,4096]{1,0:T(8,128)(2,1)} %param.13) | copy-start | bytes 1179652
Sparse Core Ops, SparseCore 0:
  111.0 35.5 reduce-scatter.3

commit v4 on v2

--- a/solution.py
+++ b/solution.py
@@ -34,9 +34,13 @@
     amp = gather_rows(gather_rows(amplitudes, "z"), "y")
     contract = (((1,), (1,)), ((), ()))
     terms = lax.dot_general(amp, masked, contract, preferred_element_type=jnp.float32)
-    ladder = lax.psum_scatter(
-        terms.astype(jnp.bfloat16), NARROW, scatter_dimension=0, tiled=True
-    ).astype(jnp.float32)
+    nx, nc = lax.axis_size("x"), lax.axis_size("c")
+    block = terms.shape[0] // (nx * nc)
+    parts = terms.astype(jnp.bfloat16).reshape(nx, nc, block, terms.shape[1])
+    parts = lax.all_to_all(parts, "c", 1, 1, tiled=True)
+    parts = parts.astype(jnp.float32).sum(axis=1).astype(jnp.bfloat16)
+    parts = lax.all_to_all(parts, "x", 0, 0, tiled=True)
+    ladder = parts.astype(jnp.float32).sum(axis=0)
     pair_rows = ladder.shape[0]
     outgoing = ladder.astype(jnp.bfloat16).reshape(pair_rows, a_local, wide_size, a_local)
     outgoing = jnp.transpose(outgoing, (2, 0, 1, 3))

time: 125 us -> 103 us (0.82)
  the two profiles are of different devices: /device:TPU:23 before, /device:TPU:16 now
where the time goes in v4:
time: 103 us
  blocking collectives  49.7 us (48%)
  waiting for transfers between devices  19.8 us (19%)
  starting transfers between devices  14.2 us (14%)
  local copies, waits for them, and re-layouts  10.2 us (10%)
  other arithmetic  5.94 us (6%)
  matrix products  2.64 us (3%)
    all_to_all x1, blocking collectives, local(): parts = lax.all_to_all(parts, 'x', 0, 0, tiled=True)  25.3 us
    all_to_all x1, blocking collectives, gather_rows(): got = lax.all_to_all(copies, name, 0, 0, tiled=True)  18.1 us
    all_to_all x1, waiting for transfers between devices, local(): got = lax.all_to_all(outgoing, WIDE, 0, 0, tiled=True)  14.2 us
    all_to_all x1, starting transfers between devices, gather_rows(): got = lax.all_to_all(copies, name, 0, 0, tiled=True)  7.43 us
    all_to_all x1, starting transfers between devices, local(): got = lax.all_to_all(outgoing, WIDE, 0, 0, tiled=True)  6.79 us
    all_to_all x1, blocking collectives, local(): parts = lax.all_to_all(parts, 'c', 1, 1, tiled=True)  6.26 us
    all_to_all x1, waiting for transfers between devices, gather_rows(): got = lax.all_to_all(copies, name, 0, 0, tiled=True)  5.65 us
    unnamed x12, local copies, waits for them, and re-layouts  4.89 us
  transfers between devices with their start and end apart: 2, of which 2 were waited for; matrix products, arithmetic and copies ran while one was open for 3% of the time, Pallas kernels for 0%

profile of v4, /device:TPU:16, one launch (start us, length us, event | category | flops | bytes accessed | tf_op | source)
XLA Modules:
  0.0 102.7 jit_solution(3345466824232297659)
XLA Ops:
  0.0 0.7 broadcast_in_dim.11
  0.7 18.1 %all_to_all.25 = bf16[8,6,256]{2,1,0:T(8,128)(2,1)S(1)} all-to-all(bf16[8,6,256]{2,1,0:T(8,128)(2,1)S(1)} %broadcast_in_dim.11), channel_id=1, replica_groups=mesh['y'=8,'z'=8,'x'=4,'c'=2] {'z'}, dimensions={0} | all-to-all | bytes 49152 | tf_op jit(solution)/shard_map/all_to_all | solution.py:14
  18.8 0.7 broadcast_in_dim.13
  19.5 7.4 %all-to-all-start.1 = ((bf16[8,48,256]{2,1,0:T(8,128)(2,1)}), bf16[8,48,256]{2,1,0:T(8,128)(2,1)S(1)}, u32[]{:S(2)}, u32[]{:S(2)}) async-start(bf16[8,48,256]{2,1,0:T(8,128)(2,1)} %broadcast_in_dim.13), calls=%async_computation.1 | async-start | bytes 393216 | tf_op jit(solution)/shard_map/all_to_all | solution.py:14
  27.0 0.8 dynamic_slice.6
  27.7 0.8 xor_bitcast_fusion
  28.5 5.6 %all-to-all-done.1 = bf16[8,48,256]{2,1,0:T(8,128)(2,1)S(1)} async-done(((bf16[8,48,256]{2,1,0:T(8,128)(2,1)}), bf16[8,48,256]{2,1,0:T(8,128)(2,1)S(1)}, u32[]{:S(2)}, u32[]{:S(2)}) %all-to-all-start.1) | async-done | bytes 196640 | tf_op jit(solution)/shard_map/all_to_all | solution.py:14
  34.1 2.6 %convolution_convert_fusion = bf16[4096,384]{0,1:T(8,128)(2,1)S(1)} fusion(bf16[384,256]{1,0:T(8,128)(2,1)S(1)} %bitcast.30, bf16[4096,256]{1,0:T(8,128)(2,1)} %param.8, s32[256]{0:T(256)} %param.10, s32[4096]{0:T(1024)S(1)} %bitcast.32), kind=kOutput, calls=%fused_computation | convolution fusion | flops 808976384 | bytes 5456896 | tf_op jit(solution)/shard_map/dot_general | solution.py:36
  36.8 0.3 copy.17
  37.1 6.3 %all_to_all.26 = bf16[4,2,48,4096]{3,2,0,1:T(8,128)(2,1)S(1)} all-to-all(bf16[4,2,48,4096]{3,2,0,1:T(8,128)(2,1)S(1)} %copy.17), channel_id=1, replica_groups=mesh['y'=8,'z'=8,'x'=4,'c'=2] {'c'}, dimensions={1} | all-to-all | bytes 6291456 | tf_op jit(solution)/shard_map/all_to_all | solution.py:40
  43.4 2.3 %reduce_sum.21 = bf16[4,48,4096]{2,1,0:T(8,128)(2,1)} reduce(bf16[4,2,48,4096]{3,2,0,1:T(8,128)(2,1)S(1)} %all_to_all.26, bf16[]{:T(256)} %constant.18.clone.1), dimensions={1}, to_apply=%region_0.1 | reduce | flops 786432 | bytes 4718594 | tf_op jit(solution)/shard_map/reduce_sum | solution.py:41
  45.7 25.3 %all_to_all.27 = bf16[4,48,4096]{2,1,0:T(8,128)(2,1)S(1)} all-to-all(bf16[4,48,4096]{2,1,0:T(8,128)(2,1)} %reduce_sum.21), channel_id=1, replica_groups=mesh['y'=8,'z'=8,'x'=4,'c'=2] {'x'}, dimensions={0} | all-to-all | bytes 3145728 | tf_op jit(solution)/shard_map/all_to_all | solution.py:42
  71.0 0.2 convert_reduce_fusion
  71.3 0.5 copy.18
  71.8 0.0 copy-start.1
  71.8 0.0 copy-start.2
  71.8 0.3 copy.26
  72.1 2.5 %reshape.78 = bf16[64,2,1536]{2,1,0:T(2,128)(2,1)} reshape(bf16[64,8,8,48]{3,2,1,0:T(8,128)(2,1)S(1)} %bitcast.26) | data formatting | bytes 786432
  74.6 6.8 %all-to-all-start.4 = ((bf16[64,2,1536]{2,1,0:T(2,128)(2,1)}), bf16[64,2,1536]{2,1,0:T(2,128)(2,1)S(1)}, u32[]{:S(2)}, u32[]{:S(2)}) async-start(bf16[64,2,1536]{2,1,0:T(2,128)(2,1)} %reshape.78), calls=%async_computation.4 | async-start | bytes 786432 | tf_op jit(solution)/shard_map/all_to_all | solution.py:47
  81.4 0.0 copy-done.1
  81.4 0.1 dynamic_slice.7
  81.5 0.0 copy-done.2
  81.5 0.1 broadcast_subtract_fusion
  81.5 0.1 sub.45
  81.7 1.3 %copy.23 = f32[6,8,8,512]{3,1,2,0:T(8,128)} copy(f32[6,8,8,512]{3,2,1,0:T(8,128)S(1)} %bitcast.28) | data formatting | bytes 1572864
  83.0 14.2 %all-to-all-done.4 = bf16[64,2,1536]{2,1,0:T(2,128)(2,1)S(1)} async-done(((bf16[64,2,1536]{2,1,0:T(2,128)(2,1)}), bf16[64,2,1536]{2,1,0:T(2,128)(2,1)S(1)}, u32[]{:S(2)}, u32[]{:S(2)}) %all-to-all-start.4) | async-done | bytes 393248 | tf_op jit(solution)/shard_map/all_to_all | solution.py:47
  97.2 1.0 %reshape.79 = bf16[64,8,8,48]{3,2,1,0:T(8,128)(2,1)S(1)} reshape(bf16[64,2,1536]{2,1,0:T(2,128)(2,1)S(1)} %all-to-all-done.4) | data formatting | bytes 786432
  98.3 0.2 convert_bitcast_fusion
  98.5 0.4 copy.20
  98.9 0.0 copy-start
  98.9 1.5 %copy.21 = f32[48,4096]{1,0:T(8,128)} copy(f32[48,4096]{0,1:T(8,128)S(1)} %bitcast.24) | data formatting | bytes 1572864 | tf_op jit(solution)/shard_map/reshape | solution.py:49
  100.4 0.0 copy-done
  100.4 2.3 %divide_convert_fusion = bf16[48,4096]{1,0:T(8,128)(2,1)} fusion(f32[48,4096]{1,0:T(8,128)} %bitcast.29, f32[48,4096]{1,0:T(8,128)} %copy.21, f32[48,4096]{1,0:T(8,128)S(1)} %convert_reduce_fusion, bf16[48,4096]{1,0:T(8,128)(2,1)S(1)} %copy-done, f32[4096]{0:T(1024)S(1)} %bitcast.31), kind=kLoop, calls=%fused_computation.7 | loop fusion | flops 1179648 | bytes 3162112 | tf_op jit(solution)/shard_map/convert_element_type | solution.py:56
  (5 shorter events, 0.1 us)
Async XLA Ops:
  19.5 14.6 %all-to-all-start.1 = ((bf16[8,48,256]{2,1,0:T(8,128)(2,1)}), bf16[8,48,256]{2,1,0:T(8,128)(2,1)S(1)}, u32[]{:S(2)}, u32[]{:S(2)}) async-start(bf16[8,48,256]{2,1,0:T(8,128)(2,1)} %broadcast_in_dim.13), calls=%async_computation.1 | async-start | bytes 393216 | tf_op jit(solution)/shard_map/all_to_all | solution.py:14
  71.8 9.6 %copy-start.1 = (f32[512]{0:T(512)S(1)}, f32[512]{0:T(512)}, u32[]{:S(2)}) copy-start(f32[512]{0:T(512)} %param.12) | copy-start | bytes 6148
  71.8 9.7 %copy-start.2 = (f32[48]{0:T(128)S(1)}, f32[48]{0:T(128)}, u32[]{:S(2)}) copy-start(f32[48]{0:T(128)} %param.11) | copy-start | bytes 580
  74.6 22.6 %all-to-all-start.4 = ((bf16[64,2,1536]{2,1,0:T(2,128)(2,1)}), bf16[64,2,1536]{2,1,0:T(2,128)(2,1)S(1)}, u32[]{:S(2)}, u32[]{:S(2)}) async-start(bf16[64,2,1536]{2,1,0:T(2,128)(2,1)} %reshape.78), calls=%async_computation.4 | async-start | bytes 786432 | tf_op jit(solution)/shard_map/all_to_all | solution.py:47
  98.9 1.5 %copy-start = (bf16[48,4096]{1,0:T(8,128)(2,1)S(1)}, bf16[48,4096]{1,0:T(8,128)(2,1)}, u32[]{:S(2)}) copy-start(bf16[48,4096]{1,0:T(8,128)(2,1)} %param.13) | copy-start | bytes 1179652

commit v5 on v2

--- a/solution.py
+++ b/solution.py
@@ -8,35 +8,57 @@
 NARROW = ("x", "c")
 
 
-def gather_rows(block, name):
-    n = lax.axis_size(name)
+def gather_rows(block, name, n):
     copies = jnp.broadcast_to(block[None], (n,) + block.shape)
-    got = lax.all_to_all(copies, name, 0, 0, tiled=True)
-    return got.reshape((n * block.shape[0],) + block.shape[1:])
+    return lax.all_to_all(copies, name, 0, 0, tiled=True)
 
 
 def local(
     amplitudes, integrals, virtual_irrep, column_irrep, pair_energy, virtual_energy, residual_in
 ):
-    nz = lax.axis_size("z")
-    wide_size = lax.axis_size("y") * nz
+    ny, nz = lax.axis_size("y"), lax.axis_size("z")
+    nx, nc = lax.axis_size("x"), lax.axis_size("c")
+    wide_size = ny * nz
     num_virt = virtual_irrep.shape[0]
     a_local = num_virt // wide_size
+    cd_local = integrals.shape[1]
+    core = lax.axis_index("c")
     wide_index = lax.axis_index("y") * nz + lax.axis_index("z")
     first_a = wide_index * a_local
+    swap = [(0, 1), (1, 0)]
+    partner_integrals = lax.ppermute(integrals, "c", swap)
+    partner_irrep = lax.ppermute(column_irrep, "c", swap)
     local_irrep = lax.dynamic_slice_in_dim(virtual_irrep, first_a, a_local, 0)
     row_irrep = jnp.bitwise_xor(local_irrep[:, None], virtual_irrep[None, :]).reshape(
         a_local * num_virt
     )
-    masked = jnp.where(
-        row_irrep[:, None] == column_irrep[None, :], integrals, jnp.zeros((), integrals.dtype)
+    zero = jnp.zeros((), integrals.dtype)
+    masked = jnp.where(row_irrep[:, None] == column_irrep[None, :], integrals, zero)
+    masked_partner = jnp.where(
+        row_irrep[:, None] == partner_irrep[None, :], partner_integrals, zero
     )
-    amp = gather_rows(gather_rows(amplitudes, "z"), "y")
+    amp = gather_rows(amplitudes, ("z", "c"), nz * nc)
+    amp = gather_rows(amp, "y", ny)
+    rows = amplitudes.shape[0]
+    amp = amp.reshape(ny // nc, nc, nz, nc, rows, cd_local)
+    amp = lax.dynamic_index_in_dim(amp, core, 1, keepdims=False)
+    own = lax.dynamic_index_in_dim(amp, core, 2, keepdims=False)
+    other = lax.dynamic_index_in_dim(amp, 1 - core, 2, keepdims=False)
+    pairs = own.shape[0] * own.shape[1] * own.shape[2]
+    own = own.reshape(pairs, cd_local)
+    other = other.reshape(pairs, cd_local)
     contract = (((1,), (1,)), ((), ()))
-    terms = lax.dot_general(amp, masked, contract, preferred_element_type=jnp.float32)
-    ladder = lax.psum_scatter(
-        terms.astype(jnp.bfloat16), NARROW, scatter_dimension=0, tiled=True
+    part_own = lax.dot_general(own, masked, contract, preferred_element_type=jnp.float32)
+    part_other = lax.dot_general(
+        other, masked_partner, contract, preferred_element_type=jnp.float32
+    )
+    pair_sum = part_own.astype(jnp.bfloat16).astype(jnp.float32) + part_other.astype(
+        jnp.bfloat16
     ).astype(jnp.float32)
+    block = pairs // nx
+    parts = pair_sum.astype(jnp.bfloat16).reshape(nx, block, pair_sum.shape[1])
+    parts = lax.all_to_all(parts, "x", 0, 0, tiled=True)
+    ladder = parts.astype(jnp.float32).sum(axis=0)
     pair_rows = ladder.shape[0]
     outgoing = ladder.astype(jnp.bfloat16).reshape(pair_rows, a_local, wide_size, a_local)
     outgoing = jnp.transpose(outgoing, (2, 0, 1, 3))

time: 125 us -> 105 us (0.84)
  the two profiles are of different devices: /device:TPU:23 before, /device:TPU:16 now
where the time goes in v5:
time: 105 us; the launch traced here: 104 us
  blocking collectives  41.4 us (39%)
  waiting for transfers between devices  22.9 us (22%)
  starting transfers between devices  20.2 us (19%)
  local copies, waits for them, and re-layouts  10.8 us (10%)
  matrix products  4.93 us (5%)
  other arithmetic  3.64 us (3%)
    all_to_all x1, blocking collectives, local(): parts = lax.all_to_all(parts, 'x', 0, 0, tiled=True)  23.2 us
    all_to_all x1, blocking collectives, gather_rows(): return lax.all_to_all(copies, name, 0, 0, tiled=True)  18.2 us
    all_to_all x1, waiting for transfers between devices, local(): got = lax.all_to_all(outgoing, WIDE, 0, 0, tiled=True)  14.1 us
    all_to_all x1, waiting for transfers between devices, gather_rows(): return lax.all_to_all(copies, name, 0, 0, tiled=True)  8.86 us
    all_to_all x1, starting transfers between devices, local(): got = lax.all_to_all(outgoing, WIDE, 0, 0, tiled=True)  8.82 us
    all_to_all x1, starting transfers between devices, gather_rows(): return lax.all_to_all(copies, name, 0, 0, tiled=True)  7.43 us
    unnamed x14, local copies, waits for them, and re-layouts  4.9 us
    dot_general x1, matrix products, local(): lax.dot_general(other, masked_partner, contract, preferred_element_type=j...  2.5 us
  transfers between devices with their start and end apart: 4, of which 2 were waited for; matrix products, arithmetic and copies ran while one was open for 8% of the time, Pallas kernels for 0%

profile of v5, /device:TPU:16, one launch (start us, length us, event | category | flops | bytes accessed | tf_op | source)
XLA Modules:
  0.0 104.1 jit_solution(4515894380242633054)
XLA Ops:
  0.0 0.0 copy-start.2
  0.0 2.0 %collective-permute-start.1 = (bf16[4096,256]{1,0:T(8,128)(2,1)}, bf16[4096,256]{1,0:T(8,128)(2,1)}, u32[]{:S(2)}, u32[]{:S(2)}) collective-permute-start(bf16[4096,256]{1,0:T(8,128)(2,1)} %param.8), channel_id=1, source_target_pairs={{0,1},{1,0},{2,3},{3,2},{4,5},{5,4},{6,7},{7,6},{8,9},{9,8},{10,11... | collective-permute-start | bytes 6291464 | tf_op jit(solution)/shard_map/ppermute | solution.py:29
  2.1 0.7 broadcast_in_dim.9
  2.7 18.2 %all_to_all.20 = bf16[16,6,256]{2,1,0:T(8,128)(2,1)S(1)} all-to-all(bf16[16,6,256]{2,1,0:T(8,128)(2,1)S(1)} %broadcast_in_dim.9), channel_id=1, replica_groups=mesh['y'=8,'z'=8,'x'=4,'c'=2] {'z','c'}, dimensions={0} | all-to-all | bytes 98304 | tf_op jit(solution)/shard_map/all_to_all | solution.py:13
  20.9 0.8 broadcast_in_dim.10
  21.7 7.4 %all-to-all-start.1 = ((bf16[8,16,6,256]{3,1,2,0:T(8,128)(2,1)}), bf16[8,16,6,256]{3,1,2,0:T(8,128)(2,1)S(1)}, u32[]{:S(2)}, u32[]{:S(2)}) async-start(bf16[8,16,6,256]{3,1,2,0:T(8,128)(2,1)} %broadcast_in_dim.10), calls=%async_computation.1 | async-start | bytes 786432 | tf_op jit(solution)/shard_map/all_to_all | solution.py:13
  29.2 1.9 %collective-permute-start = (s32[256]{0:T(256)}, s32[256]{0:T(256)S(1)}, u32[]{:S(2)}, u32[]{:S(2)}) collective-permute-start(s32[256]{0:T(256)} %param.10), channel_id=1, source_target_pairs={{0,1},{1,0},{2,3},{3,2},{4,5},{5,4},{6,7},{7,6},{8,9},{9,8},{10,11... | collective-permute-start | bytes 3080 | tf_op jit(solution)/shard_map/ppermute | solution.py:30
  31.1 0.8 dynamic_slice.16
  31.8 0.8 xor_bitcast_fusion
  32.6 8.9 %all-to-all-done.1 = bf16[8,16,6,256]{3,1,2,0:T(8,128)(2,1)S(1)} async-done(((bf16[8,16,6,256]{3,1,2,0:T(8,128)(2,1)}), bf16[8,16,6,256]{3,1,2,0:T(8,128)(2,1)S(1)}, u32[]{:S(2)}, u32[]{:S(2)}) %all-to-all-start.1) | async-done | bytes 393248 | tf_op jit(solution)/shard_map/all_to_all | solution.py:13
  41.5 0.2 reshape.83
  41.6 0.4 constant_dynamic-slice_fusion
  42.1 0.1 copy.18
  42.2 0.0 copy-done.2
  42.2 2.4 %fusion.3 = f32[192,4096]{1,0:T(8,128)S(1)} fusion(bf16[192,256]{1,0:T(8,128)(2,1)S(1)} %reshape.84, bf16[4096,256]{1,0:T(8,128)(2,1)} %param.8, s32[256]{0:T(256)S(1)} %copy-done.2, s32[4096]{0:T(1024)S(1)} %bitcast.36), kind=kOutput, calls=%fused_computation.5 | convolution fusion | flops 406323200 | bytes 5358592 | tf_op jit(solution)/shard_map/dot_general | solution.py:51
  44.6 0.1 copy.19
  44.7 0.0 collective-permute-done
  44.7 0.0 collective-permute-done.1
  44.8 2.5 %fusion.2 = bf16[192,4096]{1,0:T(8,128)(2,1)S(1)} fusion(f32[192,4096]{1,0:T(8,128)S(1)} %fusion.3, bf16[192,256]{1,0:T(8,128)(2,1)S(1)} %reshape.85, bf16[4096,256]{1,0:T(8,128)(2,1)} %collective-permute-done.1, s32[256]{0:T(256)S(1)} %collective-permute-done, s32[4096]{0:T(1024)S(1)} %bitcast.37), kind=kOutput, calls=%fused_computation.3 | convolution fusion | flops 407896064 | bytes 6931456 | tf_op jit(solution)/shard_map/dot_general | solution.py:52
  47.3 23.2 %all_to_all.21 = bf16[4,48,4096]{2,1,0:T(8,128)(2,1)S(1)} all-to-all(bf16[4,48,4096]{2,1,0:T(8,128)(2,1)S(1)} %bitcast.31), channel_id=1, replica_groups=mesh['y'=8,'z'=8,'x'=4,'c'=2] {'x'}, dimensions={0} | all-to-all | bytes 3145728 | tf_op jit(solution)/shard_map/all_to_all | solution.py:60
  70.5 0.2 convert_reduce_fusion
  70.8 0.5 copy.20
  71.3 0.0 copy-start.1
  71.3 0.0 copy-start.3
  71.3 0.3 copy.28
  71.6 2.5 %reshape.93 = bf16[64,2,1536]{2,1,0:T(2,128)(2,1)} reshape(bf16[64,8,8,48]{3,2,1,0:T(8,128)(2,1)S(1)} %bitcast.33) | data formatting | bytes 786432
  74.1 8.8 %all-to-all-start.3 = ((bf16[64,2,1536]{2,1,0:T(2,128)(2,1)}), bf16[64,2,1536]{2,1,0:T(2,128)(2,1)S(1)}, u32[]{:S(2)}, u32[]{:S(2)}) async-start(bf16[64,2,1536]{2,1,0:T(2,128)(2,1)} %reshape.93), calls=%async_computation.3 | async-start | bytes 786432 | tf_op jit(solution)/shard_map/all_to_all | solution.py:65
  82.9 0.0 copy-done.1
  82.9 0.1 dynamic_slice.18
  83.0 0.0 copy-done.3
  83.0 0.1 broadcast_subtract_fusion
  83.1 0.1 sub.49
  83.2 1.3 %copy.25 = f32[6,8,8,512]{3,1,2,0:T(8,128)} copy(f32[6,8,8,512]{3,2,1,0:T(8,128)S(1)} %bitcast.34) | data formatting | bytes 1572864
  84.5 14.1 %all-to-all-done.3 = bf16[64,2,1536]{2,1,0:T(2,128)(2,1)S(1)} async-done(((bf16[64,2,1536]{2,1,0:T(2,128)(2,1)}), bf16[64,2,1536]{2,1,0:T(2,128)(2,1)S(1)}, u32[]{:S(2)}, u32[]{:S(2)}) %all-to-all-start.3) | async-done | bytes 393248 | tf_op jit(solution)/shard_map/all_to_all | solution.py:65
  98.6 1.0 reshape.94
  99.7 0.2 convert_bitcast_fusion
  99.9 0.4 copy.22
  100.3 0.0 copy-start
  100.3 1.5 %copy.23 = f32[48,4096]{1,0:T(8,128)} copy(f32[48,4096]{0,1:T(8,128)S(1)} %bitcast.30) | data formatting | bytes 1572864 | tf_op jit(solution)/shard_map/reshape | solution.py:67
  101.8 0.0 copy-done
  101.8 2.3 %divide_convert_fusion = bf16[48,4096]{1,0:T(8,128)(2,1)} fusion(f32[48,4096]{1,0:T(8,128)} %bitcast.35, f32[48,4096]{1,0:T(8,128)} %copy.23, f32[48,4096]{1,0:T(8,128)S(1)} %convert_reduce_fusion, bf16[48,4096]{1,0:T(8,128)(2,1)S(1)} %copy-done, f32[4096]{0:T(1024)S(1)} %bitcast.38), kind=kLoop, calls=%fused_computation.16 | loop fusion | flops 1179648 | bytes 3162112 | tf_op jit(solution)/shard_map/convert_element_type | solution.py:74
  (7 shorter events, 0.1 us)
Async XLA Ops:
  0.0 42.2 %copy-start.2 = (s32[256]{0:T(256)S(1)}, s32[256]{0:T(256)}, u32[]{:S(2)}) copy-start(s32[256]{0:T(256)} %param.10) | copy-start | bytes 3076
  0.0 44.7 %collective-permute-start.1 = (bf16[4096,256]{1,0:T(8,128)(2,1)}, bf16[4096,256]{1,0:T(8,128)(2,1)}, u32[]{:S(2)}, u32[]{:S(2)}) collective-permute-start(bf16[4096,256]{1,0:T(8,128)(2,1)} %param.8), channel_id=1, source_target_pairs={{0,1},{1,0},{2,3},{3,2},{4,5},{5,4},{6,7},{7,6},{8,9},{9,8},{10,11... | collective-permute-start | bytes 6291464 | tf_op jit(solution)/shard_map/ppermute | solution.py:29
  21.7 19.7 %all-to-all-start.1 = ((bf16[8,16,6,256]{3,1,2,0:T(8,128)(2,1)}), bf16[8,16,6,256]{3,1,2,0:T(8,128)(2,1)S(1)}, u32[]{:S(2)}, u32[]{:S(2)}) async-start(bf16[8,16,6,256]{3,1,2,0:T(8,128)(2,1)} %broadcast_in_dim.10), calls=%async_computation.1 | async-start | bytes 786432 | tf_op jit(solution)/shard_map/all_to_all | solution.py:13
  29.2 15.6 %collective-permute-start = (s32[256]{0:T(256)}, s32[256]{0:T(256)S(1)}, u32[]{:S(2)}, u32[]{:S(2)}) collective-permute-start(s32[256]{0:T(256)} %param.10), channel_id=1, source_target_pairs={{0,1},{1,0},{2,3},{3,2},{4,5},{5,4},{6,7},{7,6},{8,9},{9,8},{10,11... | collective-permute-start | bytes 3080 | tf_op jit(solution)/shard_map/ppermute | solution.py:30
  71.3 11.6 %copy-start.1 = (f32[512]{0:T(512)S(1)}, f32[512]{0:T(512)}, u32[]{:S(2)}) copy-start(f32[512]{0:T(512)} %param.12) | copy-start | bytes 6148
  71.3 11.7 %copy-start.3 = (f32[48]{0:T(128)S(1)}, f32[48]{0:T(128)}, u32[]{:S(2)}) copy-start(f32[48]{0:T(128)} %param.11) | copy-start | bytes 580
  74.1 24.5 %all-to-all-start.3 = ((bf16[64,2,1536]{2,1,0:T(2,128)(2,1)}), bf16[64,2,1536]{2,1,0:T(2,128)(2,1)S(1)}, u32[]{:S(2)}, u32[]{:S(2)}) async-start(bf16[64,2,1536]{2,1,0:T(2,128)(2,1)} %reshape.93), calls=%async_computation.3 | async-start | bytes 786432 | tf_op jit(solution)/shard_map/all_to_all | solution.py:65
  100.3 1.5 %copy-start = (bf16[48,4096]{1,0:T(8,128)(2,1)S(1)}, bf16[48,4096]{1,0:T(8,128)(2,1)}, u32[]{:S(2)}) copy-start(bf16[48,4096]{1,0:T(8,128)(2,1)} %param.13) | copy-start | bytes 1179652

commit v6 on v4

--- a/solution.py
+++ b/solution.py
@@ -9,7 +9,7 @@
 
 
 def gather_rows(block, name):
-    n = lax.axis_size(name)
+    n = lax.axis_size(name) if isinstance(name, str) else lax.axis_size(name[0]) * lax.axis_size(name[1])
     copies = jnp.broadcast_to(block[None], (n,) + block.shape)
     got = lax.all_to_all(copies, name, 0, 0, tiled=True)
     return got.reshape((n * block.shape[0],) + block.shape[1:])
@@ -31,7 +31,7 @@
     masked = jnp.where(
         row_irrep[:, None] == column_irrep[None, :], integrals, jnp.zeros((), integrals.dtype)
     )
-    amp = gather_rows(gather_rows(amplitudes, "z"), "y")
+    amp = gather_rows(amplitudes, WIDE)
     contract = (((1,), (1,)), ((), ()))
     terms = lax.dot_general(amp, masked, contract, preferred_element_type=jnp.float32)
     nx, nc = lax.axis_size("x"), lax.axis_size("c")
@@ -43,8 +43,9 @@
     ladder = parts.astype(jnp.float32).sum(axis=0)
     pair_rows = ladder.shape[0]
     outgoing = ladder.astype(jnp.bfloat16).reshape(pair_rows, a_local, wide_size, a_local)
-    outgoing = jnp.transpose(outgoing, (2, 0, 1, 3))
+    outgoing = jnp.transpose(outgoing, (2, 0, 1, 3)).reshape(wide_size, -1, 128)
     got = lax.all_to_all(outgoing, WIDE, 0, 0, tiled=True)
+    got = got.reshape(wide_size, pair_rows, a_local, a_local)
     mirrored = jnp.transpose(got, (1, 3, 0, 2)).astype(jnp.float32)
     mirrored = mirrored.reshape(pair_rows, a_local * num_virt)
     local_energy = lax.dynamic_slice_in_dim(virtual_energy, first_a, a_local, 0)

time: 103 us -> 102 us (level)
  blocking collectives: 49.7 us -> 31.6 us
  starting transfers between devices: 14.2 us -> 22.1 us
  waiting for transfers between devices: 19.8 us -> 26.6 us
  local copies, waits for them, and re-layouts: 10.2 us -> 11.7 us
  other arithmetic: 5.94 us -> 7.04 us
    all_to_all x1 -> x0, blocking collectives: 18.1 us -> none  [gather_rows(): got = lax.all_to_all(copies, name, 0, 0, tiled=True)]
    all_to_all x1, starting transfers between devices: 7.43 us -> 16.5 us  [gather_rows(): got = lax.all_to_all(copies, name, 0, 0, tiled=True)]
    all_to_all x1, waiting for transfers between devices: 5.65 us -> 12.4 us  [gather_rows(): got = lax.all_to_all(copies, name, 0, 0, tiled=True)]
    unnamed x12 -> x10, local copies, waits for them, and re-layouts: 4.89 us -> 1.39 us
    reshape x2, local copies, waits for them, and re-layouts: 1.89 us -> 3.98 us  [local(): mirrored = mirrored.reshape(pair_rows, a_local * num_virt)]
    transpose x1, local copies, waits for them, and re-layouts: 0.29 us -> 1.64 us  [local(): outgoing = jnp.transpose(outgoing, (2, 0, 1, 3)).reshape(wide_size, -1, 128)]
    reshape x0 -> x2, local copies, waits for them, and re-layouts: none -> 1.12 us  [the longest x1 1.05 us: local(): outgoing = jnp.transpose(outgoing, (2, 0, 1, 3)).reshape(wide_size, -1, 128)]
    all_to_all x1, starting transfers between devices: 6.79 us -> 5.67 us  [local(): got = lax.all_to_all(outgoing, WIDE, 0, 0, tiled=True)]
where the time goes in v6:
time: 102 us
  blocking collectives  31.6 us (31%)
  waiting for transfers between devices  26.6 us (26%)
  starting transfers between devices  22.1 us (22%)
  local copies, waits for them, and re-layouts  11.7 us (11%)
  other arithmetic  7.04 us (7%)
  matrix products  2.65 us (3%)
    all_to_all x1, blocking collectives, local(): parts = lax.all_to_all(parts, 'x', 0, 0, tiled=True)  25.3 us
    all_to_all x1, starting transfers between devices, gather_rows(): got = lax.all_to_all(copies, name, 0, 0, tiled=True)  16.5 us
    all_to_all x1, waiting for transfers between devices, local(): got = lax.all_to_all(outgoing, WIDE, 0, 0, tiled=True)  14.2 us
    all_to_all x1, waiting for transfers between devices, gather_rows(): got = lax.all_to_all(copies, name, 0, 0, tiled=True)  12.4 us
    all_to_all x1, blocking collectives, local(): parts = lax.all_to_all(parts, 'c', 1, 1, tiled=True)  6.26 us
    all_to_all x1, starting transfers between devices, local(): got = lax.all_to_all(outgoing, WIDE, 0, 0, tiled=True)  5.67 us
    reshape x2, local copies, waits for them, and re-layouts, local(): mirrored = mirrored.reshape(pair_rows, a_local * num_virt)  3.98 us
    dot_general x1, matrix products, local(): lax.dot_general(amp, masked, contract, preferred_element_type=jnp.float32)  2.65 us
  transfers between devices with their start and end apart: 2, of which 2 were waited for; matrix products, arithmetic and copies ran while one was open for 3% of the time, Pallas kernels for 0%

profile of v6, /device:TPU:16, one launch (start us, length us, event | category | flops | bytes accessed | tf_op | source)
XLA Modules:
  0.0 101.8 jit_solution(9520127474257497423)
XLA Ops:
  0.0 1.4 %broadcast_in_dim.7 = bf16[64,6,256]{2,1,0:T(8,128)(2,1)} broadcast(bf16[6,256]{1,0:T(8,128)(2,1)} %param.7), dimensions={1,2} | broadcast | bytes 199680 | tf_op jit(solution)/shard_map/broadcast_in_dim | solution.py:13
  1.4 16.5 %all-to-all-start = ((bf16[64,6,256]{2,1,0:T(8,128)(2,1)}), bf16[64,6,256]{2,1,0:T(8,128)(2,1)S(1)}, u32[]{:S(2)}, u32[]{:S(2)}) async-start(bf16[64,6,256]{2,1,0:T(8,128)(2,1)} %broadcast_in_dim.7), calls=%async_computation | async-start | bytes 524288 | tf_op jit(solution)/shard_map/all_to_all | solution.py:14
  17.9 0.8 dynamic_slice.6
  18.7 0.8 xor_bitcast_fusion
  19.4 12.4 %all-to-all-done = bf16[64,6,256]{2,1,0:T(8,128)(2,1)S(1)} async-done(((bf16[64,6,256]{2,1,0:T(8,128)(2,1)}), bf16[64,6,256]{2,1,0:T(8,128)(2,1)S(1)}, u32[]{:S(2)}, u32[]{:S(2)}) %all-to-all-start) | async-done | bytes 196640 | tf_op jit(solution)/shard_map/all_to_all | solution.py:14
  31.8 0.1 reshape.75
  31.9 2.7 %convolution_convert_fusion = bf16[4096,384]{0,1:T(8,128)(2,1)S(1)} fusion(bf16[384,256]{1,0:T(8,128)(2,1)S(1)} %reshape.75, bf16[4096,256]{1,0:T(8,128)(2,1)} %param.8, s32[256]{0:T(256)} %param.10, s32[4096]{0:T(1024)S(1)} %bitcast.29), kind=kOutput, calls=%fused_computation | convolution fusion | flops 808976384 | bytes 5456896 | tf_op jit(solution)/shard_map/dot_general | solution.py:36
  34.5 0.3 copy.19
  34.9 6.3 %all_to_all.20 = bf16[4,2,48,4096]{3,2,0,1:T(8,128)(2,1)S(1)} all-to-all(bf16[4,2,48,4096]{3,2,0,1:T(8,128)(2,1)S(1)} %copy.19), channel_id=1, replica_groups=mesh['y'=8,'z'=8,'x'=4,'c'=2] {'c'}, dimensions={1} | all-to-all | bytes 6291456 | tf_op jit(solution)/shard_map/all_to_all | solution.py:40
  41.2 2.3 %reduce_sum.21 = bf16[4,48,4096]{2,1,0:T(8,128)(2,1)} reduce(bf16[4,2,48,4096]{3,2,0,1:T(8,128)(2,1)S(1)} %all_to_all.20, bf16[]{:T(256)} %constant.18.clone.1), dimensions={1}, to_apply=%region_0.1 | reduce | flops 786432 | bytes 4718594 | tf_op jit(solution)/shard_map/reduce_sum | solution.py:41
  43.5 25.3 %all_to_all.21 = bf16[4,48,4096]{2,1,0:T(8,128)(2,1)S(1)} all-to-all(bf16[4,48,4096]{2,1,0:T(8,128)(2,1)} %reduce_sum.21), channel_id=1, replica_groups=mesh['y'=8,'z'=8,'x'=4,'c'=2] {'x'}, dimensions={0} | all-to-all | bytes 3145728 | tf_op jit(solution)/shard_map/all_to_all | solution.py:42
  68.8 0.2 convert_reduce_fusion
  69.1 0.5 copy.20
  69.6 0.0 copy-start.1
  69.6 0.0 copy-start.2
  69.6 1.6 %copy.21 = bf16[64,48,8,8]{0,3,2,1:T(8,128)(2,1)S(1)} copy(bf16[64,48,8,8]{1,3,0,2:T(8,128)(2,1)S(1)} %bitcast.22) | data formatting | bytes 786432 | tf_op jit(solution)/shard_map/transpose | solution.py:46
  71.2 1.1 %copy.22 = bf16[64,24,128]{2,1,0:T(8,128)(2,1)} copy(bf16[64,24,128]{0,2,1:T(8,128)(2,1)S(1)} %bitcast.23) | data formatting | bytes 786432 | tf_op jit(solution)/shard_map/reshape | solution.py:46
  72.3 5.7 %all-to-all-start.3 = ((bf16[64,24,128]{2,1,0:T(8,128)(2,1)}), bf16[64,24,128]{2,1,0:T(8,128)(2,1)S(1)}, u32[]{:S(2)}, u32[]{:S(2)}) async-start(bf16[64,24,128]{2,1,0:T(8,128)(2,1)} %copy.22), calls=%async_computation.3 | async-start | bytes 786432 | tf_op jit(solution)/shard_map/all_to_all | solution.py:47
  78.0 0.0 copy-done.1
  78.0 0.1 dynamic_slice.7
  78.0 0.0 copy-done.2
  78.0 0.1 broadcast_subtract_fusion
  78.1 0.1 sub.45
  78.2 1.4 %copy.27 = f32[6,8,8,512]{3,1,2,0:T(8,128)} copy(f32[6,8,8,512]{3,2,1,0:T(8,128)S(1)} %bitcast.25) | data formatting | bytes 1572864
  79.6 14.2 %all-to-all-done.3 = bf16[64,24,128]{2,1,0:T(8,128)(2,1)S(1)} async-done(((bf16[64,24,128]{2,1,0:T(8,128)(2,1)}), bf16[64,24,128]{2,1,0:T(8,128)(2,1)S(1)}, u32[]{:S(2)}, u32[]{:S(2)}) %all-to-all-start.3) | async-done | bytes 393248 | tf_op jit(solution)/shard_map/all_to_all | solution.py:47
  93.8 0.4 copy.23
  94.2 1.3 %convert_bitcast_fusion = f32[48,8,64,8]{2,1,3,0:T(8,128)} fusion(bf16[64,48,8,8]{0,3,2,1:T(8,128)(2,1)S(1)} %bitcast.27), kind=kLoop, calls=%fused_computation.5 | loop fusion | flops 196608 | bytes 1179648 | tf_op jit(solution)/shard_map/reshape | solution.py:50
  95.6 2.5 %copy.24 = f32[48,8,64,8]{0,3,2,1:T(8,128)S(1)} copy(f32[48,8,64,8]{2,1,3,0:T(8,128)} %convert_bitcast_fusion) | data formatting | bytes 1572864 | tf_op jit(solution)/shard_map/reshape | solution.py:50
  98.1 0.0 copy-start
  98.1 1.5 %copy.25 = f32[48,4096]{1,0:T(8,128)} copy(f32[48,4096]{0,1:T(8,128)S(1)} %bitcast.21) | data formatting | bytes 1572864 | tf_op jit(solution)/shard_map/reshape | solution.py:50
  99.6 0.0 copy-done
  99.6 2.3 %divide_convert_fusion = bf16[48,4096]{1,0:T(8,128)(2,1)} fusion(f32[48,4096]{1,0:T(8,128)} %bitcast.26, f32[48,4096]{1,0:T(8,128)} %copy.25, f32[48,4096]{1,0:T(8,128)S(1)} %convert_reduce_fusion, bf16[48,4096]{1,0:T(8,128)(2,1)S(1)} %copy-done, f32[4096]{0:T(1024)S(1)} %bitcast.28), kind=kLoop, calls=%fused_computation.7 | loop fusion | flops 1179648 | bytes 3162112 | tf_op jit(solution)/shard_map/convert_element_type | solution.py:57
  (4 shorter events, 0.1 us)
Async XLA Ops:
  1.4 30.4 %all-to-all-start = ((bf16[64,6,256]{2,1,0:T(8,128)(2,1)}), bf16[64,6,256]{2,1,0:T(8,128)(2,1)S(1)}, u32[]{:S(2)}, u32[]{:S(2)}) async-start(bf16[64,6,256]{2,1,0:T(8,128)(2,1)} %broadcast_in_dim.7), calls=%async_computation | async-start | bytes 524288 | tf_op jit(solution)/shard_map/all_to_all | solution.py:14
  69.6 8.4 %copy-start.1 = (f32[512]{0:T(512)S(1)}, f32[512]{0:T(512)}, u32[]{:S(2)}) copy-start(f32[512]{0:T(512)} %param.12) | copy-start | bytes 6148
  69.6 8.5 %copy-start.2 = (f32[48]{0:T(128)S(1)}, f32[48]{0:T(128)}, u32[]{:S(2)}) copy-start(f32[48]{0:T(128)} %param.11) | copy-start | bytes 580
  72.3 21.5 %all-to-all-start.3 = ((bf16[64,24,128]{2,1,0:T(8,128)(2,1)}), bf16[64,24,128]{2,1,0:T(8,128)(2,1)S(1)}, u32[]{:S(2)}, u32[]{:S(2)}) async-start(bf16[64,24,128]{2,1,0:T(8,128)(2,1)} %copy.22), calls=%async_computation.3 | async-start | bytes 786432 | tf_op jit(solution)/shard_map/all_to_all | solution.py:47
  98.1 1.5 %copy-start = (bf16[48,4096]{1,0:T(8,128)(2,1)S(1)}, bf16[48,4096]{1,0:T(8,128)(2,1)}, u32[]{:S(2)}) copy-start(bf16[48,4096]{1,0:T(8,128)(2,1)} %param.13) | copy-start | bytes 1179652

commit v7 on v4

--- a/solution.py
+++ b/solution.py
@@ -9,7 +9,9 @@
 
 
 def gather_rows(block, name):
-    n = lax.axis_size(name)
+    n = 1
+    for axis in name:
+        n *= lax.axis_size(axis)
     copies = jnp.broadcast_to(block[None], (n,) + block.shape)
     got = lax.all_to_all(copies, name, 0, 0, tiled=True)
     return got.reshape((n * block.shape[0],) + block.shape[1:])
@@ -31,7 +33,7 @@
     masked = jnp.where(
         row_irrep[:, None] == column_irrep[None, :], integrals, jnp.zeros((), integrals.dtype)
     )
-    amp = gather_rows(gather_rows(amplitudes, "z"), "y")
+    amp = gather_rows(amplitudes, WIDE)
     contract = (((1,), (1,)), ((), ()))
     terms = lax.dot_general(amp, masked, contract, preferred_element_type=jnp.float32)
     nx, nc = lax.axis_size("x"), lax.axis_size("c")

time: 103 us -> 99.8 us (0.969)
  blocking collectives: 49.7 us -> 31.6 us
  starting transfers between devices: 14.2 us -> 22.1 us
  waiting for transfers between devices: 19.8 us -> 26.6 us
    all_to_all x1 -> x0, blocking collectives: 18.1 us -> none  [gather_rows(): got = lax.all_to_all(copies, name, 0, 0, tiled=True)]
    all_to_all x1, starting transfers between devices: 7.43 us -> 16.5 us  [gather_rows(): got = lax.all_to_all(copies, name, 0, 0, tiled=True)]
    all_to_all x1, waiting for transfers between devices: 5.65 us -> 12.4 us  [gather_rows(): got = lax.all_to_all(copies, name, 0, 0, tiled=True)]
    all_to_all x1, starting transfers between devices: 6.79 us -> 5.67 us  [local(): got = lax.all_to_all(outgoing, WIDE, 0, 0, tiled=True)]
where the time goes in v7:
time: 99.8 us; the launch traced here: 99.4 us
  blocking collectives  31.6 us (32%)
  waiting for transfers between devices  26.6 us (27%)
  starting transfers between devices  22.1 us (22%)
  local copies, waits for them, and re-layouts  10.3 us (10%)
  other arithmetic  5.94 us (6%)
  matrix products  2.65 us (3%)
    all_to_all x1, blocking collectives, local(): parts = lax.all_to_all(parts, 'x', 0, 0, tiled=True)  25.3 us
    all_to_all x1, starting transfers between devices, gather_rows(): got = lax.all_to_all(copies, name, 0, 0, tiled=True)  16.5 us
    all_to_all x1, waiting for transfers between devices, local(): got = lax.all_to_all(outgoing, WIDE, 0, 0, tiled=True)  14.2 us
    all_to_all x1, waiting for transfers between devices, gather_rows(): got = lax.all_to_all(copies, name, 0, 0, tiled=True)  12.4 us
    all_to_all x1, blocking collectives, local(): parts = lax.all_to_all(parts, 'c', 1, 1, tiled=True)  6.26 us
    all_to_all x1, starting transfers between devices, local(): got = lax.all_to_all(outgoing, WIDE, 0, 0, tiled=True)  5.67 us
    unnamed x12, local copies, waits for them, and re-layouts  4.89 us
    dot_general x1, matrix products, local(): lax.dot_general(amp, masked, contract, preferred_element_type=jnp.float32)  2.65 us
  transfers between devices with their start and end apart: 2, of which 2 were waited for; matrix products, arithmetic and copies ran while one was open for 3% of the time, Pallas kernels for 0%

profile of v7, /device:TPU:16, one launch (start us, length us, event | category | flops | bytes accessed | tf_op | source)
XLA Modules:
  0.0 99.4 jit_solution(8485839277947191651)
XLA Ops:
  0.0 1.4 %broadcast_in_dim.7 = bf16[64,6,256]{2,1,0:T(8,128)(2,1)} broadcast(bf16[6,256]{1,0:T(8,128)(2,1)} %param.7), dimensions={1,2} | broadcast | bytes 199680 | tf_op jit(solution)/shard_map/broadcast_in_dim | solution.py:15
  1.4 16.5 %all-to-all-start = ((bf16[64,6,256]{2,1,0:T(8,128)(2,1)}), bf16[64,6,256]{2,1,0:T(8,128)(2,1)S(1)}, u32[]{:S(2)}, u32[]{:S(2)}) async-start(bf16[64,6,256]{2,1,0:T(8,128)(2,1)} %broadcast_in_dim.7), calls=%async_computation | async-start | bytes 524288 | tf_op jit(solution)/shard_map/all_to_all | solution.py:16
  17.9 0.8 dynamic_slice.6
  18.7 0.8 xor_bitcast_fusion
  19.4 12.4 %all-to-all-done = bf16[64,6,256]{2,1,0:T(8,128)(2,1)S(1)} async-done(((bf16[64,6,256]{2,1,0:T(8,128)(2,1)}), bf16[64,6,256]{2,1,0:T(8,128)(2,1)S(1)}, u32[]{:S(2)}, u32[]{:S(2)}) %all-to-all-start) | async-done | bytes 196640 | tf_op jit(solution)/shard_map/all_to_all | solution.py:16
  31.8 0.1 reshape.69
  31.9 2.7 %convolution_convert_fusion = bf16[4096,384]{0,1:T(8,128)(2,1)S(1)} fusion(bf16[384,256]{1,0:T(8,128)(2,1)S(1)} %reshape.69, bf16[4096,256]{1,0:T(8,128)(2,1)} %param.8, s32[256]{0:T(256)} %param.10, s32[4096]{0:T(1024)S(1)} %bitcast.30), kind=kOutput, calls=%fused_computation | convolution fusion | flops 808976384 | bytes 5456896 | tf_op jit(solution)/shard_map/dot_general | solution.py:38
  34.5 0.3 copy.17
  34.9 6.3 %all_to_all.20 = bf16[4,2,48,4096]{3,2,0,1:T(8,128)(2,1)S(1)} all-to-all(bf16[4,2,48,4096]{3,2,0,1:T(8,128)(2,1)S(1)} %copy.17), channel_id=1, replica_groups=mesh['y'=8,'z'=8,'x'=4,'c'=2] {'c'}, dimensions={1} | all-to-all | bytes 6291456 | tf_op jit(solution)/shard_map/all_to_all | solution.py:42
  41.2 2.3 %reduce_sum.21 = bf16[4,48,4096]{2,1,0:T(8,128)(2,1)} reduce(bf16[4,2,48,4096]{3,2,0,1:T(8,128)(2,1)S(1)} %all_to_all.20, bf16[]{:T(256)} %constant.18.clone.1), dimensions={1}, to_apply=%region_0.1 | reduce | flops 786432 | bytes 4718594 | tf_op jit(solution)/shard_map/reduce_sum | solution.py:43
  43.5 25.3 %all_to_all.21 = bf16[4,48,4096]{2,1,0:T(8,128)(2,1)S(1)} all-to-all(bf16[4,48,4096]{2,1,0:T(8,128)(2,1)} %reduce_sum.21), channel_id=1, replica_groups=mesh['y'=8,'z'=8,'x'=4,'c'=2] {'x'}, dimensions={0} | all-to-all | bytes 3145728 | tf_op jit(solution)/shard_map/all_to_all | solution.py:44
  68.8 0.2 convert_reduce_fusion
  69.1 0.5 copy.18
  69.6 0.0 copy-start.1
  69.6 0.0 copy-start.2
  69.6 0.3 copy.26
  69.9 2.5 %reshape.77 = bf16[64,2,1536]{2,1,0:T(2,128)(2,1)} reshape(bf16[64,8,8,48]{3,2,1,0:T(8,128)(2,1)S(1)} %bitcast.25) | data formatting | bytes 786432
  72.4 5.7 %all-to-all-start.3 = ((bf16[64,2,1536]{2,1,0:T(2,128)(2,1)}), bf16[64,2,1536]{2,1,0:T(2,128)(2,1)S(1)}, u32[]{:S(2)}, u32[]{:S(2)}) async-start(bf16[64,2,1536]{2,1,0:T(2,128)(2,1)} %reshape.77), calls=%async_computation.3 | async-start | bytes 786432 | tf_op jit(solution)/shard_map/all_to_all | solution.py:49
  78.0 0.0 copy-done.1
  78.0 0.1 dynamic_slice.7
  78.1 0.0 copy-done.2
  78.1 0.1 broadcast_subtract_fusion
  78.2 0.1 sub.45
  78.3 1.3 %copy.23 = f32[6,8,8,512]{3,1,2,0:T(8,128)} copy(f32[6,8,8,512]{3,2,1,0:T(8,128)S(1)} %bitcast.27) | data formatting | bytes 1572864
  79.7 14.2 %all-to-all-done.3 = bf16[64,2,1536]{2,1,0:T(2,128)(2,1)S(1)} async-done(((bf16[64,2,1536]{2,1,0:T(2,128)(2,1)}), bf16[64,2,1536]{2,1,0:T(2,128)(2,1)S(1)}, u32[]{:S(2)}, u32[]{:S(2)}) %all-to-all-start.3) | async-done | bytes 393248 | tf_op jit(solution)/shard_map/all_to_all | solution.py:49
  93.9 1.0 %reshape.78 = bf16[64,8,8,48]{3,2,1,0:T(8,128)(2,1)S(1)} reshape(bf16[64,2,1536]{2,1,0:T(2,128)(2,1)S(1)} %all-to-all-done.3) | data formatting | bytes 786432
  94.9 0.2 convert_bitcast_fusion
  95.2 0.4 copy.20
  95.6 0.0 copy-start
  95.6 1.5 %copy.21 = f32[48,4096]{1,0:T(8,128)} copy(f32[48,4096]{0,1:T(8,128)S(1)} %bitcast.23) | data formatting | bytes 1572864 | tf_op jit(solution)/shard_map/reshape | solution.py:51
  97.1 0.0 copy-done
  97.1 2.3 %divide_convert_fusion = bf16[48,4096]{1,0:T(8,128)(2,1)} fusion(f32[48,4096]{1,0:T(8,128)} %bitcast.28, f32[48,4096]{1,0:T(8,128)} %copy.21, f32[48,4096]{1,0:T(8,128)S(1)} %convert_reduce_fusion, bf16[48,4096]{1,0:T(8,128)(2,1)S(1)} %copy-done, f32[4096]{0:T(1024)S(1)} %bitcast.29), kind=kLoop, calls=%fused_computation.7 | loop fusion | flops 1179648 | bytes 3162112 | tf_op jit(solution)/shard_map/convert_element_type | solution.py:58
  (4 shorter events, 0.1 us)
Async XLA Ops:
  1.4 30.4 %all-to-all-start = ((bf16[64,6,256]{2,1,0:T(8,128)(2,1)}), bf16[64,6,256]{2,1,0:T(8,128)(2,1)S(1)}, u32[]{:S(2)}, u32[]{:S(2)}) async-start(bf16[64,6,256]{2,1,0:T(8,128)(2,1)} %broadcast_in_dim.7), calls=%async_computation | async-start | bytes 524288 | tf_op jit(solution)/shard_map/all_to_all | solution.py:16
  69.6 8.5 %copy-start.1 = (f32[512]{0:T(512)S(1)}, f32[512]{0:T(512)}, u32[]{:S(2)}) copy-start(f32[512]{0:T(512)} %param.12) | copy-start | bytes 6148
  69.6 8.6 %copy-start.2 = (f32[48]{0:T(128)S(1)}, f32[48]{0:T(128)}, u32[]{:S(2)}) copy-start(f32[48]{0:T(128)} %param.11) | copy-start | bytes 580
  72.4 21.5 %all-to-all-start.3 = ((bf16[64,2,1536]{2,1,0:T(2,128)(2,1)}), bf16[64,2,1536]{2,1,0:T(2,128)(2,1)S(1)}, u32[]{:S(2)}, u32[]{:S(2)}) async-start(bf16[64,2,1536]{2,1,0:T(2,128)(2,1)} %reshape.77), calls=%async_computation.3 | async-start | bytes 786432 | tf_op jit(solution)/shard_map/all_to_all | solution.py:49
  95.6 1.5 %copy-start = (bf16[48,4096]{1,0:T(8,128)(2,1)S(1)}, bf16[48,4096]{1,0:T(8,128)(2,1)}, u32[]{:S(2)}) copy-start(bf16[48,4096]{1,0:T(8,128)(2,1)} %param.13) | copy-start | bytes 1179652

commit v8 on v5

--- a/solution.py
+++ b/solution.py
@@ -8,23 +8,27 @@
 NARROW = ("x", "c")
 
 
-def gather_rows(block, name, n):
+def gather_rows(block, name):
+    n = 1
+    for axis in name:
+        n *= lax.axis_size(axis)
     copies = jnp.broadcast_to(block[None], (n,) + block.shape)
-    return lax.all_to_all(copies, name, 0, 0, tiled=True)
+    got = lax.all_to_all(copies, name, 0, 0, tiled=True)
+    return got.reshape((n * block.shape[0],) + block.shape[1:])
 
 
 def local(
     amplitudes, integrals, virtual_irrep, column_irrep, pair_energy, virtual_energy, residual_in
 ):
-    ny, nz = lax.axis_size("y"), lax.axis_size("z")
-    nx, nc = lax.axis_size("x"), lax.axis_size("c")
-    wide_size = ny * nz
+    nz = lax.axis_size("z")
+    wide_size = lax.axis_size("y") * nz
     num_virt = virtual_irrep.shape[0]
     a_local = num_virt // wide_size
-    cd_local = integrals.shape[1]
-    core = lax.axis_index("c")
     wide_index = lax.axis_index("y") * nz + lax.axis_index("z")
     first_a = wide_index * a_local
+    core = lax.axis_index("c")
+    nx, nc = lax.axis_size("x"), lax.axis_size("c")
+    cd_local = integrals.shape[1]
     swap = [(0, 1), (1, 0)]
     partner_integrals = lax.ppermute(integrals, "c", swap)
     partner_irrep = lax.ppermute(column_irrep, "c", swap)
@@ -37,10 +41,9 @@
     masked_partner = jnp.where(
         row_irrep[:, None] == partner_irrep[None, :], partner_integrals, zero
     )
-    amp = gather_rows(amplitudes, ("z", "c"), nz * nc)
-    amp = gather_rows(amp, "y", ny)
     rows = amplitudes.shape[0]
-    amp = amp.reshape(ny // nc, nc, nz, nc, rows, cd_local)
+    amp = gather_rows(amplitudes, ("y", "z", "c"))
+    amp = amp.reshape(lax.axis_size("y") // nc, nc, nz, nc, rows, cd_local)
     amp = lax.dynamic_index_in_dim(amp, core, 1, keepdims=False)
     own = lax.dynamic_index_in_dim(amp, core, 2, keepdims=False)
     other = lax.dynamic_index_in_dim(amp, 1 - core, 2, keepdims=False)
@@ -55,8 +58,7 @@
     pair_sum = part_own.astype(jnp.bfloat16).astype(jnp.float32) + part_other.astype(
         jnp.bfloat16
     ).astype(jnp.float32)
-    block = pairs // nx
-    parts = pair_sum.astype(jnp.bfloat16).reshape(nx, block, pair_sum.shape[1])
+    parts = pair_sum.astype(jnp.bfloat16).reshape(nx, pairs // nx, pair_sum.shape[1])
     parts = lax.all_to_all(parts, "x", 0, 0, tiled=True)
     ladder = parts.astype(jnp.float32).sum(axis=0)
     pair_rows = ladder.shape[0]

time: 105 us -> 102 us (0.971)
  blocking collectives: 41.4 us -> 24.4 us
  starting transfers between devices: 20.2 us -> 28.6 us
  waiting for transfers between devices: 22.9 us -> 29.1 us
    all_to_all x1 -> x0, blocking collectives: 18.2 us -> none  [gather_rows(): return lax.all_to_all(copies, name, 0, 0, tiled=True)]
    all_to_all x1, starting transfers between devices: 7.43 us -> 17.5 us  [gather_rows(): got = lax.all_to_all(copies, name, 0, 0, tiled=True)]
    all_to_all x1, waiting for transfers between devices: 8.86 us -> 15 us  [gather_rows(): got = lax.all_to_all(copies, name, 0, 0, tiled=True)]
    all_to_all x1, starting transfers between devices: 8.82 us -> 7.03 us  [local(): got = lax.all_to_all(outgoing, WIDE, 0, 0, tiled=True)]
    all_to_all x1, blocking collectives: 23.2 us -> 24.4 us  [local(): parts = lax.all_to_all(parts, 'x', 0, 0, tiled=True)]
  transfers between devices with their start and end apart: 4 -> 4, of which waited for: 2 -> 2; matrix products, arithmetic and copies ran while one was open for 8% -> 7% of each run, Pallas kernels for 0% -> 0%
where the time goes in v8:
time: 102 us; the launch traced here: 101 us
  waiting for transfers between devices  29.1 us (29%)
  starting transfers between devices  28.6 us (28%)
  blocking collectives  24.4 us (24%)
  local copies, waits for them, and re-layouts  10.1 us (10%)
  matrix products  4.93 us (5%)
  other arithmetic  3.64 us (4%)
    all_to_all x1, blocking collectives, local(): parts = lax.all_to_all(parts, 'x', 0, 0, tiled=True)  24.4 us
    all_to_all x1, starting transfers between devices, gather_rows(): got = lax.all_to_all(copies, name, 0, 0, tiled=True)  17.5 us
    all_to_all x1, waiting for transfers between devices, gather_rows(): got = lax.all_to_all(copies, name, 0, 0, tiled=True)  15 us
    all_to_all x1, waiting for transfers between devices, local(): got = lax.all_to_all(outgoing, WIDE, 0, 0, tiled=True)  14.1 us
    all_to_all x1, starting transfers between devices, local(): got = lax.all_to_all(outgoing, WIDE, 0, 0, tiled=True)  7.03 us
    unnamed x14, local copies, waits for them, and re-layouts  4.9 us
    dot_general x1, matrix products, local(): lax.dot_general(other, masked_partner, contract, preferred_element_type=j...  2.5 us
    dot_general x1, matrix products, local(): lax.dot_general(own, masked, contract, preferred_element_type=jnp.float32)  2.44 us
  transfers between devices with their start and end apart: 4, of which 2 were waited for; matrix products, arithmetic and copies ran while one was open for 7% of the time, Pallas kernels for 0%

profile of v8, /device:TPU:16, one launch (start us, length us, event | category | flops | bytes accessed | tf_op | source)
XLA Modules:
  0.0 101.0 jit_solution(2875592095883974458)
XLA Ops:
  0.0 0.0 copy-start.2
  0.0 2.0 %collective-permute-start.1 = (bf16[4096,256]{1,0:T(8,128)(2,1)}, bf16[4096,256]{1,0:T(8,128)(2,1)}, u32[]{:S(2)}, u32[]{:S(2)}) collective-permute-start(bf16[4096,256]{1,0:T(8,128)(2,1)} %param.8), channel_id=1, source_target_pairs={{0,1},{1,0},{2,3},{3,2},{4,5},{5,4},{6,7},{7,6},{8,9},{9,8},{10,11... | collective-permute-start | bytes 6291464 | tf_op jit(solution)/shard_map/ppermute | solution.py:33
  2.1 1.5 %broadcast_in_dim.7 = bf16[128,6,256]{2,1,0:T(8,128)(2,1)} broadcast(bf16[6,256]{1,0:T(8,128)(2,1)} %param.7), dimensions={1,2} | broadcast | bytes 396288 | tf_op jit(solution)/shard_map/broadcast_in_dim | solution.py:15
  3.6 17.5 %all-to-all-start = ((bf16[128,6,256]{2,1,0:T(8,128)(2,1)}), bf16[128,6,256]{2,1,0:T(8,128)(2,1)S(1)}, u32[]{:S(2)}, u32[]{:S(2)}) async-start(bf16[128,6,256]{2,1,0:T(8,128)(2,1)} %broadcast_in_dim.7), calls=%async_computation | async-start | bytes 1048576 | tf_op jit(solution)/shard_map/all_to_all | solution.py:16
  21.0 2.1 %collective-permute-start = (s32[256]{0:T(256)}, s32[256]{0:T(256)S(1)}, u32[]{:S(2)}, u32[]{:S(2)}) collective-permute-start(s32[256]{0:T(256)} %param.10), channel_id=1, source_target_pairs={{0,1},{1,0},{2,3},{3,2},{4,5},{5,4},{6,7},{7,6},{8,9},{9,8},{10,11... | collective-permute-start | bytes 3080 | tf_op jit(solution)/shard_map/ppermute | solution.py:34
  23.1 0.8 dynamic_slice.16
  23.9 0.8 xor_bitcast_fusion
  24.6 15.0 %all-to-all-done = bf16[128,6,256]{2,1,0:T(8,128)(2,1)S(1)} async-done(((bf16[128,6,256]{2,1,0:T(8,128)(2,1)}), bf16[128,6,256]{2,1,0:T(8,128)(2,1)S(1)}, u32[]{:S(2)}, u32[]{:S(2)}) %all-to-all-start) | async-done | bytes 393248 | tf_op jit(solution)/shard_map/all_to_all | solution.py:16
  39.7 0.0 copy-done.2
  39.7 2.4 %fusion.3 = f32[192,4096]{1,0:T(8,128)S(1)} fusion(bf16[192,256]{1,0:T(8,128)(2,1)S(1)} %reshape.79, bf16[4096,256]{1,0:T(8,128)(2,1)} %param.8, s32[256]{0:T(256)S(1)} %copy-done.2, s32[4096]{0:T(1024)S(1)} %bitcast.30), kind=kOutput, calls=%fused_computation.5 | convolution fusion | flops 406323200 | bytes 5358592 | tf_op jit(solution)/shard_map/dot_general | solution.py:54
  42.2 0.0 collective-permute-done
  42.2 0.0 collective-permute-done.1
  42.2 2.5 %fusion.2 = bf16[192,4096]{1,0:T(8,128)(2,1)S(1)} fusion(f32[192,4096]{1,0:T(8,128)S(1)} %fusion.3, bf16[192,256]{1,0:T(8,128)(2,1)S(1)} %reshape.80, bf16[4096,256]{1,0:T(8,128)(2,1)} %collective-permute-done.1, s32[256]{0:T(256)S(1)} %collective-permute-done, s32[4096]{0:T(1024)S(1)} %bitcast.31), kind=kOutput, calls=%fused_computation.3 | convolution fusion | flops 407896064 | bytes 6931456 | tf_op jit(solution)/shard_map/dot_general | solution.py:55
  44.7 24.4 %all_to_all.15 = bf16[4,48,4096]{2,1,0:T(8,128)(2,1)S(1)} all-to-all(bf16[4,48,4096]{2,1,0:T(8,128)(2,1)S(1)} %bitcast.24), channel_id=1, replica_groups=mesh['y'=8,'z'=8,'x'=4,'c'=2] {'x'}, dimensions={0} | all-to-all | bytes 3145728 | tf_op jit(solution)/shard_map/all_to_all | solution.py:62
  69.2 0.2 convert_reduce_fusion
  69.4 0.5 copy.20
  69.9 0.0 copy-start.1
  69.9 0.0 copy-start.3
  70.0 0.3 copy.33
  70.2 2.5 %reshape.90 = bf16[64,2,1536]{2,1,0:T(2,128)(2,1)} reshape(bf16[64,8,8,48]{3,2,1,0:T(8,128)(2,1)S(1)} %bitcast.26) | data formatting | bytes 786432
  72.7 7.0 %all-to-all-start.2 = ((bf16[64,2,1536]{2,1,0:T(2,128)(2,1)}), bf16[64,2,1536]{2,1,0:T(2,128)(2,1)S(1)}, u32[]{:S(2)}, u32[]{:S(2)}) async-start(bf16[64,2,1536]{2,1,0:T(2,128)(2,1)} %reshape.90), calls=%async_computation.2 | async-start | bytes 786432 | tf_op jit(solution)/shard_map/all_to_all | solution.py:67
  79.8 0.0 copy-done.1
  79.8 0.1 dynamic_slice.18
  79.9 0.0 copy-done.3
  79.9 0.1 broadcast_subtract_fusion
  79.9 0.1 sub.49
  80.1 1.3 %copy.30 = f32[6,8,8,512]{3,1,2,0:T(8,128)} copy(f32[6,8,8,512]{3,2,1,0:T(8,128)S(1)} %bitcast.27) | data formatting | bytes 1572864
  81.4 14.1 %all-to-all-done.2 = bf16[64,2,1536]{2,1,0:T(2,128)(2,1)S(1)} async-done(((bf16[64,2,1536]{2,1,0:T(2,128)(2,1)}), bf16[64,2,1536]{2,1,0:T(2,128)(2,1)S(1)}, u32[]{:S(2)}, u32[]{:S(2)}) %all-to-all-start.2) | async-done | bytes 393248 | tf_op jit(solution)/shard_map/all_to_all | solution.py:67
  95.5 1.0 %reshape.91 = bf16[64,8,8,48]{3,2,1,0:T(8,128)(2,1)S(1)} reshape(bf16[64,2,1536]{2,1,0:T(2,128)(2,1)S(1)} %all-to-all-done.2) | data formatting | bytes 786432
  96.6 0.2 convert_bitcast_fusion
  96.8 0.4 copy.22
  97.3 0.0 copy-start
  97.3 1.5 %copy.23 = f32[48,4096]{1,0:T(8,128)} copy(f32[48,4096]{0,1:T(8,128)S(1)} %bitcast.23) | data formatting | bytes 1572864 | tf_op jit(solution)/shard_map/reshape | solution.py:69
  98.8 0.0 copy-done
  98.8 2.3 %divide_convert_fusion = bf16[48,4096]{1,0:T(8,128)(2,1)} fusion(f32[48,4096]{1,0:T(8,128)} %bitcast.28, f32[48,4096]{1,0:T(8,128)} %copy.23, f32[48,4096]{1,0:T(8,128)S(1)} %convert_reduce_fusion, bf16[48,4096]{1,0:T(8,128)(2,1)S(1)} %copy-done, f32[4096]{0:T(1024)S(1)} %bitcast.32), kind=kLoop, calls=%fused_computation.16 | loop fusion | flops 1179648 | bytes 3162112 | tf_op jit(solution)/shard_map/convert_element_type | solution.py:76
  (7 shorter events, 0.2 us)
Async XLA Ops:
  0.0 39.7 %copy-start.2 = (s32[256]{0:T(256)S(1)}, s32[256]{0:T(256)}, u32[]{:S(2)}) copy-start(s32[256]{0:T(256)} %param.10) | copy-start | bytes 3076
  0.0 42.2 %collective-permute-start.1 = (bf16[4096,256]{1,0:T(8,128)(2,1)}, bf16[4096,256]{1,0:T(8,128)(2,1)}, u32[]{:S(2)}, u32[]{:S(2)}) collective-permute-start(bf16[4096,256]{1,0:T(8,128)(2,1)} %param.8), channel_id=1, source_target_pairs={{0,1},{1,0},{2,3},{3,2},{4,5},{5,4},{6,7},{7,6},{8,9},{9,8},{10,11... | collective-permute-start | bytes 6291464 | tf_op jit(solution)/shard_map/ppermute | solution.py:33
  3.6 36.0 %all-to-all-start = ((bf16[128,6,256]{2,1,0:T(8,128)(2,1)}), bf16[128,6,256]{2,1,0:T(8,128)(2,1)S(1)}, u32[]{:S(2)}, u32[]{:S(2)}) async-start(bf16[128,6,256]{2,1,0:T(8,128)(2,1)} %broadcast_in_dim.7), calls=%async_computation | async-start | bytes 1048576 | tf_op jit(solution)/shard_map/all_to_all | solution.py:16
  21.0 21.1 %collective-permute-start = (s32[256]{0:T(256)}, s32[256]{0:T(256)S(1)}, u32[]{:S(2)}, u32[]{:S(2)}) collective-permute-start(s32[256]{0:T(256)} %param.10), channel_id=1, source_target_pairs={{0,1},{1,0},{2,3},{3,2},{4,5},{5,4},{6,7},{7,6},{8,9},{9,8},{10,11... | collective-permute-start | bytes 3080 | tf_op jit(solution)/shard_map/ppermute | solution.py:34
  69.9 9.8 %copy-start.1 = (f32[512]{0:T(512)S(1)}, f32[512]{0:T(512)}, u32[]{:S(2)}) copy-start(f32[512]{0:T(512)} %param.12) | copy-start | bytes 6148
  69.9 9.9 %copy-start.3 = (f32[48]{0:T(128)S(1)}, f32[48]{0:T(128)}, u32[]{:S(2)}) copy-start(f32[48]{0:T(128)} %param.11) | copy-start | bytes 580
  72.7 22.8 %all-to-all-start.2 = ((bf16[64,2,1536]{2,1,0:T(2,128)(2,1)}), bf16[64,2,1536]{2,1,0:T(2,128)(2,1)S(1)}, u32[]{:S(2)}, u32[]{:S(2)}) async-start(bf16[64,2,1536]{2,1,0:T(2,128)(2,1)} %reshape.90), calls=%async_computation.2 | async-start | bytes 786432 | tf_op jit(solution)/shard_map/all_to_all | solution.py:67
  97.3 1.5 %copy-start = (bf16[48,4096]{1,0:T(8,128)(2,1)S(1)}, bf16[48,4096]{1,0:T(8,128)(2,1)}, u32[]{:S(2)}) copy-start(bf16[48,4096]{1,0:T(8,128)(2,1)} %param.13) | copy-start | bytes 1179652

commit v9 on v8

--- a/solution.py
+++ b/solution.py
@@ -28,7 +28,6 @@
     first_a = wide_index * a_local
     core = lax.axis_index("c")
     nx, nc = lax.axis_size("x"), lax.axis_size("c")
-    cd_local = integrals.shape[1]
     swap = [(0, 1), (1, 0)]
     partner_integrals = lax.ppermute(integrals, "c", swap)
     partner_irrep = lax.ppermute(column_irrep, "c", swap)
@@ -41,15 +40,15 @@
     masked_partner = jnp.where(
         row_irrep[:, None] == partner_irrep[None, :], partner_integrals, zero
     )
-    rows = amplitudes.shape[0]
-    amp = gather_rows(amplitudes, ("y", "z", "c"))
-    amp = amp.reshape(lax.axis_size("y") // nc, nc, nz, nc, rows, cd_local)
-    amp = lax.dynamic_index_in_dim(amp, core, 1, keepdims=False)
-    own = lax.dynamic_index_in_dim(amp, core, 2, keepdims=False)
-    other = lax.dynamic_index_in_dim(amp, 1 - core, 2, keepdims=False)
-    pairs = own.shape[0] * own.shape[1] * own.shape[2]
-    own = own.reshape(pairs, cd_local)
-    other = other.reshape(pairs, cd_local)
+    amp = gather_rows(amplitudes, WIDE)
+    block = amp.shape[0] // (nx * nc)
+    amp = amp.reshape(nx, nc, block, amp.shape[1])
+    own = lax.dynamic_index_in_dim(amp, core, 1, keepdims=False)
+    given = lax.dynamic_index_in_dim(amp, 1 - core, 1, keepdims=False)
+    other = lax.ppermute(given, "c", swap)
+    pairs = nx * block
+    own = own.reshape(pairs, -1)
+    other = other.reshape(pairs, -1)
     contract = (((1,), (1,)), ((), ()))
     part_own = lax.dot_general(own, masked, contract, preferred_element_type=jnp.float32)
     part_other = lax.dot_general(
@@ -58,7 +57,7 @@
     pair_sum = part_own.astype(jnp.bfloat16).astype(jnp.float32) + part_other.astype(
         jnp.bfloat16
     ).astype(jnp.float32)
-    parts = pair_sum.astype(jnp.bfloat16).reshape(nx, pairs // nx, pair_sum.shape[1])
+    parts = pair_sum.astype(jnp.bfloat16).reshape(nx, block, pair_sum.shape[1])
     parts = lax.all_to_all(parts, "x", 0, 0, tiled=True)
     ladder = parts.astype(jnp.float32).sum(axis=0)
     pair_rows = ladder.shape[0]

time: 102 us -> 97.1 us (0.952)
  waiting for transfers between devices: 29.1 us -> 26 us
  matrix products: 4.93 us -> 3.75 us
  blocking collectives: 24.4 us -> 25.5 us
  starting transfers between devices: 28.6 us -> 27.5 us
    all_to_all x1, waiting for transfers between devices: 15 us -> 11.1 us  [gather_rows(): got = lax.all_to_all(copies, name, 0, 0, tiled=True)]
    ppermute x0 -> x1, starting transfers between devices: none -> 1.92 us  [local(): other = lax.ppermute(given, 'c', swap)]
    all_to_all x1, starting transfers between devices: 7.03 us -> 5.28 us  [local(): got = lax.all_to_all(outgoing, WIDE, 0, 0, tiled=True)]
    dot_general x1, matrix products: 2.5 us -> 1.31 us  [local(): lax.dot_general(other, masked_partner, contract, preferred_element_type=j...]
    all_to_all x1, blocking collectives: 24.4 us -> 25.5 us  [local(): parts = lax.all_to_all(parts, 'x', 0, 0, tiled=True)]
    unnamed x14 -> x12, local copies, waits for them, and re-layouts: 4.9 us -> 4.9 us
  transfers between devices with their start and end apart: 4 -> 5, of which waited for: 2 -> 2; matrix products, arithmetic and copies ran while one was open for 7% -> 7% of each run, Pallas kernels for 0% -> 0%
where the time goes in v9:
time: 97.1 us; the launch traced here: 96.6 us
  starting transfers between devices  27.5 us (28%)
  waiting for transfers between devices  26 us (27%)
  blocking collectives  25.5 us (26%)
  local copies, waits for them, and re-layouts  10 us (10%)
  matrix products  3.75 us (4%)
  other arithmetic  3.64 us (4%)
    all_to_all x1, blocking collectives, local(): parts = lax.all_to_all(parts, 'x', 0, 0, tiled=True)  25.5 us
    all_to_all x1, starting transfers between devices, gather_rows(): got = lax.all_to_all(copies, name, 0, 0, tiled=True)  16.5 us
    all_to_all x1, waiting for transfers between devices, local(): got = lax.all_to_all(outgoing, WIDE, 0, 0, tiled=True)  14.9 us
    all_to_all x1, waiting for transfers between devices, gather_rows(): got = lax.all_to_all(copies, name, 0, 0, tiled=True)  11.1 us
    all_to_all x1, starting transfers between devices, local(): got = lax.all_to_all(outgoing, WIDE, 0, 0, tiled=True)  5.28 us
    unnamed x12, local copies, waits for them, and re-layouts  4.9 us
    dot_general x1, matrix products, local(): lax.dot_general(own, masked, contract, preferred_element_type=jnp.float32)  2.44 us
    convert_element_type x1, other arithmetic, local(): return (total / denominator).astype(jnp.bfloat16)  2.29 us
  transfers between devices with their start and end apart: 5, of which 2 were waited for; matrix products, arithmetic and copies ran while one was open for 7% of the time, Pallas kernels for 0%

profile of v9, /device:TPU:16, one launch (start us, length us, event | category | flops | bytes accessed | tf_op | source)
XLA Modules:
  0.0 96.6 jit_solution(178811244084172550)
XLA Ops:
  0.0 1.9 %collective-permute-start.2 = (bf16[4096,256]{1,0:T(8,128)(2,1)}, bf16[4096,256]{1,0:T(8,128)(2,1)S(1)}, u32[]{:S(2)}, u32[]{:S(2)}) collective-permute-start(bf16[4096,256]{1,0:T(8,128)(2,1)} %param.8), channel_id=1, source_target_pairs={{0,1},{1,0},{2,3},{3,2},{4,5},{5,4},{6,7},{7,6},{8,9},{9,8},{10,11... | collective-permute-start | bytes 6291464 | tf_op jit(solution)/shard_map/ppermute | solution.py:32
  1.9 1.4 %broadcast_in_dim.7 = bf16[64,6,256]{2,1,0:T(8,128)(2,1)} broadcast(bf16[6,256]{1,0:T(8,128)(2,1)} %param.7), dimensions={1,2} | broadcast | bytes 199680 | tf_op jit(solution)/shard_map/broadcast_in_dim | solution.py:15
  3.3 16.5 %all-to-all-start = ((bf16[64,6,256]{2,1,0:T(8,128)(2,1)}), bf16[64,6,256]{2,1,0:T(8,128)(2,1)S(1)}, u32[]{:S(2)}, u32[]{:S(2)}) async-start(bf16[64,6,256]{2,1,0:T(8,128)(2,1)} %broadcast_in_dim.7), calls=%async_computation | async-start | bytes 524288 | tf_op jit(solution)/shard_map/all_to_all | solution.py:16
  19.8 1.9 %collective-permute-start.1 = (s32[256]{0:T(256)}, s32[256]{0:T(256)S(1)}, u32[]{:S(2)}, u32[]{:S(2)}) collective-permute-start(s32[256]{0:T(256)} %param.10), channel_id=1, source_target_pairs={{0,1},{1,0},{2,3},{3,2},{4,5},{5,4},{6,7},{7,6},{8,9},{9,8},{10,11... | collective-permute-start | bytes 3080 | tf_op jit(solution)/shard_map/ppermute | solution.py:33
  21.7 0.8 dynamic_slice.14
  22.5 0.8 xor_bitcast_fusion
  23.3 11.1 %all-to-all-done = bf16[64,6,256]{2,1,0:T(8,128)(2,1)S(1)} async-done(((bf16[64,6,256]{2,1,0:T(8,128)(2,1)}), bf16[64,6,256]{2,1,0:T(8,128)(2,1)S(1)}, u32[]{:S(2)}, u32[]{:S(2)}) %all-to-all-start) | async-done | bytes 196640 | tf_op jit(solution)/shard_map/all_to_all | solution.py:16
  34.4 0.1 reshape_reshape.3
  34.5 1.9 %collective-permute-start = (bf16[4,48,256]{2,1,0:T(8,128)(2,1)S(1)}, bf16[4,48,256]{2,1,0:T(8,128)(2,1)S(1)}, u32[]{:S(2)}, u32[]{:S(2)}) collective-permute-start(bf16[4,48,256]{2,1,0:T(8,128)(2,1)S(1)} %get-tuple-element.5), channel_id=1, source_target_pairs={{0,1},{1,0},{2,3},{3,2},{4,5},{5,4},{6,7},{7,6},{8,9},{9,8},{10,11... | collective-permute-start | bytes 294920 | tf_op jit(solution)/shard_map/ppermute | solution.py:48
  36.4 2.4 %fusion.3 = f32[192,4096]{1,0:T(8,128)S(1)} fusion(bf16[192,256]{1,0:T(8,128)(2,1)S(1)} %bitcast.32, bf16[4096,256]{1,0:T(8,128)(2,1)} %param.8, s32[256]{0:T(256)} %param.10, s32[4096]{0:T(1024)S(1)} %bitcast.33), kind=kOutput, calls=%fused_computation.5 | convolution fusion | flops 406323200 | bytes 5358592 | tf_op jit(solution)/shard_map/dot_general | solution.py:53
  38.9 0.0 collective-permute-done.1
  38.9 0.0 collective-permute-done
  38.9 0.0 collective-permute-done.2
  38.9 1.3 %fusion.2 = bf16[192,4096]{1,0:T(8,128)(2,1)S(1)} fusion(f32[192,4096]{1,0:T(8,128)S(1)} %fusion.3, bf16[192,256]{1,0:T(8,128)(2,1)S(1)} %bitcast.35, bf16[4096,256]{1,0:T(8,128)(2,1)S(1)} %collective-permute-done.2, s32[256]{0:T(256)S(1)} %collective-permute-done.1, s32[4096]{0:T(1024)S(1)} %bitcast.34), kind=kOutput, calls=%fused_computation.3 | convolution fusion | flops 407896064 | bytes 6931456 | tf_op jit(solution)/shard_map/dot_general | solution.py:54
  40.2 25.5 %all_to_all.15 = bf16[4,48,4096]{2,1,0:T(8,128)(2,1)S(1)} all-to-all(bf16[4,48,4096]{2,1,0:T(8,128)(2,1)S(1)} %bitcast.27), channel_id=1, replica_groups=mesh['y'=8,'z'=8,'x'=4,'c'=2] {'x'}, dimensions={0} | all-to-all | bytes 3145728 | tf_op jit(solution)/shard_map/all_to_all | solution.py:61
  65.7 0.2 convert_reduce_fusion
  66.0 0.5 copy.12
  66.5 0.0 copy-start.1
  66.5 0.0 copy-start.2
  66.5 0.3 copy.20
  66.8 2.5 %reshape.83 = bf16[64,2,1536]{2,1,0:T(2,128)(2,1)} reshape(bf16[64,8,8,48]{3,2,1,0:T(8,128)(2,1)S(1)} %bitcast.29) | data formatting | bytes 786432
  69.3 5.3 %all-to-all-start.2 = ((bf16[64,2,1536]{2,1,0:T(2,128)(2,1)}), bf16[64,2,1536]{2,1,0:T(2,128)(2,1)S(1)}, u32[]{:S(2)}, u32[]{:S(2)}) async-start(bf16[64,2,1536]{2,1,0:T(2,128)(2,1)} %reshape.83), calls=%async_computation.2 | async-start | bytes 786432 | tf_op jit(solution)/shard_map/all_to_all | solution.py:66
  74.6 0.0 copy-done.1
  74.6 0.1 dynamic_slice.16
  74.7 0.0 copy-done.2
  74.7 0.1 broadcast_subtract_fusion
  74.7 0.1 sub.49
  74.9 1.3 %copy.17 = f32[6,8,8,512]{3,1,2,0:T(8,128)} copy(f32[6,8,8,512]{3,2,1,0:T(8,128)S(1)} %bitcast.30) | data formatting | bytes 1572864
  76.2 14.9 %all-to-all-done.2 = bf16[64,2,1536]{2,1,0:T(2,128)(2,1)S(1)} async-done(((bf16[64,2,1536]{2,1,0:T(2,128)(2,1)}), bf16[64,2,1536]{2,1,0:T(2,128)(2,1)S(1)}, u32[]{:S(2)}, u32[]{:S(2)}) %all-to-all-start.2) | async-done | bytes 393248 | tf_op jit(solution)/shard_map/all_to_all | solution.py:66
  91.1 1.0 %reshape.84 = bf16[64,8,8,48]{3,2,1,0:T(8,128)(2,1)S(1)} reshape(bf16[64,2,1536]{2,1,0:T(2,128)(2,1)S(1)} %all-to-all-done.2) | data formatting | bytes 786432
  92.1 0.2 convert_bitcast_fusion
  92.4 0.4 copy.14
  92.8 0.0 copy-start
  92.8 1.5 %copy.15 = f32[48,4096]{1,0:T(8,128)} copy(f32[48,4096]{0,1:T(8,128)S(1)} %bitcast.26) | data formatting | bytes 1572864 | tf_op jit(solution)/shard_map/reshape | solution.py:68
  94.3 0.0 copy-done
  94.3 2.3 %divide_convert_fusion = bf16[48,4096]{1,0:T(8,128)(2,1)} fusion(f32[48,4096]{1,0:T(8,128)} %bitcast.31, f32[48,4096]{1,0:T(8,128)} %copy.15, f32[48,4096]{1,0:T(8,128)S(1)} %convert_reduce_fusion, bf16[48,4096]{1,0:T(8,128)(2,1)S(1)} %copy-done, f32[4096]{0:T(1024)S(1)} %bitcast.36), kind=kLoop, calls=%fused_computation.16 | loop fusion | flops 1179648 | bytes 3162112 | tf_op jit(solution)/shard_map/convert_element_type | solution.py:75
  (5 shorter events, 0.1 us)
Async XLA Ops:
  0.0 38.9 %collective-permute-start.2 = (bf16[4096,256]{1,0:T(8,128)(2,1)}, bf16[4096,256]{1,0:T(8,128)(2,1)S(1)}, u32[]{:S(2)}, u32[]{:S(2)}) collective-permute-start(bf16[4096,256]{1,0:T(8,128)(2,1)} %param.8), channel_id=1, source_target_pairs={{0,1},{1,0},{2,3},{3,2},{4,5},{5,4},{6,7},{7,6},{8,9},{9,8},{10,11... | collective-permute-start | bytes 6291464 | tf_op jit(solution)/shard_map/ppermute | solution.py:32
  3.3 31.1 %all-to-all-start = ((bf16[64,6,256]{2,1,0:T(8,128)(2,1)}), bf16[64,6,256]{2,1,0:T(8,128)(2,1)S(1)}, u32[]{:S(2)}, u32[]{:S(2)}) async-start(bf16[64,6,256]{2,1,0:T(8,128)(2,1)} %broadcast_in_dim.7), calls=%async_computation | async-start | bytes 524288 | tf_op jit(solution)/shard_map/all_to_all | solution.py:16
  19.8 19.1 %collective-permute-start.1 = (s32[256]{0:T(256)}, s32[256]{0:T(256)S(1)}, u32[]{:S(2)}, u32[]{:S(2)}) collective-permute-start(s32[256]{0:T(256)} %param.10), channel_id=1, source_target_pairs={{0,1},{1,0},{2,3},{3,2},{4,5},{5,4},{6,7},{7,6},{8,9},{9,8},{10,11... | collective-permute-start | bytes 3080 | tf_op jit(solution)/shard_map/ppermute | solution.py:33
  34.5 4.4 %collective-permute-start = (bf16[4,48,256]{2,1,0:T(8,128)(2,1)S(1)}, bf16[4,48,256]{2,1,0:T(8,128)(2,1)S(1)}, u32[]{:S(2)}, u32[]{:S(2)}) collective-permute-start(bf16[4,48,256]{2,1,0:T(8,128)(2,1)S(1)} %get-tuple-element.5), channel_id=1, source_target_pairs={{0,1},{1,0},{2,3},{3,2},{4,5},{5,4},{6,7},{7,6},{8,9},{9,8},{10,11... | collective-permute-start | bytes 294920 | tf_op jit(solution)/shard_map/ppermute | solution.py:48
  66.5 8.1 %copy-start.1 = (f32[512]{0:T(512)S(1)}, f32[512]{0:T(512)}, u32[]{:S(2)}) copy-start(f32[512]{0:T(512)} %param.12) | copy-start | bytes 6148
  66.5 8.2 %copy-start.2 = (f32[48]{0:T(128)S(1)}, f32[48]{0:T(128)}, u32[]{:S(2)}) copy-start(f32[48]{0:T(128)} %param.11) | copy-start | bytes 580
  69.3 21.8 %all-to-all-start.2 = ((bf16[64,2,1536]{2,1,0:T(2,128)(2,1)}), bf16[64,2,1536]{2,1,0:T(2,128)(2,1)S(1)}, u32[]{:S(2)}, u32[]{:S(2)}) async-start(bf16[64,2,1536]{2,1,0:T(2,128)(2,1)} %reshape.83), calls=%async_computation.2 | async-start | bytes 786432 | tf_op jit(solution)/shard_map/all_to_all | solution.py:66
  92.8 1.5 %copy-start = (bf16[48,4096]{1,0:T(8,128)(2,1)S(1)}, bf16[48,4096]{1,0:T(8,128)(2,1)}, u32[]{:S(2)}) copy-start(bf16[48,4096]{1,0:T(8,128)(2,1)} %param.13) | copy-start | bytes 1179652

commit v10 on v9

--- a/solution.py
+++ b/solution.py
@@ -30,25 +30,27 @@
     nx, nc = lax.axis_size("x"), lax.axis_size("c")
     swap = [(0, 1), (1, 0)]
     partner_integrals = lax.ppermute(integrals, "c", swap)
-    partner_irrep = lax.ppermute(column_irrep, "c", swap)
     local_irrep = lax.dynamic_slice_in_dim(virtual_irrep, first_a, a_local, 0)
     row_irrep = jnp.bitwise_xor(local_irrep[:, None], virtual_irrep[None, :]).reshape(
         a_local * num_virt
     )
     zero = jnp.zeros((), integrals.dtype)
     masked = jnp.where(row_irrep[:, None] == column_irrep[None, :], integrals, zero)
-    masked_partner = jnp.where(
-        row_irrep[:, None] == partner_irrep[None, :], partner_integrals, zero
-    )
     amp = gather_rows(amplitudes, WIDE)
     block = amp.shape[0] // (nx * nc)
     amp = amp.reshape(nx, nc, block, amp.shape[1])
     own = lax.dynamic_index_in_dim(amp, core, 1, keepdims=False)
     given = lax.dynamic_index_in_dim(amp, 1 - core, 1, keepdims=False)
-    other = lax.ppermute(given, "c", swap)
     pairs = nx * block
+    labels = column_irrep.astype(amp.dtype)[None, :]
+    sent = jnp.concatenate([given.reshape(pairs, -1), labels], axis=0)
+    sent = lax.ppermute(sent, "c", swap)
+    other = sent[:pairs]
+    partner_irrep = sent[pairs].astype(column_irrep.dtype)
     own = own.reshape(pairs, -1)
-    other = other.reshape(pairs, -1)
+    masked_partner = jnp.where(
+        row_irrep[:, None] == partner_irrep[None, :], partner_integrals, zero
+    )
     contract = (((1,), (1,)), ((), ()))
     part_own = lax.dot_general(own, masked, contract, preferred_element_type=jnp.float32)
     part_other = lax.dot_general(

time: 97.1 us -> 97.1 us (level)
  starting transfers between devices: 27.5 us -> 25.6 us
  waiting for transfers between devices: 26 us -> 27.3 us
    ppermute x2 -> x1, starting transfers between devices: 3.84 us -> 1.92 us  [local(): sent = lax.ppermute(sent, 'c', swap)]
    all_to_all x1, waiting for transfers between devices: 11.1 us -> 12.4 us  [gather_rows(): got = lax.all_to_all(copies, name, 0, 0, tiled=True)]
  transfers between devices with their start and end apart: 5 -> 4, of which waited for: 2 -> 2; matrix products, arithmetic and copies ran while one was open for 7% -> 8% of each run, Pallas kernels for 0% -> 0%
where the time goes in v10:
time: 97.1 us; the launch traced here: 96.6 us
  waiting for transfers between devices  27.3 us (28%)
  starting transfers between devices  25.6 us (26%)
  blocking collectives  25.5 us (26%)
  local copies, waits for them, and re-layouts  10 us (10%)
  other arithmetic  4.33 us (4%)
  matrix products  3.75 us (4%)
    all_to_all x1, blocking collectives, local(): parts = lax.all_to_all(parts, 'x', 0, 0, tiled=True)  25.5 us
    all_to_all x1, starting transfers between devices, gather_rows(): got = lax.all_to_all(copies, name, 0, 0, tiled=True)  16.5 us
    all_to_all x1, waiting for transfers between devices, local(): got = lax.all_to_all(outgoing, WIDE, 0, 0, tiled=True)  14.9 us
    all_to_all x1, waiting for transfers between devices, gather_rows(): got = lax.all_to_all(copies, name, 0, 0, tiled=True)  12.4 us
    all_to_all x1, starting transfers between devices, local(): got = lax.all_to_all(outgoing, WIDE, 0, 0, tiled=True)  5.28 us
    unnamed x12, local copies, waits for them, and re-layouts  4.89 us
    dot_general x1, matrix products, local(): lax.dot_general(own, masked, contract, preferred_element_type=jnp.float32)  2.44 us
    convert_element_type x1, other arithmetic, local(): return (total / denominator).astype(jnp.bfloat16)  2.29 us
  transfers between devices with their start and end apart: 4, of which 2 were waited for; matrix products, arithmetic and copies ran while one was open for 8% of the time, Pallas kernels for 0%

profile of v10, /device:TPU:16, one launch (start us, length us, event | category | flops | bytes accessed | tf_op | source)
XLA Modules:
  0.0 96.6 jit_solution(14905732717351204439)
XLA Ops:
  0.0 1.9 %collective-permute-start.1 = (bf16[4096,256]{1,0:T(8,128)(2,1)}, bf16[4096,256]{1,0:T(8,128)(2,1)S(1)}, u32[]{:S(2)}, u32[]{:S(2)}) collective-permute-start(bf16[4096,256]{1,0:T(8,128)(2,1)} %param.8), channel_id=1, source_target_pairs={{0,1},{1,0},{2,3},{3,2},{4,5},{5,4},{6,7},{7,6},{8,9},{9,8},{10,11... | collective-permute-start | bytes 6291464 | tf_op jit(solution)/shard_map/ppermute | solution.py:32
  1.9 1.4 %broadcast_in_dim.9 = bf16[64,6,256]{2,1,0:T(8,128)(2,1)} broadcast(bf16[6,256]{1,0:T(8,128)(2,1)} %param.7), dimensions={1,2} | broadcast | bytes 199680 | tf_op jit(solution)/shard_map/broadcast_in_dim | solution.py:15
  3.3 16.5 %all-to-all-start = ((bf16[64,6,256]{2,1,0:T(8,128)(2,1)}), bf16[64,6,256]{2,1,0:T(8,128)(2,1)S(1)}, u32[]{:S(2)}, u32[]{:S(2)}) async-start(bf16[64,6,256]{2,1,0:T(8,128)(2,1)} %broadcast_in_dim.9), calls=%async_computation | async-start | bytes 524288 | tf_op jit(solution)/shard_map/all_to_all | solution.py:16
  19.8 0.8 dynamic_slice.14
  20.6 0.8 xor_bitcast_fusion
  21.3 0.7 convert_element_type.43
  22.0 12.4 %all-to-all-done = bf16[64,6,256]{2,1,0:T(8,128)(2,1)S(1)} async-done(((bf16[64,6,256]{2,1,0:T(8,128)(2,1)}), bf16[64,6,256]{2,1,0:T(8,128)(2,1)S(1)}, u32[]{:S(2)}, u32[]{:S(2)}) %all-to-all-start) | async-done | bytes 196640 | tf_op jit(solution)/shard_map/all_to_all | solution.py:16
  34.4 0.1 reshape_reshape.3
  34.5 1.9 %collective-permute-start = (bf16[193,256]{1,0:T(8,128)(2,1)S(1)}, bf16[193,256]{1,0:T(8,128)(2,1)S(1)}, u32[]{:S(2)}, u32[]{:S(2)}) collective-permute-start(bf16[193,256]{1,0:T(8,128)(2,1)S(1)} %pad_maximum_fusion), channel_id=1, source_target_pairs={{0,1},{1,0},{2,3},{3,2},{4,5},{5,4},{6,7},{7,6},{8,9},{9,8},{10,11... | collective-permute-start | bytes 296456 | tf_op jit(solution)/shard_map/ppermute | solution.py:47
  36.5 2.4 %fusion.3 = f32[192,4096]{1,0:T(8,128)S(1)} fusion(bf16[192,256]{1,0:T(8,128)(2,1)S(1)} %bitcast.31, bf16[4096,256]{1,0:T(8,128)(2,1)} %param.8, s32[256]{0:T(256)} %param.10, s32[4096]{0:T(1024)S(1)} %bitcast.32), kind=kOutput, calls=%fused_computation.5 | convolution fusion | flops 406323200 | bytes 5358592 | tf_op jit(solution)/shard_map/dot_general | solution.py:55
  38.9 0.0 collective-permute-done
  38.9 0.0 collective-permute-done.1
  38.9 1.3 %fusion.2 = bf16[192,4096]{1,0:T(8,128)(2,1)S(1)} fusion(f32[192,4096]{1,0:T(8,128)S(1)} %fusion.3, bf16[4096,256]{1,0:T(8,128)(2,1)S(1)} %collective-permute-done.1, s32[256]{0:T(256)S(1)} %bitcast.35, s32[4096]{0:T(1024)S(1)} %bitcast.33, bf16[193,256]{1,0:T(8,128)(2,1)S(1)} %collective-permute-done), kind=kOutput, calls=%fused_computation.3 | convolution fusion | flops 407896064 | bytes 6931456 | tf_op jit(solution)/shard_map/dot_general | solution.py:56
  40.3 25.5 %all_to_all.15 = bf16[4,48,4096]{2,1,0:T(8,128)(2,1)S(1)} all-to-all(bf16[4,48,4096]{2,1,0:T(8,128)(2,1)S(1)} %bitcast.25), channel_id=1, replica_groups=mesh['y'=8,'z'=8,'x'=4,'c'=2] {'x'}, dimensions={0} | all-to-all | bytes 3145728 | tf_op jit(solution)/shard_map/all_to_all | solution.py:63
  65.7 0.2 convert_reduce_fusion
  66.0 0.5 copy.12
  66.5 0.0 copy-start.1
  66.5 0.0 copy-start.2
  66.5 0.3 copy.20
  66.8 2.5 %reshape.84 = bf16[64,2,1536]{2,1,0:T(2,128)(2,1)} reshape(bf16[64,8,8,48]{3,2,1,0:T(8,128)(2,1)S(1)} %bitcast.27) | data formatting | bytes 786432
  69.3 5.3 %all-to-all-start.2 = ((bf16[64,2,1536]{2,1,0:T(2,128)(2,1)}), bf16[64,2,1536]{2,1,0:T(2,128)(2,1)S(1)}, u32[]{:S(2)}, u32[]{:S(2)}) async-start(bf16[64,2,1536]{2,1,0:T(2,128)(2,1)} %reshape.84), calls=%async_computation.2 | async-start | bytes 786432 | tf_op jit(solution)/shard_map/all_to_all | solution.py:68
  74.6 0.0 copy-done.1
  74.6 0.1 dynamic_slice.16
  74.7 0.0 copy-done.2
  74.7 0.1 broadcast_subtract_fusion
  74.8 0.1 sub.49
  74.9 1.3 %copy.17 = f32[6,8,8,512]{3,1,2,0:T(8,128)} copy(f32[6,8,8,512]{3,2,1,0:T(8,128)S(1)} %bitcast.28) | data formatting | bytes 1572864
  76.2 14.9 %all-to-all-done.2 = bf16[64,2,1536]{2,1,0:T(2,128)(2,1)S(1)} async-done(((bf16[64,2,1536]{2,1,0:T(2,128)(2,1)}), bf16[64,2,1536]{2,1,0:T(2,128)(2,1)S(1)}, u32[]{:S(2)}, u32[]{:S(2)}) %all-to-all-start.2) | async-done | bytes 393248 | tf_op jit(solution)/shard_map/all_to_all | solution.py:68
  91.1 1.0 %reshape.85 = bf16[64,8,8,48]{3,2,1,0:T(8,128)(2,1)S(1)} reshape(bf16[64,2,1536]{2,1,0:T(2,128)(2,1)S(1)} %all-to-all-done.2) | data formatting | bytes 786432
  92.2 0.2 convert_bitcast_fusion
  92.4 0.4 copy.14
  92.8 0.0 copy-start
  92.8 1.5 %copy.15 = f32[48,4096]{1,0:T(8,128)} copy(f32[48,4096]{0,1:T(8,128)S(1)} %bitcast.24) | data formatting | bytes 1572864 | tf_op jit(solution)/shard_map/reshape | solution.py:70
  94.3 0.0 copy-done
  94.3 2.3 %divide_convert_fusion = bf16[48,4096]{1,0:T(8,128)(2,1)} fusion(f32[48,4096]{1,0:T(8,128)} %bitcast.29, f32[48,4096]{1,0:T(8,128)} %copy.15, f32[48,4096]{1,0:T(8,128)S(1)} %convert_reduce_fusion, bf16[48,4096]{1,0:T(8,128)(2,1)S(1)} %copy-done, f32[4096]{0:T(1024)S(1)} %bitcast.34), kind=kLoop, calls=%fused_computation.16 | loop fusion | flops 1179648 | bytes 3162112 | tf_op jit(solution)/shard_map/convert_element_type | solution.py:77
  (8 shorter events, 0.1 us)
Async XLA Ops:
  0.0 38.9 %collective-permute-start.1 = (bf16[4096,256]{1,0:T(8,128)(2,1)}, bf16[4096,256]{1,0:T(8,128)(2,1)S(1)}, u32[]{:S(2)}, u32[]{:S(2)}) collective-permute-start(bf16[4096,256]{1,0:T(8,128)(2,1)} %param.8), channel_id=1, source_target_pairs={{0,1},{1,0},{2,3},{3,2},{4,5},{5,4},{6,7},{7,6},{8,9},{9,8},{10,11... | collective-permute-start | bytes 6291464 | tf_op jit(solution)/shard_map/ppermute | solution.py:32
  3.3 31.1 %all-to-all-start = ((bf16[64,6,256]{2,1,0:T(8,128)(2,1)}), bf16[64,6,256]{2,1,0:T(8,128)(2,1)S(1)}, u32[]{:S(2)}, u32[]{:S(2)}) async-start(bf16[64,6,256]{2,1,0:T(8,128)(2,1)} %broadcast_in_dim.9), calls=%async_computation | async-start | bytes 524288 | tf_op jit(solution)/shard_map/all_to_all | solution.py:16
  34.5 4.4 %collective-permute-start = (bf16[193,256]{1,0:T(8,128)(2,1)S(1)}, bf16[193,256]{1,0:T(8,128)(2,1)S(1)}, u32[]{:S(2)}, u32[]{:S(2)}) collective-permute-start(bf16[193,256]{1,0:T(8,128)(2,1)S(1)} %pad_maximum_fusion), channel_id=1, source_target_pairs={{0,1},{1,0},{2,3},{3,2},{4,5},{5,4},{6,7},{7,6},{8,9},{9,8},{10,11... | collective-permute-start | bytes 296456 | tf_op jit(solution)/shard_map/ppermute | solution.py:47
  66.5 8.1 %copy-start.1 = (f32[512]{0:T(512)S(1)}, f32[512]{0:T(512)}, u32[]{:S(2)}) copy-start(f32[512]{0:T(512)} %param.12) | copy-start | bytes 6148
  66.5 8.2 %copy-start.2 = (f32[48]{0:T(128)S(1)}, f32[48]{0:T(128)}, u32[]{:S(2)}) copy-start(f32[48]{0:T(128)} %param.11) | copy-start | bytes 580
  69.3 21.8 %all-to-all-start.2 = ((bf16[64,2,1536]{2,1,0:T(2,128)(2,1)}), bf16[64,2,1536]{2,1,0:T(2,128)(2,1)S(1)}, u32[]{:S(2)}, u32[]{:S(2)}) async-start(bf16[64,2,1536]{2,1,0:T(2,128)(2,1)} %reshape.84), calls=%async_computation.2 | async-start | bytes 786432 | tf_op jit(solution)/shard_map/all_to_all | solution.py:68
  92.8 1.5 %copy-start = (bf16[48,4096]{1,0:T(8,128)(2,1)S(1)}, bf16[48,4096]{1,0:T(8,128)(2,1)}, u32[]{:S(2)}) copy-start(bf16[48,4096]{1,0:T(8,128)(2,1)} %param.13) | copy-start | bytes 1179652

commit v11 on v10

--- a/solution.py
+++ b/solution.py
@@ -66,6 +66,8 @@
     outgoing = ladder.astype(jnp.bfloat16).reshape(pair_rows, a_local, wide_size, a_local)
     outgoing = jnp.transpose(outgoing, (2, 0, 1, 3))
     got = lax.all_to_all(outgoing, WIDE, 0, 0, tiled=True)
+    partial = residual_in.astype(jnp.float32) + ladder
+    partial, got = lax.optimization_barrier((partial, got))
     mirrored = jnp.transpose(got, (1, 3, 0, 2)).astype(jnp.float32)
     mirrored = mirrored.reshape(pair_rows, a_local * num_virt)
     local_energy = lax.dynamic_slice_in_dim(virtual_energy, first_a, a_local, 0)
@@ -73,7 +75,7 @@
         pair_energy[:, None, None] - local_energy[None, :, None] - virtual_energy[None, None, :]
     )
     denominator = denominator.reshape(pair_rows, a_local * num_virt)
-    total = residual_in.astype(jnp.float32) + ladder - mirrored
+    total = partial - mirrored
     return (total / denominator).astype(jnp.bfloat16)
 
 

time: 97.1 us -> 98.1 us (1.010)
  transfers between devices with their start and end apart: 4 -> 4, of which waited for: 2 -> 2; matrix products, arithmetic and copies ran while one was open for 8% -> 7% of each run, Pallas kernels for 0% -> 0%
where the time goes in v11:
time: 98.1 us; the launch traced here: 97.6 us
  waiting for transfers between devices  28.1 us (29%)
  starting transfers between devices  25.6 us (26%)
  blocking collectives  25.6 us (26%)
  local copies, waits for them, and re-layouts  9.13 us (9%)
  other arithmetic  5.23 us (5%)
  matrix products  3.75 us (4%)
    all_to_all x1, blocking collectives, local(): parts = lax.all_to_all(parts, 'x', 0, 0, tiled=True)  25.6 us
    all_to_all x1, starting transfers between devices, gather_rows(): got = lax.all_to_all(copies, name, 0, 0, tiled=True)  16.5 us
    all_to_all x1, waiting for transfers between devices, local(): got = lax.all_to_all(outgoing, WIDE, 0, 0, tiled=True)  15.7 us
    all_to_all x1, waiting for transfers between devices, gather_rows(): got = lax.all_to_all(copies, name, 0, 0, tiled=True)  12.4 us
    all_to_all x1, starting transfers between devices, local(): got = lax.all_to_all(outgoing, WIDE, 0, 0, tiled=True)  5.28 us
    unnamed x12, local copies, waits for them, and re-layouts  4.01 us
    dot_general x1, matrix products, local(): lax.dot_general(own, masked, contract, preferred_element_type=jnp.float32)  2.44 us
    convert_element_type x1, other arithmetic, local(): return (total / denominator).astype(jnp.bfloat16)  2.24 us
  transfers between devices with their start and end apart: 4, of which 2 were waited for; matrix products, arithmetic and copies ran while one was open for 7% of the time, Pallas kernels for 0%

profile of v11, /device:TPU:16, one launch (start us, length us, event | category | flops | bytes accessed | tf_op | source)
XLA Modules:
  0.0 97.6 jit_solution(842807102693484883)
XLA Ops:
  0.0 1.9 %collective-permute-start.1 = (bf16[4096,256]{1,0:T(8,128)(2,1)}, bf16[4096,256]{1,0:T(8,128)(2,1)S(1)}, u32[]{:S(2)}, u32[]{:S(2)}) collective-permute-start(bf16[4096,256]{1,0:T(8,128)(2,1)} %param.8), channel_id=1, source_target_pairs={{0,1},{1,0},{2,3},{3,2},{4,5},{5,4},{6,7},{7,6},{8,9},{9,8},{10,11... | collective-permute-start | bytes 6291464 | tf_op jit(solution)/shard_map/ppermute | solution.py:32
  1.9 1.4 %broadcast_in_dim.9 = bf16[64,6,256]{2,1,0:T(8,128)(2,1)} broadcast(bf16[6,256]{1,0:T(8,128)(2,1)} %param.7), dimensions={1,2} | broadcast | bytes 199680 | tf_op jit(solution)/shard_map/broadcast_in_dim | solution.py:15
  3.3 16.5 %all-to-all-start = ((bf16[64,6,256]{2,1,0:T(8,128)(2,1)}), bf16[64,6,256]{2,1,0:T(8,128)(2,1)S(1)}, u32[]{:S(2)}, u32[]{:S(2)}) async-start(bf16[64,6,256]{2,1,0:T(8,128)(2,1)} %broadcast_in_dim.9), calls=%async_computation | async-start | bytes 524288 | tf_op jit(solution)/shard_map/all_to_all | solution.py:16
  19.8 0.8 dynamic_slice.14
  20.6 0.8 xor_bitcast_fusion
  21.3 0.7 convert_element_type.43
  22.0 12.4 %all-to-all-done = bf16[64,6,256]{2,1,0:T(8,128)(2,1)S(1)} async-done(((bf16[64,6,256]{2,1,0:T(8,128)(2,1)}), bf16[64,6,256]{2,1,0:T(8,128)(2,1)S(1)}, u32[]{:S(2)}, u32[]{:S(2)}) %all-to-all-start) | async-done | bytes 196640 | tf_op jit(solution)/shard_map/all_to_all | solution.py:16
  34.4 0.1 reshape_reshape.3
  34.5 1.9 %collective-permute-start = (bf16[193,256]{1,0:T(8,128)(2,1)S(1)}, bf16[193,256]{1,0:T(8,128)(2,1)S(1)}, u32[]{:S(2)}, u32[]{:S(2)}) collective-permute-start(bf16[193,256]{1,0:T(8,128)(2,1)S(1)} %pad_maximum_fusion), channel_id=1, source_target_pairs={{0,1},{1,0},{2,3},{3,2},{4,5},{5,4},{6,7},{7,6},{8,9},{9,8},{10,11... | collective-permute-start | bytes 296456 | tf_op jit(solution)/shard_map/ppermute | solution.py:47
  36.5 2.4 %fusion.3 = f32[192,4096]{1,0:T(8,128)S(1)} fusion(bf16[192,256]{1,0:T(8,128)(2,1)S(1)} %bitcast.31, bf16[4096,256]{1,0:T(8,128)(2,1)} %param.8, s32[256]{0:T(256)} %param.10, s32[4096]{0:T(1024)S(1)} %bitcast.32), kind=kOutput, calls=%fused_computation.5 | convolution fusion | flops 406323200 | bytes 5358592 | tf_op jit(solution)/shard_map/dot_general | solution.py:55
  38.9 0.0 collective-permute-done
  38.9 0.0 collective-permute-done.1
  38.9 1.3 %fusion.2 = bf16[192,4096]{1,0:T(8,128)(2,1)S(1)} fusion(f32[192,4096]{1,0:T(8,128)S(1)} %fusion.3, bf16[4096,256]{1,0:T(8,128)(2,1)S(1)} %collective-permute-done.1, s32[256]{0:T(256)S(1)} %bitcast.35, s32[4096]{0:T(1024)S(1)} %bitcast.33, bf16[193,256]{1,0:T(8,128)(2,1)S(1)} %collective-permute-done), kind=kOutput, calls=%fused_computation.3 | convolution fusion | flops 407896064 | bytes 6931456 | tf_op jit(solution)/shard_map/dot_general | solution.py:56
  40.3 0.0 copy-start
  40.3 25.6 %all_to_all.15 = bf16[4,48,4096]{2,1,0:T(8,128)(2,1)S(1)} all-to-all(bf16[4,48,4096]{2,1,0:T(8,128)(2,1)S(1)} %bitcast.24), channel_id=1, replica_groups=mesh['y'=8,'z'=8,'x'=4,'c'=2] {'x'}, dimensions={0} | all-to-all | bytes 3145728 | tf_op jit(solution)/shard_map/all_to_all | solution.py:63
  65.9 0.2 convert_reduce_fusion
  66.1 0.0 copy-done
  66.1 1.0 %fusion.13 = (bf16[48,4096]{1,0:T(8,128)(2,1)S(1)}, f32[48,4096]{1,0:T(8,128)}) fusion(f32[48,4096]{1,0:T(8,128)S(1)} %convert_reduce_fusion, bf16[48,4096]{1,0:T(8,128)(2,1)S(1)} %copy-done), kind=kLoop, calls=%fused_computation.28 | loop fusion | flops 589824 | bytes 2359296 | tf_op jit(solution)/shard_map/convert_element_type | solution.py:66
  67.1 0.5 copy.12
  67.6 0.0 copy-start.1
  67.6 0.0 copy-start.2
  67.6 0.3 copy.20
  67.9 2.5 %reshape.84 = bf16[64,2,1536]{2,1,0:T(2,128)(2,1)} reshape(bf16[64,8,8,48]{3,2,1,0:T(8,128)(2,1)S(1)} %bitcast.27) | data formatting | bytes 786432
  70.4 5.3 %all-to-all-start.2 = ((bf16[64,2,1536]{2,1,0:T(2,128)(2,1)}), bf16[64,2,1536]{2,1,0:T(2,128)(2,1)S(1)}, u32[]{:S(2)}, u32[]{:S(2)}) async-start(bf16[64,2,1536]{2,1,0:T(2,128)(2,1)} %reshape.84), calls=%async_computation.2 | async-start | bytes 786432 | tf_op jit(solution)/shard_map/all_to_all | solution.py:68
  75.7 0.0 copy-done.1
  75.7 0.1 dynamic_slice.16
  75.8 0.0 copy-done.2
  75.8 0.1 broadcast_subtract_fusion
  75.8 0.1 sub.49
  76.0 0.5 copy.17
  76.5 15.7 %all-to-all-done.2 = bf16[64,2,1536]{2,1,0:T(2,128)(2,1)S(1)} async-done(((bf16[64,2,1536]{2,1,0:T(2,128)(2,1)}), bf16[64,2,1536]{2,1,0:T(2,128)(2,1)S(1)}, u32[]{:S(2)}, u32[]{:S(2)}) %all-to-all-start.2) | async-done | bytes 393248 | tf_op jit(solution)/shard_map/all_to_all | solution.py:68
  92.2 1.0 %reshape.85 = bf16[64,8,8,48]{3,2,1,0:T(8,128)(2,1)S(1)} reshape(bf16[64,2,1536]{2,1,0:T(2,128)(2,1)S(1)} %all-to-all-done.2) | data formatting | bytes 786432
  93.2 0.2 convert_bitcast_fusion
  93.5 0.4 copy.14
  93.9 1.5 %copy.15 = f32[48,4096]{1,0:T(8,128)} copy(f32[48,4096]{0,1:T(8,128)S(1)} %bitcast.23) | data formatting | bytes 1572864 | tf_op jit(solution)/shard_map/reshape | solution.py:72
  95.4 2.2 %divide_convert_fusion = bf16[48,4096]{1,0:T(8,128)(2,1)} fusion(f32[48,4096]{1,0:T(8,128)S(1)} %bitcast.29, f32[48,4096]{1,0:T(8,128)} %get-tuple-element.7, f32[48,4096]{1,0:T(8,128)} %copy.15, f32[4096]{0:T(1024)S(1)} %bitcast.34), kind=kLoop, calls=%fused_computation.16 | loop fusion | flops 786432 | bytes 2768896 | tf_op jit(solution)/shard_map/convert_element_type | solution.py:79
  (7 shorter events, 0.1 us)
Async XLA Ops:
  0.0 38.9 %collective-permute-start.1 = (bf16[4096,256]{1,0:T(8,128)(2,1)}, bf16[4096,256]{1,0:T(8,128)(2,1)S(1)}, u32[]{:S(2)}, u32[]{:S(2)}) collective-permute-start(bf16[4096,256]{1,0:T(8,128)(2,1)} %param.8), channel_id=1, source_target_pairs={{0,1},{1,0},{2,3},{3,2},{4,5},{5,4},{6,7},{7,6},{8,9},{9,8},{10,11... | collective-permute-start | bytes 6291464 | tf_op jit(solution)/shard_map/ppermute | solution.py:32
  3.3 31.1 %all-to-all-start = ((bf16[64,6,256]{2,1,0:T(8,128)(2,1)}), bf16[64,6,256]{2,1,0:T(8,128)(2,1)S(1)}, u32[]{:S(2)}, u32[]{:S(2)}) async-start(bf16[64,6,256]{2,1,0:T(8,128)(2,1)} %broadcast_in_dim.9), calls=%async_computation | async-start | bytes 524288 | tf_op jit(solution)/shard_map/all_to_all | solution.py:16
  34.5 4.4 %collective-permute-start = (bf16[193,256]{1,0:T(8,128)(2,1)S(1)}, bf16[193,256]{1,0:T(8,128)(2,1)S(1)}, u32[]{:S(2)}, u32[]{:S(2)}) collective-permute-start(bf16[193,256]{1,0:T(8,128)(2,1)S(1)} %pad_maximum_fusion), channel_id=1, source_target_pairs={{0,1},{1,0},{2,3},{3,2},{4,5},{5,4},{6,7},{7,6},{8,9},{9,8},{10,11... | collective-permute-start | bytes 296456 | tf_op jit(solution)/shard_map/ppermute | solution.py:47
  40.3 25.9 %copy-start = (bf16[48,4096]{1,0:T(8,128)(2,1)S(1)}, bf16[48,4096]{1,0:T(8,128)(2,1)}, u32[]{:S(2)}) copy-start(bf16[48,4096]{1,0:T(8,128)(2,1)} %param.13) | copy-start | bytes 1179652
  67.6 8.1 %copy-start.1 = (f32[512]{0:T(512)S(1)}, f32[512]{0:T(512)}, u32[]{:S(2)}) copy-start(f32[512]{0:T(512)} %param.12) | copy-start | bytes 6148
  67.6 8.2 %copy-start.2 = (f32[48]{0:T(128)S(1)}, f32[48]{0:T(128)}, u32[]{:S(2)}) copy-start(f32[48]{0:T(128)} %param.11) | copy-start | bytes 580
  70.4 21.8 %all-to-all-start.2 = ((bf16[64,2,1536]{2,1,0:T(2,128)(2,1)}), bf16[64,2,1536]{2,1,0:T(2,128)(2,1)S(1)}, u32[]{:S(2)}, u32[]{:S(2)}) async-start(bf16[64,2,1536]{2,1,0:T(2,128)(2,1)} %reshape.84), calls=%async_computation.2 | async-start | bytes 786432 | tf_op jit(solution)/shard_map/all_to_all | solution.py:68

commit v12 on v10

--- a/solution.py
+++ b/solution.py
@@ -1,6 +1,8 @@
 import jax
 import jax.numpy as jnp
 from jax import lax
+from jax.experimental import pallas as pl
+from jax.experimental.pallas import tpu as pltpu
 from jax.sharding import Mesh
 from jax.sharding import PartitionSpec as P
 
@@ -17,6 +19,56 @@
     return got.reshape((n * block.shape[0],) + block.shape[1:])
 
 
+def pair_ladder(own, other, integrals, partner_integrals, local_irrep, virtual_irrep, labels, partner_labels):
+    pairs, cd_local = own.shape
+    a_local = local_irrep.shape[0]
+    num_virt = virtual_irrep.shape[0]
+
+    def kernel(li_ref, own_ref, other_ref, v_ref, vp_ref, vi_ref, col_ref, colp_ref, out_ref):
+        pair_irrep = jnp.bitwise_xor(vi_ref[...], li_ref[pl.program_id(0)])
+        zero = jnp.zeros((), v_ref.dtype)
+        v = jnp.where(pair_irrep == col_ref[...], v_ref[...], zero)
+        vp = jnp.where(pair_irrep == colp_ref[...], vp_ref[...], zero)
+        contract = (((1,), (1,)), ((), ()))
+        p1 = lax.dot_general(own_ref[...], v, contract, preferred_element_type=jnp.float32)
+        p2 = lax.dot_general(other_ref[...], vp, contract, preferred_element_type=jnp.float32)
+        total = p1.astype(jnp.bfloat16).astype(jnp.float32) + p2.astype(jnp.bfloat16).astype(
+            jnp.float32
+        )
+        out_ref[...] = total.astype(out_ref.dtype)
+
+    whole = lambda a, li: (0, 0)
+    rows = lambda a, li: (a, 0)
+    grid_spec = pltpu.PrefetchScalarGridSpec(
+        num_scalar_prefetch=1,
+        grid=(a_local,),
+        in_specs=[
+            pl.BlockSpec((pairs, cd_local), whole),
+            pl.BlockSpec((pairs, cd_local), whole),
+            pl.BlockSpec((num_virt, cd_local), rows),
+            pl.BlockSpec((num_virt, cd_local), rows),
+            pl.BlockSpec((num_virt, 1), whole),
+            pl.BlockSpec((1, cd_local), whole),
+            pl.BlockSpec((1, cd_local), whole),
+        ],
+        out_specs=pl.BlockSpec((pairs, num_virt), lambda a, li: (0, a)),
+    )
+    return pl.pallas_call(
+        kernel,
+        grid_spec=grid_spec,
+        out_shape=jax.ShapeDtypeStruct((pairs, a_local * num_virt), jnp.bfloat16),
+    )(
+        local_irrep,
+        own,
+        other,
+        integrals,
+        partner_integrals,
+        virtual_irrep.reshape(num_virt, 1),
+        labels.reshape(1, cd_local),
+        partner_labels.reshape(1, cd_local),
+    )
+
+
 def local(
     amplitudes, integrals, virtual_irrep, column_irrep, pair_energy, virtual_energy, residual_in
 ):
@@ -31,11 +83,6 @@
     swap = [(0, 1), (1, 0)]
     partner_integrals = lax.ppermute(integrals, "c", swap)
     local_irrep = lax.dynamic_slice_in_dim(virtual_irrep, first_a, a_local, 0)
-    row_irrep = jnp.bitwise_xor(local_irrep[:, None], virtual_irrep[None, :]).reshape(
-        a_local * num_virt
-    )
-    zero = jnp.zeros((), integrals.dtype)
-    masked = jnp.where(row_irrep[:, None] == column_irrep[None, :], integrals, zero)
     amp = gather_rows(amplitudes, WIDE)
     block = amp.shape[0] // (nx * nc)
     amp = amp.reshape(nx, nc, block, amp.shape[1])
@@ -48,18 +95,11 @@
     other = sent[:pairs]
     partner_irrep = sent[pairs].astype(column_irrep.dtype)
     own = own.reshape(pairs, -1)
-    masked_partner = jnp.where(
-        row_irrep[:, None] == partner_irrep[None, :], partner_integrals, zero
+    pair_sum = pair_ladder(
+        own, other, integrals, partner_integrals, local_irrep, virtual_irrep,
+        column_irrep, partner_irrep,
     )
-    contract = (((1,), (1,)), ((), ()))
-    part_own = lax.dot_general(own, masked, contract, preferred_element_type=jnp.float32)
-    part_other = lax.dot_general(
-        other, masked_partner, contract, preferred_element_type=jnp.float32
-    )
-    pair_sum = part_own.astype(jnp.bfloat16).astype(jnp.float32) + part_other.astype(
-        jnp.bfloat16
-    ).astype(jnp.float32)
-    parts = pair_sum.astype(jnp.bfloat16).reshape(nx, block, pair_sum.shape[1])
+    parts = pair_sum.reshape(nx, block, pair_sum.shape[1])
     parts = lax.all_to_all(parts, "x", 0, 0, tiled=True)
     ladder = parts.astype(jnp.float32).sum(axis=0)
     pair_rows = ladder.shape[0]

time: 97.1 us -> 108 us (1.11)
  Pallas kernels: 0 us -> 8.28 us
  local copies, waits for them, and re-layouts: 10 us -> 14.7 us
  matrix products: 3.75 us -> 0 us
  waiting for transfers between devices: 27.3 us -> 28.8 us
    pallas_call x0 -> x1, Pallas kernels: none -> 8.28 us  [pair_ladder(): pl.pallas_call(kernel, grid_spec=grid_spec, out_shape=jax.ShapeDtypeStruc...]
    dot_general x2 -> x0, matrix products: 3.75 us -> none  [the longest x1 2.44 us: local(): lax.dot_general(own, masked, contract, preferred_element_type=jnp.float32)]
    reshape x0 -> x1, local copies, waits for them, and re-layouts: none -> 1.53 us  [pair_ladder(): virtual_irrep.reshape(num_virt, 1)]
    all_to_all x1, waiting for transfers between devices: 12.4 us -> 13.9 us  [gather_rows(): got = lax.all_to_all(copies, name, 0, 0, tiled=True)]
    unnamed x12 -> x13, local copies, waits for them, and re-layouts: 4.89 us -> 6.24 us
where the time goes in v12:
time: 108 us; the launch traced here: 107 us
  waiting for transfers between devices  28.8 us (27%)
  blocking collectives  25.7 us (24%)
  starting transfers between devices  25.6 us (24%)
  local copies, waits for them, and re-layouts  14.7 us (14%)
  Pallas kernels  8.28 us (8%)
  other arithmetic  4.16 us (4%)
    all_to_all x1, blocking collectives, local(): parts = lax.all_to_all(parts, 'x', 0, 0, tiled=True)  25.7 us
    all_to_all x1, starting transfers between devices, gather_rows(): got = lax.all_to_all(copies, name, 0, 0, tiled=True)  16.5 us
    all_to_all x1, waiting for transfers between devices, local(): got = lax.all_to_all(outgoing, WIDE, 0, 0, tiled=True)  14.9 us
    all_to_all x1, waiting for transfers between devices, gather_rows(): got = lax.all_to_all(copies, name, 0, 0, tiled=True)  13.9 us
    pallas_call x1, Pallas kernels, pair_ladder(): pl.pallas_call(kernel, grid_spec=grid_spec, out_shape=jax.ShapeDtypeStruc...  8.28 us
    unnamed x13, local copies, waits for them, and re-layouts  6.24 us
    all_to_all x1, starting transfers between devices, local(): got = lax.all_to_all(outgoing, WIDE, 0, 0, tiled=True)  5.27 us
    convert_element_type x1, other arithmetic, local(): return (total / denominator).astype(jnp.bfloat16)  2.29 us
  transfers between devices with their start and end apart: 4, of which 2 were waited for; matrix products, arithmetic and copies ran while one was open for 8% of the time, Pallas kernels for 0%

profile of v12, /device:TPU:16, one launch (start us, length us, event | category | flops | bytes accessed | tf_op | source)
XLA Modules:
  0.0 107.4 jit_solution(1392656491078390330)
XLA Ops:
  0.0 1.9 %collective-permute-start.1 = (bf16[4096,256]{1,0:T(8,128)(2,1)}, bf16[4096,256]{1,0:T(8,128)(2,1)S(1)}, u32[]{:S(2)}, u32[]{:S(2)}) collective-permute-start(bf16[4096,256]{1,0:T(8,128)(2,1)} %v_ref.1), channel_id=1, source_target_pairs={{0,1},{1,0},{2,3},{3,2},{4,5},{5,4},{6,7},{7,6},{8,9},{9,8},{10,11... | collective-permute-start | bytes 6291464 | tf_op jit(solution)/shard_map/ppermute | solution.py:84
  1.9 1.4 %broadcast_in_dim.4 = bf16[64,6,256]{2,1,0:T(8,128)(2,1)} broadcast(bf16[6,256]{1,0:T(8,128)(2,1)} %param.7), dimensions={1,2} | broadcast | bytes 199680 | tf_op jit(solution)/shard_map/broadcast_in_dim | solution.py:17
  3.3 16.5 %all-to-all-start = ((bf16[64,6,256]{2,1,0:T(8,128)(2,1)}), bf16[64,6,256]{2,1,0:T(8,128)(2,1)S(1)}, u32[]{:S(2)}, u32[]{:S(2)}) async-start(bf16[64,6,256]{2,1,0:T(8,128)(2,1)} %broadcast_in_dim.4), calls=%async_computation | async-start | bytes 524288 | tf_op jit(solution)/shard_map/all_to_all | solution.py:18
  19.8 0.7 convert_element_type.28
  20.5 13.9 %all-to-all-done = bf16[64,6,256]{2,1,0:T(8,128)(2,1)S(1)} async-done(((bf16[64,6,256]{2,1,0:T(8,128)(2,1)}), bf16[64,6,256]{2,1,0:T(8,128)(2,1)S(1)}, u32[]{:S(2)}, u32[]{:S(2)}) %all-to-all-start) | async-done | bytes 196640 | tf_op jit(solution)/shard_map/all_to_all | solution.py:18
  34.4 0.1 reshape_reshape.3
  34.5 0.7 constant_dynamic-slice_fusion
  35.1 1.9 %collective-permute-start = (bf16[193,256]{1,0:T(8,128)(2,1)S(1)}, bf16[193,256]{1,0:T(8,128)(2,1)S(1)}, u32[]{:S(2)}, u32[]{:S(2)}) collective-permute-start(bf16[193,256]{1,0:T(8,128)(2,1)S(1)} %pad_maximum_fusion), channel_id=1, source_target_pairs={{0,1},{1,0},{2,3},{3,2},{4,5},{5,4},{6,7},{7,6},{8,9},{9,8},{10,11... | collective-permute-start | bytes 296456 | tf_op jit(solution)/shard_map/ppermute | solution.py:94
  37.1 1.3 %dynamic_slice.13.li_ref = s32[8]{0:T(128)} dynamic-slice(s32[512]{0:T(512)} %param.9, s32[]{:T(128)S(6)} %select_n.11), dynamic_slice_sizes={8} | dynamic-slice | bytes 68 | tf_op jit(solution)/shard_map/dynamic_slice | solution.py:85
  38.4 1.5 %copy.13.vi_ref = s32[512,1]{1,0:T(8,128)} copy(s32[512,1]{0,1:T(1,128)} %bitcast.30) | data formatting | bytes 4096 | tf_op jit(solution)/shard_map/reshape | solution.py:66
  40.0 0.0 collective-permute-done
  40.0 0.6 slice.8.other_ref
  40.6 0.6 slice_convert_fusion.colp_ref
  41.2 0.0 collective-permute-done.1.vp_ref
  41.2 0.0 copy-start
  41.2 1.3 %copy-done = bf16[4096,256]{1,0:T(8,128)(2,1)} copy-done((bf16[4096,256]{1,0:T(8,128)(2,1)}, bf16[4096,256]{1,0:T(8,128)(2,1)S(1)}, u32[]{:S(2)}) %copy-start) | copy-done | bytes 2097176
  42.5 8.3 %shard_map.73 = bf16[192,4096]{1,0:T(8,128)(2,1)} custom-call(s32[8]{0:T(128)} %dynamic_slice.13.li_ref, bf16[192,256]{1,0:T(8,128)(2,1)} %bitcast.28, bf16[192,256]{1,0:T(8,128)(2,1)} %slice.8.other_ref, bf16[4096,256]{1,0:T(8,128)(2,1)} %v_ref.1, bf16[4096,256]{1,0:T(8,128)(2,1)} %copy-done, s32[512,1]{1,0:T(8,128)} %copy.13.vi_ref, s32[1,256]{1,0:T(1,128)} %bitcast.31, ...), custom_call_target="tpu_custom_call" | custom-call | tf_op jit(solution)/shard_map/pallas_call | solution.py:56
  50.8 25.7 %all_to_all.15 = bf16[4,48,4096]{2,1,0:T(8,128)(2,1)S(1)} all-to-all(bf16[4,48,4096]{2,1,0:T(8,128)(2,1)} %bitcast.22), channel_id=1, replica_groups=mesh['y'=8,'z'=8,'x'=4,'c'=2] {'x'}, dimensions={0} | all-to-all | bytes 3145728 | tf_op jit(solution)/shard_map/all_to_all | solution.py:103
  76.5 0.2 convert_reduce_fusion
  76.8 0.5 copy.14
  77.3 0.0 copy-start.2
  77.3 0.0 copy-start.3
  77.3 0.3 copy.21
  77.6 2.5 %reshape.75 = bf16[64,2,1536]{2,1,0:T(2,128)(2,1)} reshape(bf16[64,8,8,48]{3,2,1,0:T(8,128)(2,1)S(1)} %bitcast.24) | data formatting | bytes 786432
  80.1 5.3 %all-to-all-start.2 = ((bf16[64,2,1536]{2,1,0:T(2,128)(2,1)}), bf16[64,2,1536]{2,1,0:T(2,128)(2,1)S(1)}, u32[]{:S(2)}, u32[]{:S(2)}) async-start(bf16[64,2,1536]{2,1,0:T(2,128)(2,1)} %reshape.75), calls=%async_computation.2 | async-start | bytes 786432 | tf_op jit(solution)/shard_map/all_to_all | solution.py:108
  85.3 0.0 copy-done.2
  85.3 0.1 dynamic_slice.16
  85.4 0.0 copy-done.3
  85.4 0.1 broadcast_subtract_fusion
  85.5 0.1 sub.49
  85.6 1.3 %copy.18 = f32[6,8,8,512]{3,1,2,0:T(8,128)} copy(f32[6,8,8,512]{3,2,1,0:T(8,128)S(1)} %bitcast.25) | data formatting | bytes 1572864
  87.0 14.9 %all-to-all-done.2 = bf16[64,2,1536]{2,1,0:T(2,128)(2,1)S(1)} async-done(((bf16[64,2,1536]{2,1,0:T(2,128)(2,1)}), bf16[64,2,1536]{2,1,0:T(2,128)(2,1)S(1)}, u32[]{:S(2)}, u32[]{:S(2)}) %all-to-all-start.2) | async-done | bytes 393248 | tf_op jit(solution)/shard_map/all_to_all | solution.py:108
  101.9 1.0 reshape.76
  102.9 0.2 convert_bitcast_fusion
  103.2 0.4 copy.16
  103.6 0.0 copy-start.1
  103.6 1.5 %copy.17 = f32[48,4096]{1,0:T(8,128)} copy(f32[48,4096]{0,1:T(8,128)S(1)} %bitcast.21) | data formatting | bytes 1572864 | tf_op jit(solution)/shard_map/reshape | solution.py:110
  105.1 0.0 copy-done.1
  105.1 2.3 %divide_convert_fusion = bf16[48,4096]{1,0:T(8,128)(2,1)} fusion(f32[48,4096]{1,0:T(8,128)} %bitcast.26, f32[48,4096]{1,0:T(8,128)} %copy.17, f32[48,4096]{1,0:T(8,128)S(1)} %convert_reduce_fusion, bf16[48,4096]{1,0:T(8,128)(2,1)S(1)} %copy-done.1, f32[4096]{0:T(1024)S(1)} %bitcast.29), kind=kLoop, calls=%fused_computation.2 | loop fusion | flops 1179648 | bytes 3162112 | tf_op jit(solution)/shard_map/convert_element_type | solution.py:117
  (5 shorter events, 0.1 us)
Async XLA Ops:
  0.0 41.2 %collective-permute-start.1 = (bf16[4096,256]{1,0:T(8,128)(2,1)}, bf16[4096,256]{1,0:T(8,128)(2,1)S(1)}, u32[]{:S(2)}, u32[]{:S(2)}) collective-permute-start(bf16[4096,256]{1,0:T(8,128)(2,1)} %v_ref.1), channel_id=1, source_target_pairs={{0,1},{1,0},{2,3},{3,2},{4,5},{5,4},{6,7},{7,6},{8,9},{9,8},{10,11... | collective-permute-start | bytes 6291464 | tf_op jit(solution)/shard_map/ppermute | solution.py:84
  3.3 31.1 %all-to-all-start = ((bf16[64,6,256]{2,1,0:T(8,128)(2,1)}), bf16[64,6,256]{2,1,0:T(8,128)(2,1)S(1)}, u32[]{:S(2)}, u32[]{:S(2)}) async-start(bf16[64,6,256]{2,1,0:T(8,128)(2,1)} %broadcast_in_dim.4), calls=%async_computation | async-start | bytes 524288 | tf_op jit(solution)/shard_map/all_to_all | solution.py:18
  35.1 4.8 %collective-permute-start = (bf16[193,256]{1,0:T(8,128)(2,1)S(1)}, bf16[193,256]{1,0:T(8,128)(2,1)S(1)}, u32[]{:S(2)}, u32[]{:S(2)}) collective-permute-start(bf16[193,256]{1,0:T(8,128)(2,1)S(1)} %pad_maximum_fusion), channel_id=1, source_target_pairs={{0,1},{1,0},{2,3},{3,2},{4,5},{5,4},{6,7},{7,6},{8,9},{9,8},{10,11... | collective-permute-start | bytes 296456 | tf_op jit(solution)/shard_map/ppermute | solution.py:94
  41.2 1.3 %copy-start = (bf16[4096,256]{1,0:T(8,128)(2,1)}, bf16[4096,256]{1,0:T(8,128)(2,1)S(1)}, u32[]{:S(2)}) copy-start(bf16[4096,256]{1,0:T(8,128)(2,1)S(1)} %collective-permute-done.1.vp_ref) | copy-start | bytes 6291460
  77.3 8.1 %copy-start.2 = (f32[512]{0:T(512)S(1)}, f32[512]{0:T(512)}, u32[]{:S(2)}) copy-start(f32[512]{0:T(512)} %param.12) | copy-start | bytes 6148
  77.3 8.2 %copy-start.3 = (f32[48]{0:T(128)S(1)}, f32[48]{0:T(128)}, u32[]{:S(2)}) copy-start(f32[48]{0:T(128)} %param.11) | copy-start | bytes 580
  80.1 21.8 %all-to-all-start.2 = ((bf16[64,2,1536]{2,1,0:T(2,128)(2,1)}), bf16[64,2,1536]{2,1,0:T(2,128)(2,1)S(1)}, u32[]{:S(2)}, u32[]{:S(2)}) async-start(bf16[64,2,1536]{2,1,0:T(2,128)(2,1)} %reshape.75), calls=%async_computation.2 | async-start | bytes 786432 | tf_op jit(solution)/shard_map/all_to_all | solution.py:108
  103.6 1.5 %copy-start.1 = (bf16[48,4096]{1,0:T(8,128)(2,1)S(1)}, bf16[48,4096]{1,0:T(8,128)(2,1)}, u32[]{:S(2)}) copy-start(bf16[48,4096]{1,0:T(8,128)(2,1)} %param.13) | copy-start | bytes 1179652

commit v13 on v10

--- a/solution.py
+++ b/solution.py
@@ -60,8 +60,12 @@
         jnp.bfloat16
     ).astype(jnp.float32)
     parts = pair_sum.astype(jnp.bfloat16).reshape(nx, block, pair_sum.shape[1])
-    parts = lax.all_to_all(parts, "x", 0, 0, tiled=True)
-    ladder = parts.astype(jnp.float32).sum(axis=0)
+    here = lax.axis_index("x")
+    ladder = lax.dynamic_index_in_dim(parts, here, 0, keepdims=False).astype(jnp.float32)
+    for step in range(1, nx):
+        outgoing_block = lax.dynamic_index_in_dim(parts, (here + step) % nx, 0, keepdims=False)
+        pairs_step = [(i, (i + step) % nx) for i in range(nx)]
+        ladder = ladder + lax.ppermute(outgoing_block, "x", pairs_step).astype(jnp.float32)
     pair_rows = ladder.shape[0]
     outgoing = ladder.astype(jnp.bfloat16).reshape(pair_rows, a_local, wide_size, a_local)
     outgoing = jnp.transpose(outgoing, (2, 0, 1, 3))

time: 97.1 us -> 106 us (1.092)
  the two profiles are of different devices: /device:TPU:16 before, /device:TPU:2 now
where the time goes in v13:
time: 106 us
  waiting for transfers between devices  45.4 us (43%)
  starting transfers between devices  35.5 us (33%)
  local copies, waits for them, and re-layouts  13.2 us (12%)
  other arithmetic  6.39 us (6%)
  matrix products  4.94 us (5%)
    all_to_all x1, starting transfers between devices, gather_rows(): got = lax.all_to_all(copies, name, 0, 0, tiled=True)  16.6 us
    all_to_all x1, waiting for transfers between devices, local(): got = lax.all_to_all(outgoing, WIDE, 0, 0, tiled=True)  16.4 us
    ppermute x3, waiting for transfers between devices, local(): lax.ppermute(outgoing_block, 'x', pairs_step).astype(jnp.float32)  16 us
    all_to_all x1, waiting for transfers between devices, gather_rows(): got = lax.all_to_all(copies, name, 0, 0, tiled=True)  13 us
    ppermute x3, starting transfers between devices, local(): lax.ppermute(outgoing_block, 'x', pairs_step).astype(jnp.float32)  10.5 us
    unnamed x16, local copies, waits for them, and re-layouts  6.11 us
    all_to_all x1, starting transfers between devices, local(): got = lax.all_to_all(outgoing, WIDE, 0, 0, tiled=True)  4.63 us
    convert_element_type x1, other arithmetic, local(): return (total / denominator).astype(jnp.bfloat16)  2.69 us
  transfers between devices with their start and end apart: 7, of which 5 were waited for; matrix products, arithmetic and copies ran while one was open for 7% of the time, Pallas kernels for 0%

profile of v13, /device:TPU:2, one launch (start us, length us, event | category | flops | bytes accessed | tf_op | source)
XLA Modules:
  0.0 105.7 jit_solution(15421422959406041987)
XLA Ops:
  0.0 1.9 %collective-permute-start.1 = (bf16[4096,256]{1,0:T(8,128)(2,1)}, bf16[4096,256]{1,0:T(8,128)(2,1)S(1)}, u32[]{:S(2)}, u32[]{:S(2)}) collective-permute-start(bf16[4096,256]{1,0:T(8,128)(2,1)} %param.8), channel_id=1, source_target_pairs={{0,1},{1,0},{2,3},{3,2},{4,5},{5,4},{6,7},{7,6},{8,9},{9,8},{10,11... | collective-permute-start | bytes 6291464 | tf_op jit(solution)/shard_map/ppermute | solution.py:32
  1.9 1.4 %broadcast_in_dim.9 = bf16[64,6,256]{2,1,0:T(8,128)(2,1)} broadcast(bf16[6,256]{1,0:T(8,128)(2,1)} %param.7), dimensions={1,2} | broadcast | bytes 199680 | tf_op jit(solution)/shard_map/broadcast_in_dim | solution.py:15
  3.3 16.6 %all-to-all-start = ((bf16[64,6,256]{2,1,0:T(8,128)(2,1)}), bf16[64,6,256]{2,1,0:T(8,128)(2,1)S(1)}, u32[]{:S(2)}, u32[]{:S(2)}) async-start(bf16[64,6,256]{2,1,0:T(8,128)(2,1)} %broadcast_in_dim.9), calls=%async_computation | async-start | bytes 524288 | tf_op jit(solution)/shard_map/all_to_all | solution.py:16
  20.0 0.8 dynamic_slice.27
  20.7 0.8 xor_bitcast_fusion
  21.5 0.7 convert_element_type.51
  22.2 13.0 %all-to-all-done = bf16[64,6,256]{2,1,0:T(8,128)(2,1)S(1)} async-done(((bf16[64,6,256]{2,1,0:T(8,128)(2,1)}), bf16[64,6,256]{2,1,0:T(8,128)(2,1)S(1)}, u32[]{:S(2)}, u32[]{:S(2)}) %all-to-all-start) | async-done | bytes 196640 | tf_op jit(solution)/shard_map/all_to_all | solution.py:16
  35.2 0.1 reshape_reshape.3
  35.3 1.9 %collective-permute-start = (bf16[193,256]{1,0:T(8,128)(2,1)S(1)}, bf16[193,256]{1,0:T(8,128)(2,1)S(1)}, u32[]{:S(2)}, u32[]{:S(2)}) collective-permute-start(bf16[193,256]{1,0:T(8,128)(2,1)S(1)} %pad_maximum_fusion), channel_id=1, source_target_pairs={{0,1},{1,0},{2,3},{3,2},{4,5},{5,4},{6,7},{7,6},{8,9},{9,8},{10,11... | collective-permute-start | bytes 296456 | tf_op jit(solution)/shard_map/ppermute | solution.py:47
  37.2 2.4 %fusion.3 = f32[192,4096]{1,0:T(8,128)S(1)} fusion(bf16[192,256]{1,0:T(8,128)(2,1)S(1)} %bitcast.46, bf16[4096,256]{1,0:T(8,128)(2,1)} %param.8, s32[256]{0:T(256)} %param.10, s32[4096]{0:T(1024)S(1)} %bitcast.47), kind=kOutput, calls=%fused_computation.5 | convolution fusion | flops 406323200 | bytes 5358592 | tf_op jit(solution)/shard_map/dot_general | solution.py:55
  39.7 0.0 collective-permute-done
  39.7 0.0 collective-permute-done.1
  39.7 0.0 copy-start.1
  39.7 1.3 %copy-done.1 = bf16[4096,256]{1,0:T(8,128)(2,1)} copy-done((bf16[4096,256]{1,0:T(8,128)(2,1)}, bf16[4096,256]{1,0:T(8,128)(2,1)S(1)}, u32[]{:S(2)}) %copy-start.1) | copy-done | bytes 2097176
  41.1 2.5 %fusion.2 = bf16[192,4096]{1,0:T(8,128)(2,1)S(1)} fusion(f32[192,4096]{1,0:T(8,128)S(1)} %fusion.3, bf16[4096,256]{1,0:T(8,128)(2,1)} %copy-done.1, s32[256]{0:T(256)S(1)} %bitcast.50, s32[4096]{0:T(1024)S(1)} %bitcast.48, bf16[193,256]{1,0:T(8,128)(2,1)S(1)} %collective-permute-done), kind=kOutput, calls=%fused_computation.3 | convolution fusion | flops 407896064 | bytes 6931456 | tf_op jit(solution)/shard_map/dot_general | solution.py:56
  43.6 0.0 copy-start
  43.6 1.0 dynamic-slice_bitcast_fusion.2
  44.5 3.4 %collective-permute-start.2 = (bf16[48,4096]{1,0:T(8,128)(2,1)}, bf16[48,4096]{1,0:T(8,128)(2,1)S(1)}, u32[]{:S(2)}, u32[]{:S(2)}) collective-permute-start(bf16[48,4096]{1,0:T(8,128)(2,1)} %get-tuple-element.5), channel_id=1, source_target_pairs={{0,2},{2,4},{4,6},{6,0},{1,3},{3,5},{5,7},{7,1},{8,10},{10,12},{12... | collective-permute-start | bytes 1179656 | tf_op jit(solution)/shard_map/ppermute | solution.py:68
  47.9 3.0 %collective-permute-start.3 = (bf16[48,4096]{1,0:T(8,128)(2,1)S(1)}, bf16[48,4096]{1,0:T(8,128)(2,1)}, u32[]{:S(2)}, u32[]{:S(2)}) collective-permute-start(bf16[48,4096]{1,0:T(8,128)(2,1)S(1)} %get-tuple-element.7), channel_id=1, source_target_pairs={{0,4},{2,6},{4,0},{6,2},{1,5},{3,7},{5,1},{7,3},{8,12},{10,14},{12... | collective-permute-start | bytes 1179656 | tf_op jit(solution)/shard_map/ppermute | solution.py:68
  51.0 4.1 %collective-permute-start.4 = (bf16[48,4096]{1,0:T(8,128)(2,1)S(1)}, bf16[48,4096]{1,0:T(8,128)(2,1)S(1)}, u32[]{:S(2)}, u32[]{:S(2)}) collective-permute-start(bf16[48,4096]{1,0:T(8,128)(2,1)S(1)} %get-tuple-element.6), channel_id=1, source_target_pairs={{0,6},{2,0},{4,2},{6,4},{1,7},{3,1},{5,3},{7,5},{8,14},{10,8},{12,... | collective-permute-start | bytes 1179656 | tf_op jit(solution)/shard_map/ppermute | solution.py:68
  55.0 3.5 %collective-permute-done.2 = bf16[48,4096]{1,0:T(8,128)(2,1)S(1)} collective-permute-done((bf16[48,4096]{1,0:T(8,128)(2,1)}, bf16[48,4096]{1,0:T(8,128)(2,1)S(1)}, u32[]{:S(2)}, u32[]{:S(2)}) %collective-permute-start.2) | collective-permute-done | bytes 393248 | tf_op jit(solution)/shard_map/ppermute | solution.py:68
  58.5 4.9 %collective-permute-done.3 = bf16[48,4096]{1,0:T(8,128)(2,1)} collective-permute-done((bf16[48,4096]{1,0:T(8,128)(2,1)S(1)}, bf16[48,4096]{1,0:T(8,128)(2,1)}, u32[]{:S(2)}, u32[]{:S(2)}) %collective-permute-start.3) | collective-permute-done | bytes 393248 | tf_op jit(solution)/shard_map/ppermute | solution.py:68
  63.4 7.6 %collective-permute-done.4 = bf16[48,4096]{1,0:T(8,128)(2,1)S(1)} collective-permute-done((bf16[48,4096]{1,0:T(8,128)(2,1)S(1)}, bf16[48,4096]{1,0:T(8,128)(2,1)S(1)}, u32[]{:S(2)}, u32[]{:S(2)}) %collective-permute-start.4) | collective-permute-done | bytes 393248 | tf_op jit(solution)/shard_map/ppermute | solution.py:68
  71.0 0.0 copy-start.2
  71.0 0.8 copy-done.2
  71.8 1.9 %fusion.12 = bf16[48,4096]{1,0:T(8,128)(2,1)} fusion(bf16[48,4096]{1,0:T(8,128)(2,1)S(1)} %collective-permute-done.4, bf16[48,4096]{1,0:T(8,128)(2,1)} %collective-permute-done.3, bf16[48,4096]{1,0:T(8,128)(2,1)S(1)} %collective-permute-done.2, bf16[4,48,4096]{2,1,0:T(8,128)(2,1)S(1)} %bitcast.39, s32[]{:T(128)S(6)} %select_n.51), kind=kLoop, calls=%fused_computation.22 | loop fusion | flops 1572864 | bytes 1966084 | tf_op jit(solution)/shard_map/convert_element_type | solution.py:70
  73.7 0.0 copy-done
  73.7 1.5 %copy.24 = bf16[48,4096]{0,1:T(8,128)(2,1)S(1)} copy(bf16[48,4096]{1,0:T(8,128)(2,1)} %fusion.12) | data formatting | bytes 786432 | tf_op jit(solution)/shard_map/convert_element_type | solution.py:70
  75.2 0.0 copy-start.3
  75.2 0.0 copy-start.4
  75.2 0.3 copy.32
  75.5 2.5 %reshape.88 = bf16[64,2,1536]{2,1,0:T(2,128)(2,1)} reshape(bf16[64,8,8,48]{3,2,1,0:T(8,128)(2,1)S(1)} %bitcast.42) | data formatting | bytes 786432
  78.0 4.6 %all-to-all-start.1 = ((bf16[64,2,1536]{2,1,0:T(2,128)(2,1)}), bf16[64,2,1536]{2,1,0:T(2,128)(2,1)S(1)}, u32[]{:S(2)}, u32[]{:S(2)}) async-start(bf16[64,2,1536]{2,1,0:T(2,128)(2,1)} %reshape.88), calls=%async_computation.1 | async-start | bytes 786432 | tf_op jit(solution)/shard_map/all_to_all | solution.py:72
  82.6 0.0 copy-done.3
  82.6 0.1 dynamic_slice.33
  82.7 0.0 copy-done.4
  82.7 0.1 broadcast_subtract_fusion
  82.8 0.1 sub.49
  82.9 0.5 copy.29
  83.4 16.4 %all-to-all-done.1 = bf16[64,2,1536]{2,1,0:T(2,128)(2,1)S(1)} async-done(((bf16[64,2,1536]{2,1,0:T(2,128)(2,1)}), bf16[64,2,1536]{2,1,0:T(2,128)(2,1)S(1)}, u32[]{:S(2)}, u32[]{:S(2)}) %all-to-all-start.1) | async-done | bytes 393248 | tf_op jit(solution)/shard_map/all_to_all | solution.py:72
  99.8 1.0 reshape.89
  100.9 0.2 convert_bitcast_fusion
  101.1 0.4 copy.26
  101.5 1.5 %copy.27 = f32[48,4096]{1,0:T(8,128)} copy(f32[48,4096]{0,1:T(8,128)S(1)} %bitcast.37) | data formatting | bytes 1572864 | tf_op jit(solution)/shard_map/reshape | solution.py:74
  103.0 2.7 %divide_convert_fusion = bf16[48,4096]{1,0:T(8,128)(2,1)} fusion(f32[48,4096]{1,0:T(8,128)S(1)} %bitcast.44, f32[48,4096]{1,0:T(8,128)} %copy.27, bf16[48,4096]{1,0:T(8,128)(2,1)} %param.13, f32[4096]{0:T(1024)S(1)} %bitcast.49, bf16[48,4096]{1,0:T(8,128)(2,1)} %copy-done.2, bf16[48,4096]{1,0:T(8,128)(2,1)} %collective-permute-done.3, ...), kind=kLoop, calls=%fused_computation.18 | loop fusion | flops 2555904 | bytes 3948548 | tf_op jit(solution)/shard_map/convert_element_type | solution.py:81
  (7 shorter events, 0.1 us)
Async XLA Ops:
  0.0 39.7 %collective-permute-start.1 = (bf16[4096,256]{1,0:T(8,128)(2,1)}, bf16[4096,256]{1,0:T(8,128)(2,1)S(1)}, u32[]{:S(2)}, u32[]{:S(2)}) collective-permute-start(bf16[4096,256]{1,0:T(8,128)(2,1)} %param.8), channel_id=1, source_target_pairs={{0,1},{1,0},{2,3},{3,2},{4,5},{5,4},{6,7},{7,6},{8,9},{9,8},{10,11... | collective-permute-start | bytes 6291464 | tf_op jit(solution)/shard_map/ppermute | solution.py:32
  3.3 31.9 %all-to-all-start = ((bf16[64,6,256]{2,1,0:T(8,128)(2,1)}), bf16[64,6,256]{2,1,0:T(8,128)(2,1)S(1)}, u32[]{:S(2)}, u32[]{:S(2)}) async-start(bf16[64,6,256]{2,1,0:T(8,128)(2,1)} %broadcast_in_dim.9), calls=%async_computation | async-start | bytes 524288 | tf_op jit(solution)/shard_map/all_to_all | solution.py:16
  35.3 4.4 %collective-permute-start = (bf16[193,256]{1,0:T(8,128)(2,1)S(1)}, bf16[193,256]{1,0:T(8,128)(2,1)S(1)}, u32[]{:S(2)}, u32[]{:S(2)}) collective-permute-start(bf16[193,256]{1,0:T(8,128)(2,1)S(1)} %pad_maximum_fusion), channel_id=1, source_target_pairs={{0,1},{1,0},{2,3},{3,2},{4,5},{5,4},{6,7},{7,6},{8,9},{9,8},{10,11... | collective-permute-start | bytes 296456 | tf_op jit(solution)/shard_map/ppermute | solution.py:47
  39.7 1.3 %copy-start.1 = (bf16[4096,256]{1,0:T(8,128)(2,1)}, bf16[4096,256]{1,0:T(8,128)(2,1)S(1)}, u32[]{:S(2)}) copy-start(bf16[4096,256]{1,0:T(8,128)(2,1)S(1)} %collective-permute-done.1) | copy-start | bytes 6291460
  43.6 30.2 %copy-start = (bf16[192,4096]{1,0:T(8,128)(2,1)}, bf16[192,4096]{1,0:T(8,128)(2,1)S(1)}, u32[]{:S(2)}) copy-start(bf16[192,4096]{1,0:T(8,128)(2,1)S(1)} %fusion.2) | copy-start | bytes 4718596
  44.5 14.0 %collective-permute-start.2 = (bf16[48,4096]{1,0:T(8,128)(2,1)}, bf16[48,4096]{1,0:T(8,128)(2,1)S(1)}, u32[]{:S(2)}, u32[]{:S(2)}) collective-permute-start(bf16[48,4096]{1,0:T(8,128)(2,1)} %get-tuple-element.5), channel_id=1, source_target_pairs={{0,2},{2,4},{4,6},{6,0},{1,3},{3,5},{5,7},{7,1},{8,10},{10,12},{12... | collective-permute-start | bytes 1179656 | tf_op jit(solution)/shard_map/ppermute | solution.py:68
  47.9 15.5 %collective-permute-start.3 = (bf16[48,4096]{1,0:T(8,128)(2,1)S(1)}, bf16[48,4096]{1,0:T(8,128)(2,1)}, u32[]{:S(2)}, u32[]{:S(2)}) collective-permute-start(bf16[48,4096]{1,0:T(8,128)(2,1)S(1)} %get-tuple-element.7), channel_id=1, source_target_pairs={{0,4},{2,6},{4,0},{6,2},{1,5},{3,7},{5,1},{7,3},{8,12},{10,14},{12... | collective-permute-start | bytes 1179656 | tf_op jit(solution)/shard_map/ppermute | solution.py:68
  51.0 20.0 %collective-permute-start.4 = (bf16[48,4096]{1,0:T(8,128)(2,1)S(1)}, bf16[48,4096]{1,0:T(8,128)(2,1)S(1)}, u32[]{:S(2)}, u32[]{:S(2)}) collective-permute-start(bf16[48,4096]{1,0:T(8,128)(2,1)S(1)} %get-tuple-element.6), channel_id=1, source_target_pairs={{0,6},{2,0},{4,2},{6,4},{1,7},{3,1},{5,3},{7,5},{8,14},{10,8},{12,... | collective-permute-start | bytes 1179656 | tf_op jit(solution)/shard_map/ppermute | solution.py:68
  71.0 0.8 copy-start.2
  75.2 7.4 %copy-start.3 = (f32[512]{0:T(512)S(1)}, f32[512]{0:T(512)}, u32[]{:S(2)}) copy-start(f32[512]{0:T(512)} %param.12) | copy-start | bytes 6148
  75.2 7.5 %copy-start.4 = (f32[48]{0:T(128)S(1)}, f32[48]{0:T(128)}, u32[]{:S(2)}) copy-start(f32[48]{0:T(128)} %param.11) | copy-start | bytes 580
  78.0 21.8 %all-to-all-start.1 = ((bf16[64,2,1536]{2,1,0:T(2,128)(2,1)}), bf16[64,2,1536]{2,1,0:T(2,128)(2,1)S(1)}, u32[]{:S(2)}, u32[]{:S(2)}) async-start(bf16[64,2,1536]{2,1,0:T(2,128)(2,1)} %reshape.88), calls=%async_computation.1 | async-start | bytes 786432 | tf_op jit(solution)/shard_map/all_to_all | solution.py:72

commit v14 on v10

--- a/solution.py
+++ b/solution.py
@@ -66,8 +66,8 @@
     outgoing = ladder.astype(jnp.bfloat16).reshape(pair_rows, a_local, wide_size, a_local)
     outgoing = jnp.transpose(outgoing, (2, 0, 1, 3))
     got = lax.all_to_all(outgoing, WIDE, 0, 0, tiled=True)
-    mirrored = jnp.transpose(got, (1, 3, 0, 2)).astype(jnp.float32)
-    mirrored = mirrored.reshape(pair_rows, a_local * num_virt)
+    mirrored = jnp.transpose(got, (1, 3, 0, 2)).reshape(pair_rows, a_local * num_virt)
+    mirrored = lax.optimization_barrier(mirrored).astype(jnp.float32)
     local_energy = lax.dynamic_slice_in_dim(virtual_energy, first_a, a_local, 0)
     denominator = (
         pair_energy[:, None, None] - local_energy[None, :, None] - virtual_energy[None, None, :]

time: 97.1 us -> 94.7 us (0.975)
  local copies, waits for them, and re-layouts: 10 us -> 8.28 us
  other arithmetic: 4.33 us -> 2.74 us
    reshape x2 -> x0, local copies, waits for them, and re-layouts: 1.89 us -> none  [local(): mirrored = mirrored.reshape(pair_rows, a_local * num_virt)]
    convert_element_type x1, other arithmetic: 2.29 us -> 0.94 us  [local(): return (total / denominator).astype(jnp.bfloat16)]
  transfers between devices with their start and end apart: 4 -> 4, of which waited for: 2 -> 2; matrix products, arithmetic and copies ran while one was open for 8% -> 7% of each run, Pallas kernels for 0% -> 0%
where the time goes in v14:
time: 94.7 us; the launch traced here: 94.2 us
  waiting for transfers between devices  28.1 us (30%)
  starting transfers between devices  25.6 us (27%)
  blocking collectives  25.5 us (27%)
  local copies, waits for them, and re-layouts  8.28 us (9%)
  matrix products  3.75 us (4%)
  other arithmetic  2.74 us (3%)
    all_to_all x1, blocking collectives, local(): parts = lax.all_to_all(parts, 'x', 0, 0, tiled=True)  25.5 us
    all_to_all x1, starting transfers between devices, gather_rows(): got = lax.all_to_all(copies, name, 0, 0, tiled=True)  16.5 us
    all_to_all x1, waiting for transfers between devices, local(): got = lax.all_to_all(outgoing, WIDE, 0, 0, tiled=True)  15.7 us
    all_to_all x1, waiting for transfers between devices, gather_rows(): got = lax.all_to_all(copies, name, 0, 0, tiled=True)  12.4 us
    all_to_all x1, starting transfers between devices, local(): got = lax.all_to_all(outgoing, WIDE, 0, 0, tiled=True)  5.28 us
    unnamed x12, local copies, waits for them, and re-layouts  4.52 us
    dot_general x1, matrix products, local(): lax.dot_general(own, masked, contract, preferred_element_type=jnp.float32)  2.44 us
    ppermute x1, starting transfers between devices, local(): sent = lax.ppermute(sent, 'c', swap)  1.92 us
  transfers between devices with their start and end apart: 4, of which 2 were waited for; matrix products, arithmetic and copies ran while one was open for 7% of the time, Pallas kernels for 0%

profile of v14, /device:TPU:16, one launch (start us, length us, event | category | flops | bytes accessed | tf_op | source)
XLA Modules:
  0.0 94.2 jit_solution(5123246378857810193)
XLA Ops:
  0.0 1.9 %collective-permute-start.1 = (bf16[4096,256]{1,0:T(8,128)(2,1)}, bf16[4096,256]{1,0:T(8,128)(2,1)S(1)}, u32[]{:S(2)}, u32[]{:S(2)}) collective-permute-start(bf16[4096,256]{1,0:T(8,128)(2,1)} %param.8), channel_id=1, source_target_pairs={{0,1},{1,0},{2,3},{3,2},{4,5},{5,4},{6,7},{7,6},{8,9},{9,8},{10,11... | collective-permute-start | bytes 6291464 | tf_op jit(solution)/shard_map/ppermute | solution.py:32
  1.9 1.4 %broadcast_in_dim.9 = bf16[64,6,256]{2,1,0:T(8,128)(2,1)} broadcast(bf16[6,256]{1,0:T(8,128)(2,1)} %param.7), dimensions={1,2} | broadcast | bytes 199680 | tf_op jit(solution)/shard_map/broadcast_in_dim | solution.py:15
  3.3 16.5 %all-to-all-start = ((bf16[64,6,256]{2,1,0:T(8,128)(2,1)}), bf16[64,6,256]{2,1,0:T(8,128)(2,1)S(1)}, u32[]{:S(2)}, u32[]{:S(2)}) async-start(bf16[64,6,256]{2,1,0:T(8,128)(2,1)} %broadcast_in_dim.9), calls=%async_computation | async-start | bytes 524288 | tf_op jit(solution)/shard_map/all_to_all | solution.py:16
  19.8 0.8 dynamic_slice.14
  20.6 0.8 xor_bitcast_fusion
  21.3 0.7 convert_element_type.42
  22.0 12.4 %all-to-all-done = bf16[64,6,256]{2,1,0:T(8,128)(2,1)S(1)} async-done(((bf16[64,6,256]{2,1,0:T(8,128)(2,1)}), bf16[64,6,256]{2,1,0:T(8,128)(2,1)S(1)}, u32[]{:S(2)}, u32[]{:S(2)}) %all-to-all-start) | async-done | bytes 196640 | tf_op jit(solution)/shard_map/all_to_all | solution.py:16
  34.4 0.1 reshape_reshape.3
  34.5 1.9 %collective-permute-start = (bf16[193,256]{1,0:T(8,128)(2,1)S(1)}, bf16[193,256]{1,0:T(8,128)(2,1)S(1)}, u32[]{:S(2)}, u32[]{:S(2)}) collective-permute-start(bf16[193,256]{1,0:T(8,128)(2,1)S(1)} %pad_maximum_fusion), channel_id=1, source_target_pairs={{0,1},{1,0},{2,3},{3,2},{4,5},{5,4},{6,7},{7,6},{8,9},{9,8},{10,11... | collective-permute-start | bytes 296456 | tf_op jit(solution)/shard_map/ppermute | solution.py:47
  36.5 2.4 %fusion.3 = f32[192,4096]{1,0:T(8,128)S(1)} fusion(bf16[192,256]{1,0:T(8,128)(2,1)S(1)} %bitcast.31, bf16[4096,256]{1,0:T(8,128)(2,1)} %param.8, s32[256]{0:T(256)} %param.10, s32[4096]{0:T(1024)S(1)} %bitcast.32), kind=kOutput, calls=%fused_computation.5 | convolution fusion | flops 406323200 | bytes 5358592 | tf_op jit(solution)/shard_map/dot_general | solution.py:55
  38.9 0.0 collective-permute-done
  38.9 0.0 collective-permute-done.1
  38.9 1.3 %fusion.2 = bf16[192,4096]{1,0:T(8,128)(2,1)S(1)} fusion(f32[192,4096]{1,0:T(8,128)S(1)} %fusion.3, bf16[4096,256]{1,0:T(8,128)(2,1)S(1)} %collective-permute-done.1, s32[256]{0:T(256)S(1)} %bitcast.35, s32[4096]{0:T(1024)S(1)} %bitcast.33, bf16[193,256]{1,0:T(8,128)(2,1)S(1)} %collective-permute-done), kind=kOutput, calls=%fused_computation.3 | convolution fusion | flops 407896064 | bytes 6931456 | tf_op jit(solution)/shard_map/dot_general | solution.py:56
  40.3 25.5 %all_to_all.15 = bf16[4,48,4096]{2,1,0:T(8,128)(2,1)S(1)} all-to-all(bf16[4,48,4096]{2,1,0:T(8,128)(2,1)S(1)} %bitcast.24), channel_id=1, replica_groups=mesh['y'=8,'z'=8,'x'=4,'c'=2] {'x'}, dimensions={0} | all-to-all | bytes 3145728 | tf_op jit(solution)/shard_map/all_to_all | solution.py:63
  65.7 0.2 convert_reduce_fusion
  66.0 0.5 copy.12
  66.5 0.0 copy-start.1
  66.5 0.0 copy-start.2
  66.5 0.3 copy.20
  66.8 2.5 %reshape.76 = bf16[64,2,1536]{2,1,0:T(2,128)(2,1)} reshape(bf16[64,8,8,48]{3,2,1,0:T(8,128)(2,1)S(1)} %bitcast.26) | data formatting | bytes 786432
  69.3 5.3 %all-to-all-start.2 = ((bf16[64,2,1536]{2,1,0:T(2,128)(2,1)}), bf16[64,2,1536]{2,1,0:T(2,128)(2,1)S(1)}, u32[]{:S(2)}, u32[]{:S(2)}) async-start(bf16[64,2,1536]{2,1,0:T(2,128)(2,1)} %reshape.76), calls=%async_computation.2 | async-start | bytes 786432 | tf_op jit(solution)/shard_map/all_to_all | solution.py:68
  74.6 0.0 copy-done.1
  74.6 0.1 dynamic_slice.16
  74.7 0.0 copy-done.2
  74.7 0.1 broadcast_subtract_fusion
  74.8 0.1 sub.49
  74.9 0.5 copy.17
  75.4 15.7 %all-to-all-done.2 = bf16[64,2,1536]{2,1,0:T(2,128)(2,1)S(1)} async-done(((bf16[64,2,1536]{2,1,0:T(2,128)(2,1)}), bf16[64,2,1536]{2,1,0:T(2,128)(2,1)S(1)}, u32[]{:S(2)}, u32[]{:S(2)}) %all-to-all-start.2) | async-done | bytes 393248 | tf_op jit(solution)/shard_map/all_to_all | solution.py:68
  91.1 1.0 %reshape.77 = bf16[64,8,8,48]{3,2,1,0:T(8,128)(2,1)S(1)} reshape(bf16[64,2,1536]{2,1,0:T(2,128)(2,1)S(1)} %all-to-all-done.2) | data formatting | bytes 786432
  92.2 0.1 bitcast_bitcast_fusion
  92.2 0.0 copy-start
  92.2 0.1 copy.14
  92.4 0.3 copy.15
  92.7 0.5 copy-done
  93.2 0.9 %divide_convert_fusion = bf16[48,4096]{1,0:T(8,128)(2,1)} fusion(f32[48,4096]{1,0:T(8,128)S(1)} %bitcast.29, bf16[48,4096]{1,0:T(8,128)(2,1)S(1)} %copy.15, f32[48,4096]{1,0:T(8,128)S(1)} %convert_reduce_fusion, bf16[48,4096]{1,0:T(8,128)(2,1)S(1)} %copy-done, f32[4096]{0:T(1024)S(1)} %bitcast.34), kind=kLoop, calls=%fused_computation.15 | loop fusion | flops 1376256 | bytes 2768896 | tf_op jit(solution)/shard_map/convert_element_type | solution.py:77
  (8 shorter events, 0.1 us)
Async XLA Ops:
  0.0 38.9 %collective-permute-start.1 = (bf16[4096,256]{1,0:T(8,128)(2,1)}, bf16[4096,256]{1,0:T(8,128)(2,1)S(1)}, u32[]{:S(2)}, u32[]{:S(2)}) collective-permute-start(bf16[4096,256]{1,0:T(8,128)(2,1)} %param.8), channel_id=1, source_target_pairs={{0,1},{1,0},{2,3},{3,2},{4,5},{5,4},{6,7},{7,6},{8,9},{9,8},{10,11... | collective-permute-start | bytes 6291464 | tf_op jit(solution)/shard_map/ppermute | solution.py:32
  3.3 31.1 %all-to-all-start = ((bf16[64,6,256]{2,1,0:T(8,128)(2,1)}), bf16[64,6,256]{2,1,0:T(8,128)(2,1)S(1)}, u32[]{:S(2)}, u32[]{:S(2)}) async-start(bf16[64,6,256]{2,1,0:T(8,128)(2,1)} %broadcast_in_dim.9), calls=%async_computation | async-start | bytes 524288 | tf_op jit(solution)/shard_map/all_to_all | solution.py:16
  34.5 4.4 %collective-permute-start = (bf16[193,256]{1,0:T(8,128)(2,1)S(1)}, bf16[193,256]{1,0:T(8,128)(2,1)S(1)}, u32[]{:S(2)}, u32[]{:S(2)}) collective-permute-start(bf16[193,256]{1,0:T(8,128)(2,1)S(1)} %pad_maximum_fusion), channel_id=1, source_target_pairs={{0,1},{1,0},{2,3},{3,2},{4,5},{5,4},{6,7},{7,6},{8,9},{9,8},{10,11... | collective-permute-start | bytes 296456 | tf_op jit(solution)/shard_map/ppermute | solution.py:47
  66.5 8.1 %copy-start.1 = (f32[512]{0:T(512)S(1)}, f32[512]{0:T(512)}, u32[]{:S(2)}) copy-start(f32[512]{0:T(512)} %param.12) | copy-start | bytes 6148
  66.5 8.2 %copy-start.2 = (f32[48]{0:T(128)S(1)}, f32[48]{0:T(128)}, u32[]{:S(2)}) copy-start(f32[48]{0:T(128)} %param.11) | copy-start | bytes 580
  69.3 21.8 %all-to-all-start.2 = ((bf16[64,2,1536]{2,1,0:T(2,128)(2,1)}), bf16[64,2,1536]{2,1,0:T(2,128)(2,1)S(1)}, u32[]{:S(2)}, u32[]{:S(2)}) async-start(bf16[64,2,1536]{2,1,0:T(2,128)(2,1)} %reshape.76), calls=%async_computation.2 | async-start | bytes 786432 | tf_op jit(solution)/shard_map/all_to_all | solution.py:68
  92.2 1.0 %copy-start = (bf16[48,4096]{1,0:T(8,128)(2,1)S(1)}, bf16[48,4096]{1,0:T(8,128)(2,1)}, u32[]{:S(2)}) copy-start(bf16[48,4096]{1,0:T(8,128)(2,1)} %param.13) | copy-start | bytes 1179652

commit v15 on v14

--- a/solution.py
+++ b/solution.py
@@ -64,8 +64,10 @@
     ladder = parts.astype(jnp.float32).sum(axis=0)
     pair_rows = ladder.shape[0]
     outgoing = ladder.astype(jnp.bfloat16).reshape(pair_rows, a_local, wide_size, a_local)
-    outgoing = jnp.transpose(outgoing, (2, 0, 1, 3))
+    outgoing = jnp.transpose(outgoing, (2, 0, 1, 3)).reshape(wide_size, 2, -1)
+    outgoing = lax.optimization_barrier(outgoing)
     got = lax.all_to_all(outgoing, WIDE, 0, 0, tiled=True)
+    got = got.reshape(wide_size, pair_rows, a_local, a_local)
     mirrored = jnp.transpose(got, (1, 3, 0, 2)).reshape(pair_rows, a_local * num_virt)
     mirrored = lax.optimization_barrier(mirrored).astype(jnp.float32)
     local_energy = lax.dynamic_slice_in_dim(virtual_energy, first_a, a_local, 0)

time: 94.7 us -> 95.7 us (1.011)
  other arithmetic: 2.74 us -> 3.74 us
    unnamed x12 -> x8, local copies, waits for them, and re-layouts: 4.52 us -> 0.49 us
    transpose x1, local copies, waits for them, and re-layouts: 0.29 us -> 1.64 us  [local(): outgoing = jnp.transpose(outgoing, (2, 0, 1, 3)).reshape(wide_size, 2, -1)]
    optimization_barrier x0 -> x1, local copies, waits for them, and re-layouts: none -> 1.11 us  [local(): outgoing = lax.optimization_barrier(outgoing)]
    transpose x2 -> x1, local copies, waits for them, and re-layouts: 0.21 us -> 1.21 us  [local(): jnp.transpose(got, (1, 3, 0, 2)).reshape(pair_rows, a_local * num_virt)]
    convert_element_type x1, other arithmetic: 0.94 us -> 1.94 us  [local(): return (total / denominator).astype(jnp.bfloat16)]
where the time goes in v15:
time: 95.7 us; the launch traced here: 95.2 us
  waiting for transfers between devices  28.1 us (29%)
  starting transfers between devices  25.6 us (27%)
  blocking collectives  25.5 us (27%)
  local copies, waits for them, and re-layouts  8.31 us (9%)
  matrix products  3.75 us (4%)
  other arithmetic  3.74 us (4%)
    all_to_all x1, blocking collectives, local(): parts = lax.all_to_all(parts, 'x', 0, 0, tiled=True)  25.5 us
    all_to_all x1, starting transfers between devices, gather_rows(): got = lax.all_to_all(copies, name, 0, 0, tiled=True)  16.5 us
    all_to_all x1, waiting for transfers between devices, local(): got = lax.all_to_all(outgoing, WIDE, 0, 0, tiled=True)  15.7 us
    all_to_all x1, waiting for transfers between devices, gather_rows(): got = lax.all_to_all(copies, name, 0, 0, tiled=True)  12.4 us
    all_to_all x1, starting transfers between devices, local(): got = lax.all_to_all(outgoing, WIDE, 0, 0, tiled=True)  5.28 us
    dot_general x1, matrix products, local(): lax.dot_general(own, masked, contract, preferred_element_type=jnp.float32)  2.44 us
    convert_element_type x1, other arithmetic, local(): return (total / denominator).astype(jnp.bfloat16)  1.94 us
    ppermute x1, starting transfers between devices, local(): sent = lax.ppermute(sent, 'c', swap)  1.92 us
  transfers between devices with their start and end apart: 4, of which 2 were waited for; matrix products, arithmetic and copies ran while one was open for 7% of the time, Pallas kernels for 0%

profile of v15, /device:TPU:16, one launch (start us, length us, event | category | flops | bytes accessed | tf_op | source)
XLA Modules:
  0.0 95.2 jit_solution(18395600251941285161)
XLA Ops:
  0.0 1.9 %collective-permute-start.1 = (bf16[4096,256]{1,0:T(8,128)(2,1)}, bf16[4096,256]{1,0:T(8,128)(2,1)S(1)}, u32[]{:S(2)}, u32[]{:S(2)}) collective-permute-start(bf16[4096,256]{1,0:T(8,128)(2,1)} %param.8), channel_id=1, source_target_pairs={{0,1},{1,0},{2,3},{3,2},{4,5},{5,4},{6,7},{7,6},{8,9},{9,8},{10,11... | collective-permute-start | bytes 6291464 | tf_op jit(solution)/shard_map/ppermute | solution.py:32
  1.9 1.4 %broadcast_in_dim.9 = bf16[64,6,256]{2,1,0:T(8,128)(2,1)} broadcast(bf16[6,256]{1,0:T(8,128)(2,1)} %param.7), dimensions={1,2} | broadcast | bytes 199680 | tf_op jit(solution)/shard_map/broadcast_in_dim | solution.py:15
  3.3 16.5 %all-to-all-start = ((bf16[64,6,256]{2,1,0:T(8,128)(2,1)}), bf16[64,6,256]{2,1,0:T(8,128)(2,1)S(1)}, u32[]{:S(2)}, u32[]{:S(2)}) async-start(bf16[64,6,256]{2,1,0:T(8,128)(2,1)} %broadcast_in_dim.9), calls=%async_computation | async-start | bytes 524288 | tf_op jit(solution)/shard_map/all_to_all | solution.py:16
  19.8 0.8 dynamic_slice.14
  20.6 0.8 xor_bitcast_fusion
  21.3 0.7 convert_element_type.42
  22.0 12.4 %all-to-all-done = bf16[64,6,256]{2,1,0:T(8,128)(2,1)S(1)} async-done(((bf16[64,6,256]{2,1,0:T(8,128)(2,1)}), bf16[64,6,256]{2,1,0:T(8,128)(2,1)S(1)}, u32[]{:S(2)}, u32[]{:S(2)}) %all-to-all-start) | async-done | bytes 196640 | tf_op jit(solution)/shard_map/all_to_all | solution.py:16
  34.4 0.1 reshape_reshape.3
  34.5 1.9 %collective-permute-start = (bf16[193,256]{1,0:T(8,128)(2,1)S(1)}, bf16[193,256]{1,0:T(8,128)(2,1)S(1)}, u32[]{:S(2)}, u32[]{:S(2)}) collective-permute-start(bf16[193,256]{1,0:T(8,128)(2,1)S(1)} %pad_maximum_fusion), channel_id=1, source_target_pairs={{0,1},{1,0},{2,3},{3,2},{4,5},{5,4},{6,7},{7,6},{8,9},{9,8},{10,11... | collective-permute-start | bytes 296456 | tf_op jit(solution)/shard_map/ppermute | solution.py:47
  36.5 2.4 %fusion.3 = f32[192,4096]{1,0:T(8,128)S(1)} fusion(bf16[192,256]{1,0:T(8,128)(2,1)S(1)} %bitcast.29, bf16[4096,256]{1,0:T(8,128)(2,1)} %param.8, s32[256]{0:T(256)} %param.10, s32[4096]{0:T(1024)S(1)} %bitcast.30), kind=kOutput, calls=%fused_computation.5 | convolution fusion | flops 406323200 | bytes 5358592 | tf_op jit(solution)/shard_map/dot_general | solution.py:55
  38.9 0.0 collective-permute-done
  38.9 0.0 collective-permute-done.1
  38.9 1.3 %fusion.2 = bf16[192,4096]{1,0:T(8,128)(2,1)S(1)} fusion(f32[192,4096]{1,0:T(8,128)S(1)} %fusion.3, bf16[4096,256]{1,0:T(8,128)(2,1)S(1)} %collective-permute-done.1, s32[256]{0:T(256)S(1)} %bitcast.33, s32[4096]{0:T(1024)S(1)} %bitcast.31, bf16[193,256]{1,0:T(8,128)(2,1)S(1)} %collective-permute-done), kind=kOutput, calls=%fused_computation.3 | convolution fusion | flops 407896064 | bytes 6931456 | tf_op jit(solution)/shard_map/dot_general | solution.py:56
  40.3 25.5 %all_to_all.15 = bf16[4,48,4096]{2,1,0:T(8,128)(2,1)S(1)} all-to-all(bf16[4,48,4096]{2,1,0:T(8,128)(2,1)S(1)} %bitcast.21), channel_id=1, replica_groups=mesh['y'=8,'z'=8,'x'=4,'c'=2] {'x'}, dimensions={0} | all-to-all | bytes 3145728 | tf_op jit(solution)/shard_map/all_to_all | solution.py:63
  65.7 0.2 convert_reduce_fusion
  66.0 0.5 copy.12
  66.5 0.0 copy-start
  66.5 0.0 copy-start.1
  66.5 1.6 %copy.13 = bf16[64,48,8,8]{0,3,2,1:T(8,128)(2,1)S(1)} copy(bf16[64,48,8,8]{1,3,0,2:T(8,128)(2,1)S(1)} %bitcast.22) | data formatting | bytes 786432 | tf_op jit(solution)/shard_map/transpose | solution.py:67
  68.2 1.1 %copy.14 = bf16[64,2,1536]{2,1,0:T(2,128)(2,1)} copy(bf16[64,2,1536]{0,2,1:T(8,128)(2,1)S(1)} %bitcast.24) | data formatting | bytes 786432 | tf_op jit(solution)/shard_map/optimization_barrier | solution.py:68
  69.3 5.3 %all-to-all-start.2 = ((bf16[64,2,1536]{2,1,0:T(2,128)(2,1)}), bf16[64,2,1536]{2,1,0:T(2,128)(2,1)S(1)}, u32[]{:S(2)}, u32[]{:S(2)}) async-start(bf16[64,2,1536]{2,1,0:T(2,128)(2,1)} %copy.14), calls=%async_computation.2 | async-start | bytes 786432 | tf_op jit(solution)/shard_map/all_to_all | solution.py:69
  74.6 0.0 copy-done
  74.6 0.1 dynamic_slice.16
  74.7 0.0 copy-done.1
  74.7 0.1 broadcast_subtract_fusion
  74.7 0.1 sub.49
  74.9 0.5 copy.19
  75.3 15.7 %all-to-all-done.2 = bf16[64,2,1536]{2,1,0:T(2,128)(2,1)S(1)} async-done(((bf16[64,2,1536]{2,1,0:T(2,128)(2,1)}), bf16[64,2,1536]{2,1,0:T(2,128)(2,1)S(1)}, u32[]{:S(2)}, u32[]{:S(2)}) %all-to-all-start.2) | async-done | bytes 393248 | tf_op jit(solution)/shard_map/all_to_all | solution.py:69
  91.1 0.6 copy.15
  91.7 1.2 %copy.16 = bf16[48,8,64,8]{0,3,2,1:T(8,128)(2,1)S(1)} copy(bf16[48,8,64,8]{2,1,3,0:T(8,128)(2,1)S(1)} %bitcast.25) | data formatting | bytes 786432 | tf_op jit(solution)/shard_map/transpose | solution.py:71
  92.9 0.3 copy.17
  93.2 1.9 %divide_convert_fusion = bf16[48,4096]{1,0:T(8,128)(2,1)} fusion(f32[48,4096]{1,0:T(8,128)S(1)} %bitcast.27, bf16[48,4096]{1,0:T(8,128)(2,1)S(1)} %copy.17, f32[48,4096]{1,0:T(8,128)S(1)} %convert_reduce_fusion, bf16[48,4096]{1,0:T(8,128)(2,1)} %param.13, f32[4096]{0:T(1024)S(1)} %bitcast.32), kind=kLoop, calls=%fused_computation.15 | loop fusion | flops 1376256 | bytes 2768896 | tf_op jit(solution)/shard_map/convert_element_type | solution.py:79
  (8 shorter events, 0.1 us)
Async XLA Ops:
  0.0 38.9 %collective-permute-start.1 = (bf16[4096,256]{1,0:T(8,128)(2,1)}, bf16[4096,256]{1,0:T(8,128)(2,1)S(1)}, u32[]{:S(2)}, u32[]{:S(2)}) collective-permute-start(bf16[4096,256]{1,0:T(8,128)(2,1)} %param.8), channel_id=1, source_target_pairs={{0,1},{1,0},{2,3},{3,2},{4,5},{5,4},{6,7},{7,6},{8,9},{9,8},{10,11... | collective-permute-start | bytes 6291464 | tf_op jit(solution)/shard_map/ppermute | solution.py:32
  3.3 31.1 %all-to-all-start = ((bf16[64,6,256]{2,1,0:T(8,128)(2,1)}), bf16[64,6,256]{2,1,0:T(8,128)(2,1)S(1)}, u32[]{:S(2)}, u32[]{:S(2)}) async-start(bf16[64,6,256]{2,1,0:T(8,128)(2,1)} %broadcast_in_dim.9), calls=%async_computation | async-start | bytes 524288 | tf_op jit(solution)/shard_map/all_to_all | solution.py:16
  34.5 4.4 %collective-permute-start = (bf16[193,256]{1,0:T(8,128)(2,1)S(1)}, bf16[193,256]{1,0:T(8,128)(2,1)S(1)}, u32[]{:S(2)}, u32[]{:S(2)}) collective-permute-start(bf16[193,256]{1,0:T(8,128)(2,1)S(1)} %pad_maximum_fusion), channel_id=1, source_target_pairs={{0,1},{1,0},{2,3},{3,2},{4,5},{5,4},{6,7},{7,6},{8,9},{9,8},{10,11... | collective-permute-start | bytes 296456 | tf_op jit(solution)/shard_map/ppermute | solution.py:47
  66.5 8.1 %copy-start = (f32[512]{0:T(512)S(1)}, f32[512]{0:T(512)}, u32[]{:S(2)}) copy-start(f32[512]{0:T(512)} %param.12) | copy-start | bytes 6148
  66.5 8.2 %copy-start.1 = (f32[48]{0:T(128)S(1)}, f32[48]{0:T(128)}, u32[]{:S(2)}) copy-start(f32[48]{0:T(128)} %param.11) | copy-start | bytes 580
  69.3 21.8 %all-to-all-start.2 = ((bf16[64,2,1536]{2,1,0:T(2,128)(2,1)}), bf16[64,2,1536]{2,1,0:T(2,128)(2,1)S(1)}, u32[]{:S(2)}, u32[]{:S(2)}) async-start(bf16[64,2,1536]{2,1,0:T(2,128)(2,1)} %copy.14), calls=%async_computation.2 | async-start | bytes 786432 | tf_op jit(solution)/shard_map/all_to_all | solution.py:69

commit v16 on v14

--- a/solution.py
+++ b/solution.py
@@ -56,9 +56,8 @@
     part_other = lax.dot_general(
         other, masked_partner, contract, preferred_element_type=jnp.float32
     )
-    pair_sum = part_own.astype(jnp.bfloat16).astype(jnp.float32) + part_other.astype(
-        jnp.bfloat16
-    ).astype(jnp.float32)
+    part_own = lax.optimization_barrier(part_own.astype(jnp.bfloat16))
+    pair_sum = part_own.astype(jnp.float32) + part_other.astype(jnp.bfloat16).astype(jnp.float32)
     parts = pair_sum.astype(jnp.bfloat16).reshape(nx, block, pair_sum.shape[1])
     parts = lax.all_to_all(parts, "x", 0, 0, tiled=True)
     ladder = parts.astype(jnp.float32).sum(axis=0)

time: 94.7 us -> 94.7 us (level)
  no operation moved by 1% of the time
where the time goes in v16:
time: 94.7 us; the launch traced here: 94.2 us
  waiting for transfers between devices  28.1 us (30%)
  starting transfers between devices  25.6 us (27%)
  blocking collectives  25.5 us (27%)
  local copies, waits for them, and re-layouts  8.28 us (9%)
  matrix products  3.78 us (4%)
  other arithmetic  2.74 us (3%)
    all_to_all x1, blocking collectives, local(): parts = lax.all_to_all(parts, 'x', 0, 0, tiled=True)  25.5 us
    all_to_all x1, starting transfers between devices, gather_rows(): got = lax.all_to_all(copies, name, 0, 0, tiled=True)  16.5 us
    all_to_all x1, waiting for transfers between devices, local(): got = lax.all_to_all(outgoing, WIDE, 0, 0, tiled=True)  15.7 us
    all_to_all x1, waiting for transfers between devices, gather_rows(): got = lax.all_to_all(copies, name, 0, 0, tiled=True)  12.4 us
    all_to_all x1, starting transfers between devices, local(): got = lax.all_to_all(outgoing, WIDE, 0, 0, tiled=True)  5.28 us
    unnamed x12, local copies, waits for them, and re-layouts  4.52 us
    dot_general x1, matrix products, local(): lax.dot_general(own, masked, contract, preferred_element_type=jnp.float32)  2.47 us
    ppermute x1, starting transfers between devices, local(): sent = lax.ppermute(sent, 'c', swap)  1.92 us
  transfers between devices with their start and end apart: 4, of which 2 were waited for; matrix products, arithmetic and copies ran while one was open for 7% of the time, Pallas kernels for 0%

profile of v16, /device:TPU:16, one launch (start us, length us, event | category | flops | bytes accessed | tf_op | source)
XLA Modules:
  0.0 94.2 jit_solution(12225395198036709557)
XLA Ops:
  0.0 1.9 %collective-permute-start.1 = (bf16[4096,256]{1,0:T(8,128)(2,1)}, bf16[4096,256]{1,0:T(8,128)(2,1)S(1)}, u32[]{:S(2)}, u32[]{:S(2)}) collective-permute-start(bf16[4096,256]{1,0:T(8,128)(2,1)} %param.8), channel_id=1, source_target_pairs={{0,1},{1,0},{2,3},{3,2},{4,5},{5,4},{6,7},{7,6},{8,9},{9,8},{10,11... | collective-permute-start | bytes 6291464 | tf_op jit(solution)/shard_map/ppermute | solution.py:32
  1.9 1.4 %broadcast_in_dim.9 = bf16[64,6,256]{2,1,0:T(8,128)(2,1)} broadcast(bf16[6,256]{1,0:T(8,128)(2,1)} %param.7), dimensions={1,2} | broadcast | bytes 199680 | tf_op jit(solution)/shard_map/broadcast_in_dim | solution.py:15
  3.3 16.5 %all-to-all-start = ((bf16[64,6,256]{2,1,0:T(8,128)(2,1)}), bf16[64,6,256]{2,1,0:T(8,128)(2,1)S(1)}, u32[]{:S(2)}, u32[]{:S(2)}) async-start(bf16[64,6,256]{2,1,0:T(8,128)(2,1)} %broadcast_in_dim.9), calls=%async_computation | async-start | bytes 524288 | tf_op jit(solution)/shard_map/all_to_all | solution.py:16
  19.8 0.8 dynamic_slice.14
  20.6 0.8 xor_bitcast_fusion
  21.3 0.7 convert_element_type.42
  22.0 12.4 %all-to-all-done = bf16[64,6,256]{2,1,0:T(8,128)(2,1)S(1)} async-done(((bf16[64,6,256]{2,1,0:T(8,128)(2,1)}), bf16[64,6,256]{2,1,0:T(8,128)(2,1)S(1)}, u32[]{:S(2)}, u32[]{:S(2)}) %all-to-all-start) | async-done | bytes 196640 | tf_op jit(solution)/shard_map/all_to_all | solution.py:16
  34.4 0.1 reshape_reshape.3
  34.5 1.9 %collective-permute-start = (bf16[193,256]{1,0:T(8,128)(2,1)S(1)}, bf16[193,256]{1,0:T(8,128)(2,1)S(1)}, u32[]{:S(2)}, u32[]{:S(2)}) collective-permute-start(bf16[193,256]{1,0:T(8,128)(2,1)S(1)} %pad_maximum_fusion), channel_id=1, source_target_pairs={{0,1},{1,0},{2,3},{3,2},{4,5},{5,4},{6,7},{7,6},{8,9},{9,8},{10,11... | collective-permute-start | bytes 296456 | tf_op jit(solution)/shard_map/ppermute | solution.py:47
  36.5 2.5 %convolution_convert_fusion.1 = bf16[192,4096]{1,0:T(8,128)(2,1)S(1)} fusion(bf16[192,256]{1,0:T(8,128)(2,1)S(1)} %bitcast.31, bf16[4096,256]{1,0:T(8,128)(2,1)} %param.8, s32[256]{0:T(256)} %param.10, s32[4096]{0:T(1024)S(1)} %bitcast.33), kind=kOutput, calls=%fused_computation.4 | convolution fusion | flops 405536768 | bytes 3785728 | tf_op jit(solution)/shard_map/dot_general | solution.py:55
  38.9 0.0 collective-permute-done
  39.0 0.0 collective-permute-done.1
  39.0 1.3 %fusion.2 = bf16[192,4096]{1,0:T(8,128)(2,1)S(1)} fusion(bf16[192,4096]{1,0:T(8,128)(2,1)S(1)} %convolution_convert_fusion.1, bf16[4096,256]{1,0:T(8,128)(2,1)S(1)} %collective-permute-done.1, s32[256]{0:T(256)S(1)} %bitcast.35, s32[4096]{0:T(1024)S(1)} %bitcast.34, bf16[193,256]{1,0:T(8,128)(2,1)S(1)} %collective-permute-done), kind=kOutput, calls=%fused_computation.3 | convolution fusion | flops 408682496 | bytes 5358592 | tf_op jit(solution)/shard_map/dot_general | solution.py:56
  40.3 25.5 %all_to_all.15 = bf16[4,48,4096]{2,1,0:T(8,128)(2,1)S(1)} all-to-all(bf16[4,48,4096]{2,1,0:T(8,128)(2,1)S(1)} %bitcast.29), channel_id=1, replica_groups=mesh['y'=8,'z'=8,'x'=4,'c'=2] {'x'}, dimensions={0} | all-to-all | bytes 3145728 | tf_op jit(solution)/shard_map/all_to_all | solution.py:62
  65.8 0.2 convert_reduce_fusion
  66.0 0.5 copy.12
  66.5 0.0 copy-start.1
  66.5 0.0 copy-start.2
  66.6 0.3 copy.20
  66.8 2.5 %reshape.76 = bf16[64,2,1536]{2,1,0:T(2,128)(2,1)} reshape(bf16[64,8,8,48]{3,2,1,0:T(8,128)(2,1)S(1)} %bitcast.25) | data formatting | bytes 786432
  69.3 5.3 %all-to-all-start.2 = ((bf16[64,2,1536]{2,1,0:T(2,128)(2,1)}), bf16[64,2,1536]{2,1,0:T(2,128)(2,1)S(1)}, u32[]{:S(2)}, u32[]{:S(2)}) async-start(bf16[64,2,1536]{2,1,0:T(2,128)(2,1)} %reshape.76), calls=%async_computation.2 | async-start | bytes 786432 | tf_op jit(solution)/shard_map/all_to_all | solution.py:67
  74.6 0.0 copy-done.1
  74.6 0.1 dynamic_slice.16
  74.7 0.0 copy-done.2
  74.7 0.1 broadcast_subtract_fusion
  74.8 0.1 sub.49
  74.9 0.5 copy.17
  75.4 15.7 %all-to-all-done.2 = bf16[64,2,1536]{2,1,0:T(2,128)(2,1)S(1)} async-done(((bf16[64,2,1536]{2,1,0:T(2,128)(2,1)}), bf16[64,2,1536]{2,1,0:T(2,128)(2,1)S(1)}, u32[]{:S(2)}, u32[]{:S(2)}) %all-to-all-start.2) | async-done | bytes 393248 | tf_op jit(solution)/shard_map/all_to_all | solution.py:67
  91.1 1.0 %reshape.77 = bf16[64,8,8,48]{3,2,1,0:T(8,128)(2,1)S(1)} reshape(bf16[64,2,1536]{2,1,0:T(2,128)(2,1)S(1)} %all-to-all-done.2) | data formatting | bytes 786432
  92.2 0.1 bitcast_bitcast_fusion
  92.3 0.0 copy-start
  92.3 0.1 copy.14
  92.4 0.3 copy.15
  92.8 0.5 copy-done
  93.3 0.9 %divide_convert_fusion = bf16[48,4096]{1,0:T(8,128)(2,1)} fusion(f32[48,4096]{1,0:T(8,128)S(1)} %bitcast.28, bf16[48,4096]{1,0:T(8,128)(2,1)S(1)} %copy.15, f32[48,4096]{1,0:T(8,128)S(1)} %convert_reduce_fusion, bf16[48,4096]{1,0:T(8,128)(2,1)S(1)} %copy-done, f32[4096]{0:T(1024)S(1)} %bitcast.32), kind=kLoop, calls=%fused_computation.14 | loop fusion | flops 1376256 | bytes 2768896 | tf_op jit(solution)/shard_map/convert_element_type | solution.py:76
  (8 shorter events, 0.1 us)
Async XLA Ops:
  0.0 39.0 %collective-permute-start.1 = (bf16[4096,256]{1,0:T(8,128)(2,1)}, bf16[4096,256]{1,0:T(8,128)(2,1)S(1)}, u32[]{:S(2)}, u32[]{:S(2)}) collective-permute-start(bf16[4096,256]{1,0:T(8,128)(2,1)} %param.8), channel_id=1, source_target_pairs={{0,1},{1,0},{2,3},{3,2},{4,5},{5,4},{6,7},{7,6},{8,9},{9,8},{10,11... | collective-permute-start | bytes 6291464 | tf_op jit(solution)/shard_map/ppermute | solution.py:32
  3.3 31.1 %all-to-all-start = ((bf16[64,6,256]{2,1,0:T(8,128)(2,1)}), bf16[64,6,256]{2,1,0:T(8,128)(2,1)S(1)}, u32[]{:S(2)}, u32[]{:S(2)}) async-start(bf16[64,6,256]{2,1,0:T(8,128)(2,1)} %broadcast_in_dim.9), calls=%async_computation | async-start | bytes 524288 | tf_op jit(solution)/shard_map/all_to_all | solution.py:16
  34.5 4.4 %collective-permute-start = (bf16[193,256]{1,0:T(8,128)(2,1)S(1)}, bf16[193,256]{1,0:T(8,128)(2,1)S(1)}, u32[]{:S(2)}, u32[]{:S(2)}) collective-permute-start(bf16[193,256]{1,0:T(8,128)(2,1)S(1)} %pad_maximum_fusion), channel_id=1, source_target_pairs={{0,1},{1,0},{2,3},{3,2},{4,5},{5,4},{6,7},{7,6},{8,9},{9,8},{10,11... | collective-permute-start | bytes 296456 | tf_op jit(solution)/shard_map/ppermute | solution.py:47
  66.5 8.1 %copy-start.1 = (f32[512]{0:T(512)S(1)}, f32[512]{0:T(512)}, u32[]{:S(2)}) copy-start(f32[512]{0:T(512)} %param.12) | copy-start | bytes 6148
  66.5 8.2 %copy-start.2 = (f32[48]{0:T(128)S(1)}, f32[48]{0:T(128)}, u32[]{:S(2)}) copy-start(f32[48]{0:T(128)} %param.11) | copy-start | bytes 580
  69.3 21.8 %all-to-all-start.2 = ((bf16[64,2,1536]{2,1,0:T(2,128)(2,1)}), bf16[64,2,1536]{2,1,0:T(2,128)(2,1)S(1)}, u32[]{:S(2)}, u32[]{:S(2)}) async-start(bf16[64,2,1536]{2,1,0:T(2,128)(2,1)} %reshape.76), calls=%async_computation.2 | async-start | bytes 786432 | tf_op jit(solution)/shard_map/all_to_all | solution.py:67
  92.3 1.0 %copy-start = (bf16[48,4096]{1,0:T(8,128)(2,1)S(1)}, bf16[48,4096]{1,0:T(8,128)(2,1)}, u32[]{:S(2)}) copy-start(bf16[48,4096]{1,0:T(8,128)(2,1)} %param.13) | copy-start | bytes 1179652
